TPU v7x, 128 devices: a whole 4x4x4 slice. The times are simulated.
128 devices in a mesh: seq: 4 (over x), exp: 32 (over y, z, core).
Axes of the slice: x: 4, y: 4, z: 4, core: 2. Of those that a mesh axis runs over, the one named last changes fastest.
Arguments:
- resid: bfloat16 [32, 384, 2048], P('exp', 'seq'), may hold values from -6 to 6
- qkv: bfloat16 [32, 384, 6144], P('exp', 'seq'), may hold values from -8 to 8
- w_out: bfloat16 [2048, 2048], P('seq'), may hold values from -0.125 to 0.125
- norm_gain: float32 [2048], replicated, may hold values from 0.1 to 1.9
- router_w: bfloat16 [2048, 64], replicated, may hold values from -0.125 to 0.125
- expert_ids: int32 [32, 384, 6], P('exp'), may hold values from 0 to 63, all different within a row; in each aligned block of 96 rows (0 to 95, 96 to 191, ..., all dimensions but the last counted through in order) at most 12 rows name the same one
- w_gate_up: bfloat16 [64, 2048, 2, 1408], P('exp', None, None, 'seq'), may hold values from -0.125 to 0.125
- w_down: bfloat16 [64, 1408, 2048], P('exp', 'seq'), may hold values from -0.15625 to 0.15625
Outputs:
- layer_out: bfloat16 [32, 384, 2048], P('exp', 'seq')
Inputs may be any that keep to these rules, and one draw needn't show every extreme that they name: `expert_ids`: each point names 6 different experts. In each aligned block of 96 points (the points of one device, in the order of sets and then points), no expert is named by more than 12 points, and in every draw some expert is named by exactly 12 points of some block.
All inputs are finite; a program needn't handle non-finite values.
Results may differ from a plain program's by a relative error of at most 0.0065.
Values may be sent and summed in bfloat16 or wider, within the bound.
No kernel may reach another device: no remote copies, remote signals or barrier semaphores. Data moves between devices by JAX's collectives and lax.ppermute only.
A program may use at most 128 MiB of HBM per device.

v0:
```python
import math

import jax
import jax.numpy as jnp
from jax import lax
from jax.sharding import PartitionSpec as P

H = 16
HD = 128
EXPERTS = 64


epsilon = 1e-05


def gate_weights(normed_rows, router_w, chosen):
    logits = jnp.dot(normed_rows, router_w, preferred_element_type=jnp.float32)
    match = chosen[:, :, None] == jnp.arange(logits.shape[1], dtype=jnp.int32)[None, None, :]
    picked = jnp.sum(jnp.where(match, logits[:, None, :], jnp.zeros((), logits.dtype)), axis=-1)
    squashed = jax.nn.sigmoid(picked)
    return squashed / jnp.sum(squashed, axis=-1, keepdims=True)


def slot_ranks(chosen, block_rows, experts):
    blocks = chosen.shape[0] // block_rows
    grouped = chosen.reshape(blocks, block_rows * chosen.shape[1])
    hits = (grouped[:, :, None] == jnp.arange(experts, dtype=jnp.int32)[None, None, :]).astype(
        jnp.int32
    )
    ranks = jnp.sum(jnp.cumsum(hits, axis=1) * hits, axis=-1) - 1
    return ranks.reshape(chosen.shape)


def expert_part(received, w_gate_up, w_down):
    both = jnp.einsum("aend,edgf->aengf", received, w_gate_up, preferred_element_type=jnp.float32)
    hidden = (jax.nn.silu(both[:, :, :, 0]) * both[:, :, :, 1]).astype(jnp.bfloat16)
    return jnp.einsum("aenf,efd->aend", hidden, w_down, preferred_element_type=jnp.float32)


def scatter_rows(normed_rows, slot_index, buffer_rows):
    feature_width = normed_rows.shape[1]
    spread = jnp.broadcast_to(
        normed_rows[:, None, :], (slot_index.shape[0], slot_index.shape[1], feature_width)
    )
    empty = jnp.zeros((buffer_rows, feature_width), jnp.bfloat16)
    return empty.at[slot_index.reshape(-1)].set(spread.reshape(-1, feature_width))


def combine_rows(out_table, slot_index, gate_vals):
    picked = out_table[slot_index].astype(jnp.float32)
    return jnp.sum(gate_vals[:, :, None] * picked, axis=1)


def on_device(resid, qkv, w_out, norm_gain, router_w, expert_ids, w_gate_up, w_down):
    row_count = resid.shape[1]
    model_width = resid.shape[2]
    seq_size = lax.axis_size("seq")
    exp_size = lax.axis_size("exp")
    seq_length = row_count * seq_size
    head_local = H // seq_size
    local_width = head_local * HD
    packed = qkv.reshape(row_count, 3, seq_size, local_width)
    regrouped = lax.all_to_all(packed, "seq", split_axis=2, concat_axis=0, tiled=True)
    queries = regrouped[:, 0, 0].reshape(seq_length, head_local, HD)
    keys_all = regrouped[:, 1, 0].reshape(seq_length, head_local, HD)
    values_all = regrouped[:, 2, 0].reshape(seq_length, head_local, HD)
    query_block = min(seq_length, 512)

    def attend_block(query_rows):
        scores = jnp.einsum(
            "qhd,khd->hqk", query_rows, keys_all, preferred_element_type=jnp.float32
        ) / math.sqrt(HD)
        weights = jax.nn.softmax(scores, axis=-1).astype(jnp.bfloat16)
        mixed_heads = jnp.einsum(
            "hqk,khd->qhd", weights, values_all, preferred_element_type=jnp.float32
        )
        return mixed_heads.reshape(query_rows.shape[0], local_width).astype(jnp.bfloat16)

    attended = lax.map(
        attend_block, queries.reshape(seq_length // query_block, query_block, head_local, HD)
    )
    attended = attended.reshape(seq_length, local_width)
    back = lax.all_to_all(
        attended.reshape(seq_length, 1, local_width), "seq", split_axis=0, concat_axis=1, tiled=True
    )
    point_rows = back.reshape(row_count, model_width)
    projected = jnp.dot(
        point_rows,
        lax.all_gather(w_out, "seq", axis=0, tiled=True),
        preferred_element_type=jnp.float32,
    )
    mixed = resid[0].astype(jnp.float32) + projected
    meansq = jnp.mean(mixed * mixed, axis=-1, keepdims=True)
    normed = (mixed * lax.rsqrt(meansq + epsilon) * norm_gain).astype(jnp.bfloat16)
    exp_local = w_gate_up.shape[0]
    slot_cap = row_count // 8
    gathered = lax.all_gather(normed, "seq", axis=0, tiled=True)
    chosen = expert_ids[0]
    gate_vals = gate_weights(gathered, router_w, chosen)
    ranks = slot_ranks(chosen, row_count, EXPERTS)
    owner_rows = seq_size * slot_cap
    source_block = (jnp.arange(seq_length, dtype=jnp.int32) // row_count)[:, None]
    slot_index = chosen * owner_rows + source_block * slot_cap + ranks
    outgoing = scatter_rows(gathered, slot_index, EXPERTS * owner_rows)
    outgoing = outgoing.reshape(exp_size, exp_local, owner_rows, model_width)
    partial_out = expert_part(
        lax.all_to_all(outgoing, "exp", split_axis=0, concat_axis=0, tiled=True), w_gate_up, w_down
    ).astype(jnp.bfloat16)
    returned = lax.all_to_all(partial_out, "exp", split_axis=0, concat_axis=0, tiled=True)
    out_table = returned.reshape(-1, model_width)
    expert_sum = lax.psum_scatter(
        combine_rows(out_table, slot_index, gate_vals).astype(jnp.bfloat16),
        "seq",
        scatter_dimension=0,
        tiled=True,
    ).astype(jnp.float32)
    return (mixed + expert_sum).astype(jnp.bfloat16).reshape(1, row_count, model_width)


def solution(mesh):
    in_specs = (
        P("exp", "seq", None),
        P("exp", "seq", None),
        P("seq", None),
        P(),
        P(),
        P("exp", None, None),
        P("exp", None, None, "seq"),
        P("exp", "seq", None),
    )
    out_specs = P("exp", "seq", None)
    return jax.shard_map(
        on_device, mesh=mesh, in_specs=in_specs, out_specs=out_specs, check_vma=False
    )
```

profile of v0, /device:TPU:0, one launch (start us, length us, event | category | flops | bytes accessed | tf_op | source)
XLA Modules:
  0.0 654.6 jit_solution(16981379489135782566)
XLA Ops:
  6.5 0.7 all-gather.3.cloned.1.call-update
  7.3 2.9 reshape.211
  10.2 1.5 copy.95
  11.7 27.4 %all_to_all.43 = bf16[96,3,4,512]{3,0,1,2:T(8,128)(2,1)S(1)} all-to-all(bf16[96,3,4,512]{3,0,1,2:T(8,128)(2,1)S(1)} %copy.95), channel_id=1, replica_groups=mesh['seq'=4,'exp'=32] {'seq'}, dimensions={2} | all-to-all | bytes 2359296 | tf_op jit(solution)/shard_map/all_to_all | solution.py:63
  39.2 1.0 fusion.34
  40.2 1.9 copy.98
  42.2 1.9 copy.101
  44.1 0.9 copy.97
  45.0 3.5 fusion.35
  48.5 2.2 convolution_convert_fusion
  50.7 0.5 broadcast.205
  51.2 1.5 reduce.2
  52.7 1.2 copy.137
  53.9 1.0 reshape.245
  54.9 15.5 %all_to_all.44 = bf16[4,2,24576]{2,1,0:T(2,128)(2,1)S(1)} all-to-all(bf16[4,2,24576]{2,1,0:T(2,128)(2,1)} %reshape.245), channel_id=1, replica_groups=mesh['seq'=4,'exp'=32] {'seq'}, dimensions={0} | all-to-all | bytes 786432 | tf_op jit(solution)/shard_map/all_to_all | solution.py:83
  70.4 1.7 reshape.246
  72.1 1.2 copy.123
  73.3 0.3 copy.104
  73.7 30.5 %all-gather.3.cloned.1.call-done = bf16[2048,2048]{1,0:T(8,128)(2,1)} async-done(((bf16[512,2048]{1,0:T(8,128)(2,1)}), bf16[2048,2048]{1,0:T(8,128)(2,1)}) %all-gather.3.cloned.1.call-update) | async-done | bytes 8388624 | tf_op jit(solution)/shard_map/all_gather | solution.py:89
  104.1 5.0 multiply_reduce_fusion.2
  109.2 0.9 copy-done.2
  110.0 0.9 multiply_convert_fusion
  111.3 0.8 mul.85
  112.2 0.8 add.136
  113.0 0.9 copy_bitcast_fusion
  113.9 10.8 %reduce-window.6 = s32[4,64,5,128]{3,1,2,0:T(8,128)S(1)} reduce-window(s32[4,64,5,128]{3,1,2,0:T(8,128)} %copy_bitcast_fusion, s32[]{:T(128)} %constant.56.clone.1), window={size=1x1x1x128 pad=0_0x0_0x0_0x127_0}, to_apply=%region_5.6 | reduce-window | flops 20807680 | bytes 1310724 | tf_op jit(solution)/shard_map/reduce-window
  124.8 1.1 slice.37
  125.8 1.9 copy.109
  127.8 0.7 fusion.25
  128.5 0.2 bitcast_bitcast_fusion
  128.9 0.8 fusion.27
  129.7 8.7 %all-gather.5.cloned.1.call-done = bf16[384,2048]{1,0:T(8,128)(2,1)} async-done(((bf16[96,2048]{1,0:T(8,128)(2,1)}), bf16[384,2048]{1,0:T(8,128)(2,1)}) %all-gather.5.cloned.1.call-update) | async-done | bytes 1572880 | tf_op jit(solution)/shard_map/all_gather | solution.py:97
  138.3 7.0 %broadcast_in_dim.26 = bf16[384,6,2048]{2,1,0:T(8,128)(2,1)} broadcast(bf16[384,2048]{1,0:T(8,128)(2,1)} %all-gather.5.cloned.1.call-done), dimensions={0,2} | broadcast | bytes 11010048 | tf_op jit(solution)/shard_map/broadcast_in_dim | solution.py:42
  145.4 15.8 %reshape.233 = bf16[2304,2048]{1,0:T(8,128)(2,1)} reshape(bf16[384,6,2048]{2,1,0:T(8,128)(2,1)} %broadcast_in_dim.26) | data formatting | bytes 18874368 | tf_op jit(solution)/shard_map/reshape | solution.py:46
  161.2 23.8 %scatter_custom_fusion = bf16[3072,2048]{1,0:T(8,128)(2,1)} fusion(s32[2304]{0:T(1024)S(1)} %fusion.27, bf16[2304,2048]{1,0:T(8,128)(2,1)} %reshape.233, bf16[]{:T(256)} %constant.34.clone.1), kind=kCustom, calls=%fused_computation.7 | custom fusion | bytes 12583424 | tf_op jit(solution)/shard_map/scatter | solution.py:46
  185.0 147.6 %all_to_all.45 = bf16[32,2,48,2048]{3,2,1,0:T(8,128)(2,1)S(1)} all-to-all(bf16[32,2,48,2048]{3,2,1,0:T(8,128)(2,1)} %bitcast.95), channel_id=1, replica_groups=mesh['seq'=4,'exp'=32] {'exp'}, dimensions={0} | all-to-all | bytes 25165824 | tf_op jit(solution)/shard_map/all_to_all | solution.py:107
  332.6 14.3 %fusion.8 = f32[32,2,48,2,352]{4,2,3,0,1:T(8,128)} fusion(bf16[2,2048,2,352]{1,3,2,0:T(8,128)(2,1)} %param.14, bf16[32,2,48,2048]{3,2,1,0:T(8,128)(2,1)S(1)} %all_to_all.45), kind=kOutput, calls=%fused_computation.14 | convolution fusion | flops 8858370048 | bytes 27000832 | tf_op jit(solution)/shard_map/aend,edgf->aengf/dot_general | solution.py:35
  347.0 10.7 %convert_bitcast_fusion = bf16[32,2,48,2048]{3,2,0,1:T(8,128)(2,1)S(1)} fusion(bf16[2,352,2048]{2,1,0:T(8,128)(2,1)S(1)} %copy-done, f32[32,2,48,2,352]{4,2,3,0,1:T(8,128)} %fusion.8), kind=kOutput, calls=%fused_computation.6 | convolution fusion | flops 4441964544 | bytes 24117248 | tf_op jit(solution)/shard_map/aenf,efd->aend/dot_general | solution.py:37
  357.7 5.2 copy.114
  362.9 5.4 all-to-all-start.3
  368.4 0.2 sub.33
  368.9 0.6 fusion.36
  369.8 175.7 %all-to-all-done.3 = bf16[32,2,48,2048]{3,2,1,0:T(8,128)(2,1)} async-done(((bf16[32,2,48,2048]{3,2,1,0:T(8,128)(2,1)}), bf16[32,2,48,2048]{3,2,1,0:T(8,128)(2,1)}, u32[]{:S(2)}, u32[]{:S(2)}) %all-to-all-start.3) | async-done | bytes 12582944 | tf_op jit(solution)/shard_map/all_to_all | solution.py:109
  545.5 24.5 %gather_fusion = bf16[2304,2048]{1,0:T(8,128)(2,1)} fusion(bf16[3072,2048]{1,0:T(8,128)(2,1)} %bitcast.24, s32[3072]{0:T(1024)S(1)} %pad_clamp_fusion), kind=kCustom, calls=%fused_computation | custom fusion | bytes 18883584 | tf_op jit(solution)/shard_map/gather | solution.py:50
  570.0 16.9 %reshape.238 = f32[384,6,2048]{2,1,0:T(8,128)} reshape(bf16[2304,2048]{1,0:T(8,128)(2,1)} %gather_fusion) | data formatting | bytes 28311552 | tf_op jit(solution)/shard_map/convert_element_type | solution.py:50
  586.9 14.6 %multiply_reduce_fusion = bf16[384,2048]{1,0:T(8,128)(2,1)} fusion(f32[384,6,2048]{2,1,0:T(8,128)} %reshape.238, f32[384,6]{1,0:T(8,128)S(1)} %copy.105), kind=kLoop, calls=%fused_computation.3 | loop fusion | flops 8650752 | bytes 20456448 | tf_op jit(solution)/shard_map/reduce_sum | solution.py:51
  601.6 44.4 %reduce-scatter.2.cloned.1.call-done = bf16[96,2048]{1,0:T(8,128)(2,1)} async-done(((bf16[384,2048]{1,0:T(8,128)(2,1)}), bf16[96,2048]{1,0:T(8,128)(2,1)}) %reduce-scatter.2.cloned.1.call-update) | async-done | bytes 393232 | tf_op jit(solution)/shard_map/reduce_scatter | solution.py:111
  646.0 2.1 fusion.21
  (46 shorter events, 1.6 us)
Async XLA Ops:
  6.5 340.4 %copy-start = (bf16[2,352,2048]{2,1,0:T(8,128)(2,1)S(1)}, bf16[2,352,2048]{2,1,0:T(8,128)(2,1)}, u32[]{:S(2)}) copy-start(bf16[2,352,2048]{2,1,0:T(8,128)(2,1)} %param.15) | copy-start | bytes 8650756
  6.5 97.6 %all-gather.3.cloned.1.call-start = ((), (), s32[]{:S(2)}) async-start(), calls=%async_computation.5 | async-start | bytes 10485760 | tf_op jit(solution)/shard_map/all_gather | solution.py:89
  7.3 131.1 %all-gather.5.cloned.1.call-start = ((), (), s32[]{:S(2)}) async-start(), calls=%async_computation.6 | async-start | bytes 1966080 | tf_op jit(solution)/shard_map/all_gather | solution.py:97
  104.1 5.9 copy-start.9
  104.1 6.8 %copy-start.7 = (s32[1,384,6]{1,0,2:T(1,128)S(1)}, s32[1,384,6]{1,0,2:T(1,128)}, u32[]{:S(2)}) copy-start(s32[1,384,6]{1,0,2:T(1,128)} %param.13) | copy-start | bytes 27652
  109.1 0.9 copy-start.2
  111.1 1.9 copy-start.4
  362.9 5.5 copy-start.8
  362.9 5.7 copy-start.5
  362.9 6.0 copy-start.3
  362.9 6.0 copy-start.6
  362.9 182.6 %all-to-all-start.3 = ((bf16[32,2,48,2048]{3,2,1,0:T(8,128)(2,1)}), bf16[32,2,48,2048]{3,2,1,0:T(8,128)(2,1)}, u32[]{:S(2)}, u32[]{:S(2)}) async-start(bf16[32,2,48,2048]{3,2,1,0:T(8,128)(2,1)} %copy.114), calls=%async_computation.3 | async-start | bytes 25165824 | tf_op jit(solution)/shard_map/all_to_all | solution.py:109
  368.4 277.6 %reduce-scatter.2.cloned.1.call-start = ((), (), s32[]{:S(2)}) async-start(), calls=%async_computation.7 | async-start | bytes 1966080 | tf_op jit(solution)/shard_map/reduce_scatter | solution.py:111
  586.9 61.1 %copy-start.1 = (bf16[2,352,2048]{2,1,0:T(8,128)(2,1)S(1)}, bf16[2,352,2048]{2,1,0:T(8,128)(2,1)}, u32[]{:S(2)}) copy-start(bf16[2,352,2048]{2,1,0:T(8,128)(2,1)} %param.15) | copy-start | bytes 8650756
Sparse Core Ops, SparseCore 0:
  9.0 95.0 all-gather.2
  111.1 27.2 all-gather.4
  601.7 44.2 reduce-scatter.1
where the time goes:
time: 657 us; the launch traced here: 655 us
  waiting for transfers between devices  260 us (40%)
  blocking collectives  191 us (29%)
  local copies, waits for them, and re-layouts  116 us (18%)
  matrix products  36.4 us (6%)
  other arithmetic  33 us (5%)
  between operations  13.4 us (2%)
    all_to_all x1, waiting for transfers between devices, on_device(): lax.all_to_all(partial_out, 'exp', split_axis=0, concat_axis=0, tiled=True)  176 us
    all_to_all x1, blocking collectives, on_device(): lax.all_to_all(outgoing, 'exp', split_axis=0, concat_axis=0, tiled=True)  148 us
    reduce_scatter x1, waiting for transfers between devices, on_device(): lax.psum_scatter(combine_rows(out_table, slot_index, gate_vals).astype(jn...  44.4 us
    all_gather x1, waiting for transfers between devices, on_device(): lax.all_gather(w_out, 'seq', axis=0, tiled=True)  30.5 us
    all_to_all x1, blocking collectives, on_device(): lax.all_to_all(packed, 'seq', split_axis=2, concat_axis=0, tiled=True)  27.4 us
    gather x1, local copies, waits for them, and re-layouts, combine_rows(): picked = out_table[slot_index].astype(jnp.float32)  24.5 us
    scatter x1, local copies, waits for them, and re-layouts, scatter_rows(): empty.at[slot_index.reshape(-1)].set(spread.reshape(-1, feature_width))  23.8 us
    convert_element_type x1, local copies, waits for them, and re-layouts, combine_rows(): picked = out_table[slot_index].astype(jnp.float32)  16.9 us
  transfers between devices with their start and end apart: 4, of which 4 were waited for; matrix products, arithmetic and copies ran while one was open for 7% of the time, Pallas kernels for 0%

commit v1 on v0

--- a/solution.py
+++ b/solution.py
@@ -23,12 +23,17 @@
 
 def slot_ranks(chosen, block_rows, experts):
     blocks = chosen.shape[0] // block_rows
-    grouped = chosen.reshape(blocks, block_rows * chosen.shape[1])
+    width = block_rows * chosen.shape[1]
+    grouped = chosen.reshape(blocks, width)
     hits = (grouped[:, :, None] == jnp.arange(experts, dtype=jnp.int32)[None, None, :]).astype(
-        jnp.int32
+        jnp.bfloat16
     )
-    ranks = jnp.sum(jnp.cumsum(hits, axis=1) * hits, axis=-1) - 1
-    return ranks.reshape(chosen.shape)
+    lower = jnp.arange(width)[:, None] >= jnp.arange(width)[None, :]
+    counts = jnp.einsum(
+        "ij,bje->bie", lower.astype(jnp.bfloat16), hits, preferred_element_type=jnp.float32
+    )
+    ranks = jnp.sum(counts * hits.astype(jnp.float32), axis=-1) - 1
+    return ranks.astype(jnp.int32).reshape(chosen.shape)
 
 
 def expert_part(received, w_gate_up, w_down):
@@ -38,17 +43,24 @@
 
 
 def scatter_rows(normed_rows, slot_index, buffer_rows):
-    feature_width = normed_rows.shape[1]
-    spread = jnp.broadcast_to(
-        normed_rows[:, None, :], (slot_index.shape[0], slot_index.shape[1], feature_width)
+    slots = jnp.arange(buffer_rows, dtype=jnp.int32)
+    select = jnp.sum(
+        (slot_index[None, :, :] == slots[:, None, None]).astype(jnp.bfloat16), axis=-1
     )
-    empty = jnp.zeros((buffer_rows, feature_width), jnp.bfloat16)
-    return empty.at[slot_index.reshape(-1)].set(spread.reshape(-1, feature_width))
+    return jnp.dot(select, normed_rows, preferred_element_type=jnp.float32).astype(jnp.bfloat16)
 
 
 def combine_rows(out_table, slot_index, gate_vals):
-    picked = out_table[slot_index].astype(jnp.float32)
-    return jnp.sum(gate_vals[:, :, None] * picked, axis=1)
+    slots = jnp.arange(out_table.shape[0], dtype=jnp.int32)
+    weights = jnp.sum(
+        jnp.where(slot_index[:, :, None] == slots[None, None, :], gate_vals[:, :, None], 0.0),
+        axis=1,
+    )
+    high = weights.astype(jnp.bfloat16)
+    low = (weights - high.astype(jnp.float32)).astype(jnp.bfloat16)
+    return jnp.dot(high, out_table, preferred_element_type=jnp.float32) + jnp.dot(
+        low, out_table, preferred_element_type=jnp.float32
+    )
 
 
 def on_device(resid, qkv, w_out, norm_gain, router_w, expert_ids, w_gate_up, w_down):

time: 657 us -> 583 us (0.89)
  local copies, waits for them, and re-layouts: 116 us -> 23.2 us
  matrix products: 36.4 us -> 68 us
  other arithmetic: 33 us -> 18.9 us
    dot_general x0 -> x4, matrix products: none -> 30 us  [the longest x1 11 us: combine_rows(): jnp.dot(high, out_table, preferred_element_type=jnp.float32)]
    gather x1 -> x0, local copies, waits for them, and re-layouts: 24.5 us -> none  [combine_rows(): picked = out_table[slot_index].astype(jnp.float32)]
    scatter x1 -> x0, local copies, waits for them, and re-layouts: 23.8 us -> none  [scatter_rows(): empty.at[slot_index.reshape(-1)].set(spread.reshape(-1, feature_width))]
    convert_element_type x1 -> x3, local copies, waits for them, and re-layouts: 16.9 us -> 0.47 us  [slot_ranks(): return ranks.astype(jnp.int32).reshape(chosen.shape)]
    reshape x1 -> x0, local copies, waits for them, and re-layouts: 15.8 us -> none  [scatter_rows(): spread.reshape(-1, feature_width)]
    another operation x4 -> x0, other arithmetic: 12.7 us -> none
    all_gather x1, waiting for transfers between devices: 8.66 us -> 20.6 us  [on_device(): gathered = lax.all_gather(normed, 'seq', axis=0, tiled=True)]
    all_to_all x1, waiting for transfers between devices: 176 us -> 167 us  [on_device(): lax.all_to_all(partial_out, 'exp', split_axis=0, concat_axis=0, tiled=True)]
where the time goes in v1:
time: 583 us
  waiting for transfers between devices  263 us (45%)
  blocking collectives  190 us (33%)
  matrix products  68 us (12%)
  local copies, waits for them, and re-layouts  23.2 us (4%)
  other arithmetic  18.9 us (3%)
  between operations  13.3 us (2%)
    all_to_all x1, waiting for transfers between devices, on_device(): lax.all_to_all(partial_out, 'exp', split_axis=0, concat_axis=0, tiled=True)  167 us
    all_to_all x1, blocking collectives, on_device(): lax.all_to_all(outgoing, 'exp', split_axis=0, concat_axis=0, tiled=True)  148 us
    reduce_scatter x1, waiting for transfers between devices, on_device(): lax.psum_scatter(combine_rows(out_table, slot_index, gate_vals).astype(jn...  44.4 us
    all_gather x1, waiting for transfers between devices, on_device(): lax.all_gather(w_out, 'seq', axis=0, tiled=True)  30.5 us
    all_to_all x1, blocking collectives, on_device(): lax.all_to_all(packed, 'seq', split_axis=2, concat_axis=0, tiled=True)  27.4 us
    all_gather x1, waiting for transfers between devices, on_device(): gathered = lax.all_gather(normed, 'seq', axis=0, tiled=True)  20.6 us
    dot_general x1, matrix products, expert_part(): jnp.einsum('aend,edgf->aengf', received, w_gate_up, preferred_element_typ...  16 us
    all_to_all x1, blocking collectives, on_device(): lax.all_to_all(attended.reshape(seq_length, 1, local_width), 'seq', split...  15.5 us
  transfers between devices with their start and end apart: 4, of which 4 were waited for; matrix products, arithmetic and copies ran while one was open for 7% of the time, Pallas kernels for 0%

profile of v1, /device:TPU:0, one launch (start us, length us, event | category | flops | bytes accessed | tf_op | source)
XLA Modules:
  0.0 582.8 jit_solution(9345225432618470734)
XLA Ops:
  6.5 0.7 all-gather.3.cloned.1.call-update
  7.3 2.9 reshape.139
  10.2 1.5 copy.111
  11.7 27.4 %all_to_all.43 = bf16[96,3,4,512]{3,0,1,2:T(8,128)(2,1)S(1)} all-to-all(bf16[96,3,4,512]{3,0,1,2:T(8,128)(2,1)S(1)} %copy.111), channel_id=1, replica_groups=mesh['seq'=4,'exp'=32] {'seq'}, dimensions={2} | all-to-all | bytes 2359296 | tf_op jit(solution)/shard_map/all_to_all | solution.py:75
  39.2 0.1 copy.112
  39.2 1.0 fusion.48
  40.2 1.9 copy.117
  42.2 1.9 copy.113
  44.1 0.9 copy.114
  45.0 3.5 fusion.49
  48.5 2.2 convolution_convert_fusion.1
  50.7 0.5 broadcast.124
  51.2 1.5 reduce.1
  52.7 1.2 copy.150
  53.9 1.0 reshape.149
  54.9 15.5 %all_to_all.44 = bf16[4,2,24576]{2,1,0:T(2,128)(2,1)S(1)} all-to-all(bf16[4,2,24576]{2,1,0:T(2,128)(2,1)} %reshape.149), channel_id=1, replica_groups=mesh['seq'=4,'exp'=32] {'seq'}, dimensions={0} | all-to-all | bytes 786432 | tf_op jit(solution)/shard_map/all_to_all | solution.py:95
  70.4 1.7 reshape.150
  72.1 1.2 copy.138
  73.3 0.3 copy.120
  73.7 30.5 %all-gather.3.cloned.1.call-done = bf16[2048,2048]{1,0:T(8,128)(2,1)} async-done(((bf16[512,2048]{1,0:T(8,128)(2,1)}), bf16[2048,2048]{1,0:T(8,128)(2,1)}) %all-gather.3.cloned.1.call-update) | async-done | bytes 8388624 | tf_op jit(solution)/shard_map/all_gather | solution.py:101
  104.1 5.0 multiply_reduce_fusion.1
  109.2 0.9 copy-done.2
  110.1 0.9 multiply_convert_fusion
  111.0 0.1 copy.121
  111.2 0.2 eq.56
  111.3 0.5 fusion.28
  111.8 0.2 convert_element_type.105
  112.0 0.1 copy.125
  112.2 5.6 fusion.2
  117.8 20.6 %all-gather.5.cloned.1.call-done = bf16[384,2048]{1,0:T(8,128)(2,1)} async-done(((bf16[96,2048]{1,0:T(8,128)(2,1)}), bf16[384,2048]{1,0:T(8,128)(2,1)}) %all-gather.5.cloned.1.call-update) | async-done | bytes 1572880 | tf_op jit(solution)/shard_map/all_gather | solution.py:109
  138.4 8.7 %convolution_convert_fusion = bf16[3072,2048]{1,0:T(8,128)(2,1)S(1)} fusion(bf16[3072,384]{1,0:T(8,128)(2,1)} %fusion.2, bf16[384,2048]{1,0:T(8,128)(2,1)} %all-gather.5.cloned.1.call-done), kind=kOutput, calls=%fused_computation.9 | convolution fusion | flops 4838129664 | bytes 16515072 | tf_op jit(solution)/shard_map/dot_general | solution.py:50
  147.1 147.5 %all_to_all.45 = bf16[32,2,48,2048]{3,2,1,0:T(8,128)(2,1)} all-to-all(bf16[32,2,48,2048]{3,2,1,0:T(8,128)(2,1)S(1)} %bitcast.99), channel_id=1, replica_groups=mesh['seq'=4,'exp'=32] {'exp'}, dimensions={0} | all-to-all | bytes 25165824 | tf_op jit(solution)/shard_map/all_to_all | solution.py:119
  294.6 16.0 %fusion.8 = f32[32,2,48,2,352]{4,2,3,0,1:T(8,128)} fusion(bf16[2,2048,2,352]{1,3,2,0:T(8,128)(2,1)} %param.14, bf16[32,2,48,2048]{3,2,1,0:T(8,128)(2,1)} %all_to_all.45), kind=kOutput, calls=%fused_computation.16 | convolution fusion | flops 8858370048 | bytes 27000832 | tf_op jit(solution)/shard_map/aend,edgf->aengf/dot_general | solution.py:40
  310.6 10.7 %convert_bitcast_fusion = bf16[32,2,48,2048]{3,2,0,1:T(8,128)(2,1)S(1)} fusion(bf16[2,352,2048]{2,1,0:T(8,128)(2,1)S(1)} %copy-done, f32[32,2,48,2,352]{4,2,3,0,1:T(8,128)} %fusion.8), kind=kOutput, calls=%fused_computation.8 | convolution fusion | flops 4441964544 | bytes 24117248 | tf_op jit(solution)/shard_map/aenf,efd->aend/dot_general | solution.py:42
  321.3 5.2 copy.128
  326.5 5.2 all-to-all-start.3
  331.7 0.3 reduce-scatter.2.cloned.1.call-start
  332.0 0.2 convert_element_type.102
  332.2 0.1 fusion.41
  332.3 0.1 copy.123
  332.4 0.6 fusion.50
  333.0 0.1 select_reduce_fusion.1
  333.2 8.6 %select_reduce_fusion = f32[384,3072]{1,0:T(8,128)} fusion(f32[384,6]{0,1:T(8,128)S(1)} %multiply_divide_fusion, s32[384,6]{0,1:T(8,128)S(1)} %copy.123), kind=kLoop, calls=%fused_computation.2 | loop fusion | flops 20054016 | bytes 4737024 | tf_op jit(solution)/shard_map/reduce_sum | solution.py:55
  341.7 167.1 %all-to-all-done.3 = bf16[32,2,48,2048]{3,2,1,0:T(8,128)(2,1)} async-done(((bf16[32,2,48,2048]{3,2,1,0:T(8,128)(2,1)}), bf16[32,2,48,2048]{3,2,1,0:T(8,128)(2,1)}, u32[]{:S(2)}, u32[]{:S(2)}) %all-to-all-start.3) | async-done | bytes 12582944 | tf_op jit(solution)/shard_map/all_to_all | solution.py:121
  508.9 11.0 %fusion.32 = f32[384,2048]{1,0:T(8,128)S(1)} fusion(bf16[3072,2048]{1,0:T(8,128)(2,1)} %bitcast.26, f32[384,3072]{1,0:T(8,128)} %select_reduce_fusion), kind=kOutput, calls=%fused_computation.33 | convolution fusion | flops 4833017856 | bytes 20447232 | tf_op jit(solution)/shard_map/dot_general | solution.py:61
  519.9 9.8 %add_convert_fusion = bf16[384,2048]{1,0:T(8,128)(2,1)} fusion(f32[384,2048]{1,0:T(8,128)S(1)} %fusion.32, bf16[3072,2048]{1,0:T(8,128)(2,1)} %bitcast.26, f32[384,3072]{1,0:T(8,128)S(1)} %copy-done.3), kind=kOutput, calls=%fused_computation.17 | convolution fusion | flops 4838129664 | bytes 22020096 | tf_op jit(solution)/shard_map/dot_general | solution.py:61
  529.7 44.4 %reduce-scatter.2.cloned.1.call-done = bf16[96,2048]{1,0:T(8,128)(2,1)} async-done(((bf16[384,2048]{1,0:T(8,128)(2,1)}), bf16[96,2048]{1,0:T(8,128)(2,1)}) %reduce-scatter.2.cloned.1.call-update) | async-done | bytes 393232 | tf_op jit(solution)/shard_map/reduce_scatter | solution.py:123
  574.2 2.1 fusion.36
  (28 shorter events, 0.3 us)
Async XLA Ops:
  6.5 304.1 %copy-start = (bf16[2,352,2048]{2,1,0:T(8,128)(2,1)S(1)}, bf16[2,352,2048]{2,1,0:T(8,128)(2,1)}, u32[]{:S(2)}) copy-start(bf16[2,352,2048]{2,1,0:T(8,128)(2,1)} %param.15) | copy-start | bytes 8650756
  6.5 97.6 %all-gather.3.cloned.1.call-start = ((), (), s32[]{:S(2)}) async-start(), calls=%async_computation.5 | async-start | bytes 10485760 | tf_op jit(solution)/shard_map/all_gather | solution.py:101
  7.3 131.1 %all-gather.5.cloned.1.call-start = ((), (), s32[]{:S(2)}) async-start(), calls=%async_computation.6 | async-start | bytes 1966080 | tf_op jit(solution)/shard_map/all_gather | solution.py:109
  104.1 6.0 %copy-start.7 = (f32[2048]{0:T(1024)S(1)}, f32[2048]{0:T(1024)}, u32[]{:S(2)}) copy-start(f32[2048]{0:T(1024)} %param.11) | copy-start | bytes 24580
  104.1 6.9 %copy-start.6 = (s32[1,384,6]{1,0,2:T(1,128)S(1)}, s32[1,384,6]{1,0,2:T(1,128)}, u32[]{:S(2)}) copy-start(s32[1,384,6]{1,0,2:T(1,128)} %param.13) | copy-start | bytes 27652
  109.1 1.0 copy-start.2
  326.5 5.9 %copy-start.4 = (bf16[384,2048]{1,0:T(8,128)(2,1)S(1)}, bf16[384,2048]{1,0:T(8,128)(2,1)}, u32[]{:S(2)}) copy-start(bf16[384,2048]{1,0:T(8,128)(2,1)} %all-gather.5.cloned.1.call-done) | copy-start | bytes 4718596
  326.5 5.9 %copy-start.5 = (bf16[2048,64]{0,1:T(8,128)(2,1)S(1)}, bf16[2048,64]{0,1:T(8,128)(2,1)}, u32[]{:S(2)}) copy-start(bf16[2048,64]{0,1:T(8,128)(2,1)} %param.12) | copy-start | bytes 786436
  326.5 182.3 %all-to-all-start.3 = ((bf16[32,2,48,2048]{3,2,1,0:T(8,128)(2,1)}), bf16[32,2,48,2048]{3,2,1,0:T(8,128)(2,1)}, u32[]{:S(2)}, u32[]{:S(2)}) async-start(bf16[32,2,48,2048]{3,2,1,0:T(8,128)(2,1)} %copy.128), calls=%async_computation.3 | async-start | bytes 25165824 | tf_op jit(solution)/shard_map/all_to_all | solution.py:121
  331.7 242.5 %reduce-scatter.2.cloned.1.call-start = ((), (), s32[]{:S(2)}) async-start(), calls=%async_computation.7 | async-start | bytes 1966080 | tf_op jit(solution)/shard_map/reduce_scatter | solution.py:123
  508.9 11.0 %copy-start.3 = (f32[384,3072]{1,0:T(8,128)S(1)}, f32[384,3072]{1,0:T(8,128)}, u32[]{:S(2)}) copy-start(f32[384,3072]{1,0:T(8,128)} %select_reduce_fusion) | copy-start | bytes 14155780
  519.9 56.3 %copy-start.1 = (bf16[2,352,2048]{2,1,0:T(8,128)(2,1)S(1)}, bf16[2,352,2048]{2,1,0:T(8,128)(2,1)}, u32[]{:S(2)}) copy-start(bf16[2,352,2048]{2,1,0:T(8,128)(2,1)} %param.15) | copy-start | bytes 8650756
Sparse Core Ops, SparseCore 0:
  9.0 95.0 all-gather.2
  111.1 27.2 all-gather.4
  529.9 44.2 reduce-scatter.1

commit v2 on v1

--- a/solution.py
+++ b/solution.py
@@ -63,55 +63,58 @@
     )
 
 
+def seq_shift(x, shift, size):
+    return lax.ppermute(x, "seq", [(i, (i + shift) % size) for i in range(size)])
+
+
 def on_device(resid, qkv, w_out, norm_gain, router_w, expert_ids, w_gate_up, w_down):
     row_count = resid.shape[1]
     model_width = resid.shape[2]
     seq_size = lax.axis_size("seq")
     exp_size = lax.axis_size("exp")
+    me = lax.axis_index("seq")
     seq_length = row_count * seq_size
     head_local = H // seq_size
     local_width = head_local * HD
-    packed = qkv.reshape(row_count, 3, seq_size, local_width)
-    regrouped = lax.all_to_all(packed, "seq", split_axis=2, concat_axis=0, tiled=True)
-    queries = regrouped[:, 0, 0].reshape(seq_length, head_local, HD)
-    keys_all = regrouped[:, 1, 0].reshape(seq_length, head_local, HD)
-    values_all = regrouped[:, 2, 0].reshape(seq_length, head_local, HD)
-    query_block = min(seq_length, 512)
-
-    def attend_block(query_rows):
-        scores = jnp.einsum(
-            "qhd,khd->hqk", query_rows, keys_all, preferred_element_type=jnp.float32
-        ) / math.sqrt(HD)
-        weights = jax.nn.softmax(scores, axis=-1).astype(jnp.bfloat16)
-        mixed_heads = jnp.einsum(
-            "hqk,khd->qhd", weights, values_all, preferred_element_type=jnp.float32
-        )
-        return mixed_heads.reshape(query_rows.shape[0], local_width).astype(jnp.bfloat16)
-
-    attended = lax.map(
-        attend_block, queries.reshape(seq_length // query_block, query_block, head_local, HD)
+    packed = qkv[0].reshape(row_count, 3, seq_size, local_width)
+    pieces = []
+    for shift in range(seq_size):
+        target = (me + shift) % seq_size
+        piece = lax.dynamic_index_in_dim(packed, target, axis=2, keepdims=False)
+        pieces.append(piece if shift == 0 else seq_shift(piece, shift, seq_size))
+    regrouped = jnp.stack(pieces, axis=0).reshape(seq_length, 3, local_width)
+    queries = regrouped[:, 0].reshape(seq_length, head_local, HD)
+    keys_all = regrouped[:, 1].reshape(seq_length, head_local, HD)
+    values_all = regrouped[:, 2].reshape(seq_length, head_local, HD)
+    scores = jnp.einsum(
+        "qhd,khd->hqk", queries, keys_all, preferred_element_type=jnp.float32
+    ) / math.sqrt(HD)
+    weights = jax.nn.softmax(scores, axis=-1).astype(jnp.bfloat16)
+    attended = jnp.einsum(
+        "hqk,khd->qhd", weights, values_all, preferred_element_type=jnp.float32
+    ).reshape(seq_length, local_width).astype(jnp.bfloat16)
+    partial = jnp.dot(attended, w_out, preferred_element_type=jnp.float32).reshape(
+        seq_size, row_count, model_width
     )
-    attended = attended.reshape(seq_length, local_width)
-    back = lax.all_to_all(
-        attended.reshape(seq_length, 1, local_width), "seq", split_axis=0, concat_axis=1, tiled=True
-    )
-    point_rows = back.reshape(row_count, model_width)
-    projected = jnp.dot(
-        point_rows,
-        lax.all_gather(w_out, "seq", axis=0, tiled=True),
-        preferred_element_type=jnp.float32,
-    )
+    projected = partial[0]
+    for shift in range(1, seq_size):
+        projected = projected + seq_shift(partial[shift], -shift, seq_size)
     mixed = resid[0].astype(jnp.float32) + projected
     meansq = jnp.mean(mixed * mixed, axis=-1, keepdims=True)
     normed = (mixed * lax.rsqrt(meansq + epsilon) * norm_gain).astype(jnp.bfloat16)
     exp_local = w_gate_up.shape[0]
     slot_cap = row_count // 8
-    gathered = lax.all_gather(normed, "seq", axis=0, tiled=True)
-    chosen = expert_ids[0]
+    gathered = jnp.concatenate(
+        [normed] + [seq_shift(normed, shift, seq_size) for shift in range(1, seq_size)], axis=0
+    )
+    blocks_abs = (me - jnp.arange(seq_size, dtype=jnp.int32)) % seq_size
+    chosen = jnp.take(expert_ids[0].reshape(seq_size, row_count, -1), blocks_abs, axis=0).reshape(
+        seq_length, -1
+    )
     gate_vals = gate_weights(gathered, router_w, chosen)
     ranks = slot_ranks(chosen, row_count, EXPERTS)
     owner_rows = seq_size * slot_cap
-    source_block = (jnp.arange(seq_length, dtype=jnp.int32) // row_count)[:, None]
+    source_block = jnp.repeat(blocks_abs, row_count)[:, None]
     slot_index = chosen * owner_rows + source_block * slot_cap + ranks
     outgoing = scatter_rows(gathered, slot_index, EXPERTS * owner_rows)
     outgoing = outgoing.reshape(exp_size, exp_local, owner_rows, model_width)
@@ -120,12 +123,14 @@
     ).astype(jnp.bfloat16)
     returned = lax.all_to_all(partial_out, "exp", split_axis=0, concat_axis=0, tiled=True)
     out_table = returned.reshape(-1, model_width)
-    expert_sum = lax.psum_scatter(
-        combine_rows(out_table, slot_index, gate_vals).astype(jnp.bfloat16),
-        "seq",
-        scatter_dimension=0,
-        tiled=True,
-    ).astype(jnp.float32)
+    combined = combine_rows(out_table, slot_index, gate_vals).reshape(
+        seq_size, row_count, model_width
+    )
+    expert_sum = combined[0]
+    for shift in range(1, seq_size):
+        expert_sum = expert_sum + seq_shift(
+            combined[shift].astype(jnp.bfloat16), -shift, seq_size
+        ).astype(jnp.float32)
     return (mixed + expert_sum).astype(jnp.bfloat16).reshape(1, row_count, model_width)
 
 

time: 583 us -> 553 us (0.949)
  the two profiles are of different devices: /device:TPU:0 before, /device:TPU:48 now
where the time goes in v2:
time: 553 us; the launch traced here: 548 us
  waiting for transfers between devices  267 us (48%)
  blocking collectives  145 us (26%)
  matrix products  60.6 us (11%)
  starting transfers between devices  31.6 us (6%)
  local copies, waits for them, and re-layouts  25.4 us (5%)
  other arithmetic  17.5 us (3%)
    all_to_all x1, waiting for transfers between devices, on_device(): lax.all_to_all(partial_out, 'exp', split_axis=0, concat_axis=0, tiled=True)  188 us
    all_to_all x1, blocking collectives, on_device(): lax.all_to_all(outgoing, 'exp', split_axis=0, concat_axis=0, tiled=True)  145 us
    ppermute x12, waiting for transfers between devices, seq_shift(): lax.ppermute(x, 'seq', [(i, (i + shift) % size) for i in range(size)])  79.7 us
    all_to_all x1, starting transfers between devices, on_device(): lax.all_to_all(partial_out, 'exp', split_axis=0, concat_axis=0, tiled=True)  16.8 us
    dot_general x1, matrix products, expert_part(): jnp.einsum('aend,edgf->aengf', received, w_gate_up, preferred_element_typ...  15.9 us
    ppermute x12, starting transfers between devices, seq_shift(): lax.ppermute(x, 'seq', [(i, (i + shift) % size) for i in range(size)])  14.8 us
  transfers between devices with their start and end apart: 13, of which 9 were waited for; matrix products, arithmetic and copies ran while one was open for 3% of the time, Pallas kernels for 0%

profile of v2, /device:TPU:48, one launch (start us, length us, event | category | flops | bytes accessed | tf_op | source)
XLA Modules:
  0.0 548.0 jit_solution(15126770422562671379)
XLA Ops:
  0.0 2.9 reshape_squeeze.15
  2.9 5.1 constant_dynamic-slice_fusion.3
  8.1 0.8 copy.108
  8.8 2.8 collective-permute-start.2
  11.6 0.7 copy.109
  12.3 0.8 collective-permute-start.1
  13.1 0.7 copy.110
  13.9 0.9 collective-permute-start
  15.0 0.6 gather_fusion
  15.8 8.7 %collective-permute-done.2 = bf16[96,3,512]{2,0,1:T(8,128)(2,1)} collective-permute-done((bf16[96,3,512]{2,0,1:T(8,128)(2,1)}, bf16[96,3,512]{2,0,1:T(8,128)(2,1)}, u32[]{:S(2)}, u32[]{:S(2)}) %collective-permute-start.2) | collective-permute-done | bytes 294944 | tf_op jit(solution)/shard_map/ppermute | solution.py:67
  24.5 4.4 collective-permute-done
  28.9 1.3 pad_maximum_fusion.1
  30.3 0.9 fusion.58
  31.3 1.9 copy.78
  33.2 1.9 copy.79
  35.1 0.9 copy.80
  36.0 3.4 fusion.59
  39.5 2.2 convolution_convert_fusion.1
  41.8 1.0 fusion.61
  42.8 1.5 fusion.56
  44.3 2.1 collective-permute-start.4
  46.3 1.4 collective-permute-start.3
  47.8 0.5 fusion.28
  49.0 33.1 %collective-permute-done.5 = f32[96,2048]{1,0:T(8,128)} collective-permute-done((f32[96,2048]{1,0:T(8,128)}, f32[96,2048]{1,0:T(8,128)}, u32[]{:S(2)}, u32[]{:S(2)}) %collective-permute-start.5) | collective-permute-done | bytes 786464 | tf_op jit(solution)/shard_map/ppermute | solution.py:67
  82.1 0.6 collective-permute-done.3
  82.7 2.2 multiply_reduce_fusion.1
  85.0 0.9 copy-done.3
  86.0 2.4 collective-permute-start.8
  88.4 1.2 collective-permute-start.6
  89.6 3.9 fusion.2
  93.5 11.6 %collective-permute-done.8 = bf16[96,2048]{1,0:T(8,128)(2,1)S(1)} collective-permute-done((bf16[96,2048]{1,0:T(8,128)(2,1)S(1)}, bf16[96,2048]{1,0:T(8,128)(2,1)S(1)}, u32[]{:S(2)}, u32[]{:S(2)}) %collective-permute-start.8) | collective-permute-done | bytes 393248 | tf_op jit(solution)/shard_map/ppermute | solution.py:67
  105.1 3.6 collective-permute-done.6
  108.7 7.0 %convolution_convert_fusion = bf16[3072,2048]{1,0:T(8,128)(2,1)S(1)} fusion(bf16[3072,384]{1,0:T(8,128)(2,1)S(1)} %fusion.2, bf16[96,2048]{1,0:T(8,128)(2,1)S(1)} %collective-permute-done.8, bf16[96,2048]{1,0:T(8,128)(2,1)S(1)} %collective-permute-done.7, bf16[96,2048]{1,0:T(8,128)(2,1)S(1)} %collective-permute-done.6, ...), kind=kOutput, calls=%fused_computation.10 | convolution fusion | flops 4844421120 | bytes 16515072 | tf_op jit(solution)/shard_map/dot_general | solution.py:50
  115.7 145.3 %all_to_all.10 = bf16[32,2,48,2048]{3,2,1,0:T(8,128)(2,1)} all-to-all(bf16[32,2,48,2048]{3,2,1,0:T(8,128)(2,1)S(1)} %bitcast.96), channel_id=1, replica_groups=mesh['seq'=4,'exp'=32] {'exp'}, dimensions={0} | all-to-all | bytes 25165824 | tf_op jit(solution)/shard_map/all_to_all | solution.py:122
  261.0 15.9 %fusion.8 = f32[32,2,48,2,352]{4,2,3,0,1:T(8,128)} fusion(bf16[2,2048,2,352]{1,3,2,0:T(8,128)(2,1)} %param.14, bf16[32,2,48,2048]{3,2,1,0:T(8,128)(2,1)} %all_to_all.10), kind=kOutput, calls=%fused_computation.17 | convolution fusion | flops 8858370048 | bytes 27000832 | tf_op jit(solution)/shard_map/aend,edgf->aengf/dot_general | solution.py:40
  277.0 10.7 %convert_bitcast_fusion = bf16[32,2,48,2048]{3,2,0,1:T(8,128)(2,1)S(1)} fusion(bf16[2,352,2048]{2,1,0:T(8,128)(2,1)S(1)} %copy-done, f32[32,2,48,2,352]{4,2,3,0,1:T(8,128)} %fusion.8), kind=kOutput, calls=%fused_computation.9 | convolution fusion | flops 4441964544 | bytes 24117248 | tf_op jit(solution)/shard_map/aenf,efd->aend/dot_general | solution.py:42
  287.7 5.1 copy.90
  292.8 16.8 %all-to-all-start.1 = ((bf16[32,2,48,2048]{3,2,1,0:T(8,128)(2,1)}), bf16[32,2,48,2048]{3,2,1,0:T(8,128)(2,1)}, u32[]{:S(2)}, u32[]{:S(2)}) async-start(bf16[32,2,48,2048]{3,2,1,0:T(8,128)(2,1)} %copy.90), calls=%async_computation.1 | async-start | bytes 25165824 | tf_op jit(solution)/shard_map/all_to_all | solution.py:124
  309.7 0.6 fusion.45
  310.5 8.6 %select_reduce_fusion = f32[384,3072]{1,0:T(8,128)} fusion(f32[384,6]{0,1:T(8,128)S(1)} %multiply_divide_fusion, s32[384,6]{0,1:T(8,128)S(1)} %get-tuple-element.7), kind=kLoop, calls=%fused_computation.3 | loop fusion | flops 20054016 | bytes 4737024 | tf_op jit(solution)/shard_map/reduce_sum | solution.py:55
  319.1 187.5 %all-to-all-done.1 = bf16[32,2,48,2048]{3,2,1,0:T(8,128)(2,1)} async-done(((bf16[32,2,48,2048]{3,2,1,0:T(8,128)(2,1)}), bf16[32,2,48,2048]{3,2,1,0:T(8,128)(2,1)}, u32[]{:S(2)}, u32[]{:S(2)}) %all-to-all-start.1) | async-done | bytes 12582944 | tf_op jit(solution)/shard_map/all_to_all | solution.py:124
  506.6 11.0 %fusion.32 = f32[384,2048]{1,0:T(8,128)S(1)} fusion(bf16[3072,2048]{1,0:T(8,128)(2,1)} %bitcast.27, f32[384,3072]{1,0:T(8,128)} %select_reduce_fusion), kind=kOutput, calls=%fused_computation.35 | convolution fusion | flops 4833017856 | bytes 20447232 | tf_op jit(solution)/shard_map/dot_general | solution.py:61
  517.6 8.2 %fusion.60 = (bf16[384,2048]{1,0:T(8,128)(2,1)S(1)}, f32[384,2048]{1,0:T(8,128)S(1)}) fusion(f32[384,2048]{1,0:T(8,128)S(1)} %fusion.32, bf16[3072,2048]{1,0:T(8,128)(2,1)} %bitcast.27, f32[384,3072]{1,0:T(8,128)S(1)} %copy-done.5), kind=kOutput, calls=%fused_computation.95 | convolution fusion | flops 4838129664 | bytes 25165824 | tf_op jit(solution)/shard_map/dot_general | solution.py:61
  526.0 2.3 collective-permute-start.10
  528.3 1.0 collective-permute-start.9
  529.2 17.0 %collective-permute-done.11 = bf16[96,2048]{1,0:T(8,128)(2,1)S(1)} collective-permute-done((bf16[96,2048]{1,0:T(8,128)(2,1)S(1)}, bf16[96,2048]{1,0:T(8,128)(2,1)S(1)}, u32[]{:S(2)}, u32[]{:S(2)}) %collective-permute-start.11) | collective-permute-done | bytes 393248 | tf_op jit(solution)/shard_map/ppermute | solution.py:67
  546.2 0.6 collective-permute-done.9
  546.8 1.0 fusion.43
  (70 shorter events, 1.9 us)
Async XLA Ops:
  0.0 277.0 %copy-start = (bf16[2,352,2048]{2,1,0:T(8,128)(2,1)S(1)}, bf16[2,352,2048]{2,1,0:T(8,128)(2,1)}, u32[]{:S(2)}) copy-start(bf16[2,352,2048]{2,1,0:T(8,128)(2,1)} %param.15) | copy-start | bytes 8650756
  2.9 11.9 %copy-start.9 = (s32[1,384,6]{1,0,2:T(1,128)S(1)}, s32[1,384,6]{1,0,2:T(1,128)}, u32[]{:S(2)}) copy-start(s32[1,384,6]{1,0,2:T(1,128)} %param.13) | copy-start | bytes 27652
  8.8 15.7 %collective-permute-start.2 = (bf16[96,3,512]{2,0,1:T(8,128)(2,1)}, bf16[96,3,512]{2,0,1:T(8,128)(2,1)}, u32[]{:S(2)}, u32[]{:S(2)}) collective-permute-start(bf16[96,3,512]{2,0,1:T(8,128)(2,1)} %bitcast.92), channel_id=1, source_target_pairs={{0,96},{32,0},{64,32},{96,64},{1,97},{33,1},{65,33},{97,65},{2,98}... | collective-permute-start | bytes 884744 | tf_op jit(solution)/shard_map/ppermute | solution.py:67
  12.3 12.2 %collective-permute-start.1 = (bf16[96,3,512]{2,0,1:T(8,128)(2,1)}, bf16[96,3,512]{2,0,1:T(8,128)(2,1)}, u32[]{:S(2)}, u32[]{:S(2)}) collective-permute-start(bf16[96,3,512]{2,0,1:T(8,128)(2,1)} %bitcast.93), channel_id=1, source_target_pairs={{0,64},{32,96},{64,0},{96,32},{1,65},{33,97},{65,1},{97,33},{2,66}... | collective-permute-start | bytes 884744 | tf_op jit(solution)/shard_map/ppermute | solution.py:67
  13.9 15.1 %collective-permute-start = (bf16[96,3,512]{2,0,1:T(8,128)(2,1)}, bf16[96,3,512]{2,0,1:T(8,128)(2,1)}, u32[]{:S(2)}, u32[]{:S(2)}) collective-permute-start(bf16[96,3,512]{2,0,1:T(8,128)(2,1)} %bitcast.94), channel_id=1, source_target_pairs={{0,32},{32,64},{64,96},{96,0},{1,33},{33,65},{65,97},{97,1},{2,34}... | collective-permute-start | bytes 884744 | tf_op jit(solution)/shard_map/ppermute | solution.py:67
  36.0 3.4 copy-start.8
  39.5 2.3 copy-start.6
  42.8 5.5 copy-start.2
  42.8 39.9 %copy-start.7 = (bf16[1,96,2048]{2,1,0:T(8,128)(2,1)S(1)}, bf16[1,96,2048]{2,1,0:T(8,128)(2,1)}, u32[]{:S(2)}) copy-start(bf16[1,96,2048]{2,1,0:T(8,128)(2,1)} %param.8) | copy-start | bytes 1179652
  44.3 37.8 %collective-permute-start.5 = (f32[96,2048]{1,0:T(8,128)}, f32[96,2048]{1,0:T(8,128)}, u32[]{:S(2)}, u32[]{:S(2)}) collective-permute-start(f32[96,2048]{1,0:T(8,128)} %get-tuple-element.10), channel_id=1, source_target_pairs={{0,32},{32,64},{64,96},{96,0},{1,33},{33,65},{65,97},{97,1},{2,34}... | collective-permute-start | bytes 2359304 | tf_op jit(solution)/shard_map/ppermute | solution.py:67
  44.3 37.8 %collective-permute-start.4 = (f32[96,2048]{1,0:T(8,128)}, f32[96,2048]{1,0:T(8,128)}, u32[]{:S(2)}, u32[]{:S(2)}) collective-permute-start(f32[96,2048]{1,0:T(8,128)} %get-tuple-element.11), channel_id=1, source_target_pairs={{0,64},{32,96},{64,0},{96,32},{1,65},{33,97},{65,1},{97,33},{2,66}... | collective-permute-start | bytes 2359304 | tf_op jit(solution)/shard_map/ppermute | solution.py:67
  46.3 36.4 %collective-permute-start.3 = (f32[96,2048]{1,0:T(8,128)}, f32[96,2048]{1,0:T(8,128)}, u32[]{:S(2)}, u32[]{:S(2)}) collective-permute-start(f32[96,2048]{1,0:T(8,128)} %get-tuple-element.9), channel_id=1, source_target_pairs={{0,96},{32,0},{64,32},{96,64},{1,97},{33,1},{65,33},{97,65},{2,98}... | collective-permute-start | bytes 2359304 | tf_op jit(solution)/shard_map/ppermute | solution.py:67
  47.8 38.1 %copy-start.10 = (f32[2048]{0:T(1024)S(1)}, f32[2048]{0:T(1024)}, u32[]{:S(2)}) copy-start(f32[2048]{0:T(1024)} %param.11) | copy-start | bytes 24580
  85.0 0.9 copy-start.3
  86.0 19.1 %collective-permute-start.8 = (bf16[96,2048]{1,0:T(8,128)(2,1)S(1)}, bf16[96,2048]{1,0:T(8,128)(2,1)S(1)}, u32[]{:S(2)}, u32[]{:S(2)}) collective-permute-start(bf16[96,2048]{1,0:T(8,128)(2,1)S(1)} %multiply_convert_fusion), channel_id=1, source_target_pairs={{0,96},{32,0},{64,32},{96,64},{1,97},{33,1},{65,33},{97,65},{2,98}... | collective-permute-start | bytes 1179656 | tf_op jit(solution)/shard_map/ppermute | solution.py:67
  88.4 16.7 %collective-permute-start.7 = (bf16[96,2048]{1,0:T(8,128)(2,1)S(1)}, bf16[96,2048]{1,0:T(8,128)(2,1)S(1)}, u32[]{:S(2)}, u32[]{:S(2)}) collective-permute-start(bf16[96,2048]{1,0:T(8,128)(2,1)S(1)} %multiply_convert_fusion), channel_id=1, source_target_pairs={{0,64},{32,96},{64,0},{96,32},{1,65},{33,97},{65,1},{97,33},{2,66}... | collective-permute-start | bytes 1179656 | tf_op jit(solution)/shard_map/ppermute | solution.py:67
  88.4 20.3 %collective-permute-start.6 = (bf16[96,2048]{1,0:T(8,128)(2,1)S(1)}, bf16[96,2048]{1,0:T(8,128)(2,1)S(1)}, u32[]{:S(2)}, u32[]{:S(2)}) collective-permute-start(bf16[96,2048]{1,0:T(8,128)(2,1)S(1)} %multiply_convert_fusion), channel_id=1, source_target_pairs={{0,32},{32,64},{64,96},{96,0},{1,33},{33,65},{65,97},{97,1},{2,34}... | collective-permute-start | bytes 1179656 | tf_op jit(solution)/shard_map/ppermute | solution.py:67
  105.1 10.6 %copy-start.11 = (bf16[96,2048]{1,0:T(8,128)(2,1)}, bf16[96,2048]{1,0:T(8,128)(2,1)S(1)}, u32[]{:S(2)}) copy-start(bf16[96,2048]{1,0:T(8,128)(2,1)S(1)} %collective-permute-done.8) | copy-start | bytes 1179652
  105.1 10.6 %copy-start.13 = (bf16[96,2048]{1,0:T(8,128)(2,1)}, bf16[96,2048]{1,0:T(8,128)(2,1)S(1)}, u32[]{:S(2)}) copy-start(bf16[96,2048]{1,0:T(8,128)(2,1)S(1)} %collective-permute-done.7) | copy-start | bytes 1179652
  108.7 7.0 %copy-start.15 = (bf16[96,2048]{1,0:T(8,128)(2,1)}, bf16[96,2048]{1,0:T(8,128)(2,1)S(1)}, u32[]{:S(2)}) copy-start(bf16[96,2048]{1,0:T(8,128)(2,1)S(1)} %collective-permute-done.6) | copy-start | bytes 1179652
  292.8 16.9 %copy-start.12 = (bf16[96,2048]{1,0:T(8,128)(2,1)S(1)}, bf16[96,2048]{1,0:T(8,128)(2,1)}, u32[]{:S(2)}) copy-start(bf16[96,2048]{1,0:T(8,128)(2,1)} %copy-done.11) | copy-start | bytes 1179652
  292.8 16.9 %copy-start.14 = (bf16[96,2048]{1,0:T(8,128)(2,1)S(1)}, bf16[96,2048]{1,0:T(8,128)(2,1)}, u32[]{:S(2)}) copy-start(bf16[96,2048]{1,0:T(8,128)(2,1)} %copy-done.13) | copy-start | bytes 1179652
  292.8 16.9 %copy-start.16 = (bf16[96,2048]{1,0:T(8,128)(2,1)S(1)}, bf16[96,2048]{1,0:T(8,128)(2,1)}, u32[]{:S(2)}) copy-start(bf16[96,2048]{1,0:T(8,128)(2,1)} %copy-done.15) | copy-start | bytes 1179652
  292.8 16.9 %copy-start.17 = (bf16[2048,64]{0,1:T(8,128)(2,1)S(1)}, bf16[2048,64]{0,1:T(8,128)(2,1)}, u32[]{:S(2)}) copy-start(bf16[2048,64]{0,1:T(8,128)(2,1)} %param.12) | copy-start | bytes 786436
  292.8 213.8 %all-to-all-start.1 = ((bf16[32,2,48,2048]{3,2,1,0:T(8,128)(2,1)}), bf16[32,2,48,2048]{3,2,1,0:T(8,128)(2,1)}, u32[]{:S(2)}, u32[]{:S(2)}) async-start(bf16[32,2,48,2048]{3,2,1,0:T(8,128)(2,1)} %copy.90), calls=%async_computation.1 | async-start | bytes 25165824 | tf_op jit(solution)/shard_map/all_to_all | solution.py:124
  506.6 11.0 %copy-start.5 = (f32[384,3072]{1,0:T(8,128)S(1)}, f32[384,3072]{1,0:T(8,128)}, u32[]{:S(2)}) copy-start(f32[384,3072]{1,0:T(8,128)} %select_reduce_fusion) | copy-start | bytes 14155780
  517.6 29.2 %copy-start.4 = (f32[96,2048]{1,0:T(8,128)S(1)}, f32[96,2048]{1,0:T(8,128)}, u32[]{:S(2)}) copy-start(f32[96,2048]{1,0:T(8,128)} %copy-done.3) | copy-start | bytes 2359300
  517.6 30.2 %copy-start.1 = (bf16[2,352,2048]{2,1,0:T(8,128)(2,1)S(1)}, bf16[2,352,2048]{2,1,0:T(8,128)(2,1)}, u32[]{:S(2)}) copy-start(bf16[2,352,2048]{2,1,0:T(8,128)(2,1)} %param.15) | copy-start | bytes 8650756
  525.9 20.3 %collective-permute-start.11 = (bf16[96,2048]{1,0:T(8,128)(2,1)S(1)}, bf16[96,2048]{1,0:T(8,128)(2,1)S(1)}, u32[]{:S(2)}, u32[]{:S(2)}) collective-permute-start(bf16[96,2048]{1,0:T(8,128)(2,1)S(1)} %get-tuple-element.13), channel_id=1, source_target_pairs={{0,32},{32,64},{64,96},{96,0},{1,33},{33,65},{65,97},{97,1},{2,34}... | collective-permute-start | bytes 1179656 | tf_op jit(solution)/shard_map/ppermute | solution.py:67
  526.0 20.2 %collective-permute-start.10 = (bf16[96,2048]{1,0:T(8,128)(2,1)S(1)}, bf16[96,2048]{1,0:T(8,128)(2,1)S(1)}, u32[]{:S(2)}, u32[]{:S(2)}) collective-permute-start(bf16[96,2048]{1,0:T(8,128)(2,1)S(1)} %get-tuple-element.14), channel_id=1, source_target_pairs={{0,64},{32,96},{64,0},{96,32},{1,65},{33,97},{65,1},{97,33},{2,66}... | collective-permute-start | bytes 1179656 | tf_op jit(solution)/shard_map/ppermute | solution.py:67
  528.3 18.5 %collective-permute-start.9 = (bf16[96,2048]{1,0:T(8,128)(2,1)S(1)}, bf16[96,2048]{1,0:T(8,128)(2,1)S(1)}, u32[]{:S(2)}, u32[]{:S(2)}) collective-permute-start(bf16[96,2048]{1,0:T(8,128)(2,1)S(1)} %get-tuple-element.12), channel_id=1, source_target_pairs={{0,96},{32,0},{64,32},{96,64},{1,97},{33,1},{65,33},{97,65},{2,98}... | collective-permute-start | bytes 1179656 | tf_op jit(solution)/shard_map/ppermute | solution.py:67

commit v3 on v2

--- a/solution.py
+++ b/solution.py
@@ -36,10 +36,10 @@
     return ranks.astype(jnp.int32).reshape(chosen.shape)
 
 
-def expert_part(received, w_gate_up, w_down):
-    both = jnp.einsum("aend,edgf->aengf", received, w_gate_up, preferred_element_type=jnp.float32)
-    hidden = (jax.nn.silu(both[:, :, :, 0]) * both[:, :, :, 1]).astype(jnp.bfloat16)
-    return jnp.einsum("aenf,efd->aend", hidden, w_down, preferred_element_type=jnp.float32)
+def expert_one(rows, gate_up, down):
+    both = jnp.einsum("nd,dgf->ngf", rows, gate_up, preferred_element_type=jnp.float32)
+    hidden = (jax.nn.silu(both[:, 0]) * both[:, 1]).astype(jnp.bfloat16)
+    return jnp.dot(hidden, down, preferred_element_type=jnp.float32).astype(jnp.bfloat16)
 
 
 def scatter_rows(normed_rows, slot_index, buffer_rows):
@@ -106,31 +106,43 @@
     slot_cap = row_count // 8
     gathered = jnp.concatenate(
         [normed] + [seq_shift(normed, shift, seq_size) for shift in range(1, seq_size)], axis=0
-    )
+    ).reshape(seq_size, row_count, model_width)
+    far = seq_size // 2
     blocks_abs = (me - jnp.arange(seq_size, dtype=jnp.int32)) % seq_size
-    chosen = jnp.take(expert_ids[0].reshape(seq_size, row_count, -1), blocks_abs, axis=0).reshape(
-        seq_length, -1
-    )
-    gate_vals = gate_weights(gathered, router_w, chosen)
+    chosen_all = jnp.take(expert_ids[0].reshape(seq_size, row_count, -1), blocks_abs, axis=0)
+    direct_rows = jnp.concatenate([gathered[0], gathered[far]], axis=0)
+    chosen = jnp.concatenate([chosen_all[0], chosen_all[far]], axis=0)
+    gate_vals = gate_weights(direct_rows, router_w, chosen)
     ranks = slot_ranks(chosen, row_count, EXPERTS)
-    owner_rows = seq_size * slot_cap
-    source_block = jnp.repeat(blocks_abs, row_count)[:, None]
-    slot_index = chosen * owner_rows + source_block * slot_cap + ranks
-    outgoing = scatter_rows(gathered, slot_index, EXPERTS * owner_rows)
-    outgoing = outgoing.reshape(exp_size, exp_local, owner_rows, model_width)
-    partial_out = expert_part(
-        lax.all_to_all(outgoing, "exp", split_axis=0, concat_axis=0, tiled=True), w_gate_up, w_down
-    ).astype(jnp.bfloat16)
-    returned = lax.all_to_all(partial_out, "exp", split_axis=0, concat_axis=0, tiled=True)
-    out_table = returned.reshape(-1, model_width)
-    combined = combine_rows(out_table, slot_index, gate_vals).reshape(
-        seq_size, row_count, model_width
-    )
-    expert_sum = combined[0]
-    for shift in range(1, seq_size):
-        expert_sum = expert_sum + seq_shift(
-            combined[shift].astype(jnp.bfloat16), -shift, seq_size
-        ).astype(jnp.float32)
+    kind = (jnp.arange(2 * row_count, dtype=jnp.int32) // row_count)[:, None]
+    slot_index = chosen * (2 * slot_cap) + kind * slot_cap + ranks
+    outgoing = scatter_rows(direct_rows, slot_index, EXPERTS * 2 * slot_cap)
+    outgoing = outgoing.reshape(exp_size, exp_local, 2, slot_cap, model_width)
+    homes = []
+    for local in range(exp_local):
+        received = lax.all_to_all(
+            outgoing[:, local], "exp", split_axis=0, concat_axis=0, tiled=True
+        )
+        own_rows = received[:, 0]
+        left_rows = seq_shift(own_rows, 1, seq_size)
+        right_rows = seq_shift(own_rows, -1, seq_size)
+        rows_in = jnp.stack([own_rows, received[:, 1], left_rows, right_rows], axis=0)
+        parts = expert_one(
+            rows_in.reshape(-1, model_width), w_gate_up[local], w_down[local]
+        ).reshape(rows_in.shape)
+        from_right = seq_shift(parts[2], -1, seq_size)
+        from_left = seq_shift(parts[3], 1, seq_size)
+        own_sum = (
+            parts[0].astype(jnp.float32)
+            + from_right.astype(jnp.float32)
+            + from_left.astype(jnp.float32)
+        ).astype(jnp.bfloat16)
+        back = jnp.stack([own_sum, parts[1]], axis=1)
+        homes.append(lax.all_to_all(back, "exp", split_axis=0, concat_axis=0, tiled=True))
+    out_table = jnp.stack(homes, axis=1).reshape(-1, model_width)
+    combined = combine_rows(out_table, slot_index, gate_vals)
+    far_part = seq_shift(combined[row_count:].astype(jnp.bfloat16), far, seq_size)
+    expert_sum = combined[:row_count] + far_part.astype(jnp.float32)
     return (mixed + expert_sum).astype(jnp.bfloat16).reshape(1, row_count, model_width)
 
 

time: 553 us -> 502 us (0.908)
  the two profiles are of different devices: /device:TPU:48 before, /device:TPU:0 now
where the time goes in v3:
time: 502 us; the launch traced here: 492 us
  waiting for transfers between devices  192 us (38%)
  local copies, waits for them, and re-layouts  163 us (32%)
  starting transfers between devices  51.5 us (10%)
  other arithmetic  43 us (9%)
  matrix products  42.7 us (9%)
    ppermute x16, waiting for transfers between devices, seq_shift(): lax.ppermute(x, 'seq', [(i, (i + shift) % size) for i in range(size)])  94.6 us
    all_to_all x2, waiting for transfers between devices, on_device(): lax.all_to_all(outgoing[:, local], 'exp', split_axis=0, concat_axis=0, ti...  58.4 us
    all_to_all x2, waiting for transfers between devices, on_device(): lax.all_to_all(back, 'exp', split_axis=0, concat_axis=0, tiled=True)  38.5 us
    ppermute x16, starting transfers between devices, seq_shift(): lax.ppermute(x, 'seq', [(i, (i + shift) % size) for i in range(size)])  25 us
    reshape x2, local copies, waits for them, and re-layouts, on_device(): rows_in.reshape(-1, model_width)  21.4 us
    slice x2, local copies, waits for them, and re-layouts, on_device(): received[:, 1]  18.8 us
    squeeze x3, local copies, waits for them, and re-layouts, on_device(): outgoing[:, local]  17.4 us
    dot_general x2, matrix products, expert_one(): jnp.einsum('nd,dgf->ngf', rows, gate_up, preferred_element_type=jnp.float32)  15.6 us
  transfers between devices with their start and end apart: 20, of which 12 were waited for; matrix products, arithmetic and copies ran while one was open for 33% of the time, Pallas kernels for 0%

profile of v3, /device:TPU:0, one launch (start us, length us, event | category | flops | bytes accessed | tf_op | source)
XLA Modules:
  0.0 492.2 jit_solution(11956903328029741981)
XLA Ops:
  15.4 7.5 %collective-permute-done.1 = bf16[96,3,512]{2,0,1:T(8,128)(2,1)S(1)} collective-permute-done((bf16[96,3,512]{2,0,1:T(8,128)(2,1)}, bf16[96,3,512]{2,0,1:T(8,128)(2,1)S(1)}, u32[]{:S(2)}, u32[]{:S(2)}) %collective-permute-start.1) | collective-permute-done | bytes 294944 | tf_op jit(solution)/shard_map/ppermute | solution.py:67
  24.8 3.3 fusion.67
  39.0 31.2 %collective-permute-done.3 = f32[96,2048]{1,0:T(8,128)S(1)} collective-permute-done((f32[96,2048]{1,0:T(8,128)}, f32[96,2048]{1,0:T(8,128)S(1)}, u32[]{:S(2)}, u32[]{:S(2)}) %collective-permute-start.3) | collective-permute-done | bytes 786464 | tf_op jit(solution)/shard_map/ppermute | solution.py:67
  70.2 3.7 collective-permute-done.5
  78.7 9.9 %collective-permute-done.6 = bf16[96,2048]{1,0:T(8,128)(2,1)S(1)} collective-permute-done((bf16[96,2048]{1,0:T(8,128)(2,1)S(1)}, bf16[96,2048]{1,0:T(8,128)(2,1)S(1)}, u32[]{:S(2)}, u32[]{:S(2)}) %collective-permute-start.6) | collective-permute-done | bytes 393248 | tf_op jit(solution)/shard_map/ppermute | solution.py:67
  88.6 4.5 convolution_convert_fusion.2
  93.1 10.6 %reshape.246 = bf16[32,2,2,12,2048]{4,3,2,1,0:T(8,128)(2,1)} reshape(bf16[1536,2048]{1,0:T(8,128)(2,1)} %convolution_convert_fusion.2) | data formatting | bytes 12582912 | tf_op jit(solution)/shard_map/reshape | solution.py:120
  103.7 5.4 %slice_bitcast_fusion.1 = (bf16[32,2,12,2048]{3,2,1,0:T(8,128)(2,1)S(1)}, bf16[32,2,12,2048]{3,2,1,0:T(8,128)(2,1)}) fusion(bf16[32,2,2,12,2048]{4,3,2,1,0:T(8,128)(2,1)} %reshape.246), kind=kLoop, calls=%fused_computation.13 | loop fusion | bytes 12582912 | tf_op jit(solution)/shard_map/squeeze | solution.py:124
  109.0 5.0 %copy.147 = bf16[32,2,12,2048]{3,1,2,0:T(2,128)(2,1)} copy(bf16[32,2,12,2048]{3,2,1,0:T(8,128)(2,1)S(1)} %get-tuple-element.7) | data formatting | bytes 6291456 | tf_op jit(solution)/shard_map/squeeze | solution.py:124
  114.0 8.6 %all-to-all-start = ((bf16[32,2,12,2048]{3,1,2,0:T(2,128)(2,1)}), bf16[32,2,12,2048]{3,1,2,0:T(2,128)(2,1)}, u32[]{:S(2)}, u32[]{:S(2)}) async-start(bf16[32,2,12,2048]{3,1,2,0:T(2,128)(2,1)} %copy.147), calls=%async_computation | async-start | bytes 6291456 | tf_op jit(solution)/shard_map/all_to_all | solution.py:123
  122.7 7.1 %copy.156 = bf16[32,2,12,2048]{3,1,2,0:T(2,128)(2,1)} copy(bf16[32,2,12,2048]{3,2,1,0:T(8,128)(2,1)} %get-tuple-element.8) | data formatting | bytes 6291456 | tf_op jit(solution)/shard_map/squeeze | solution.py:124
  129.8 33.1 %all-to-all-done = bf16[32,2,12,2048]{3,1,2,0:T(2,128)(2,1)} async-done(((bf16[32,2,12,2048]{3,1,2,0:T(2,128)(2,1)}), bf16[32,2,12,2048]{3,1,2,0:T(2,128)(2,1)}, u32[]{:S(2)}, u32[]{:S(2)}) %all-to-all-start) | async-done | bytes 3145760 | tf_op jit(solution)/shard_map/all_to_all | solution.py:123
  162.8 5.2 %all-to-all-start.2 = ((bf16[32,2,12,2048]{3,1,2,0:T(2,128)(2,1)}), bf16[32,2,12,2048]{3,1,2,0:T(2,128)(2,1)}, u32[]{:S(2)}, u32[]{:S(2)}) async-start(bf16[32,2,12,2048]{3,1,2,0:T(2,128)(2,1)} %copy.156), calls=%async_computation.2 | async-start | bytes 6291456 | tf_op jit(solution)/shard_map/all_to_all | solution.py:123
  168.1 9.8 %fusion.63 = (bf16[32,1,12,2048]{3,1,2,0:T(2,128)(2,1)}, bf16[32,1,12,2048]{3,1,2,0:T(2,128)(2,1)S(1)}) fusion(bf16[32,2,12,2048]{3,1,2,0:T(2,128)(2,1)} %all-to-all-done), kind=kLoop, calls=%fused_computation.125 | loop fusion | bytes 6291456 | tf_op jit(solution)/shard_map/slice | solution.py:129
  179.7 3.2 collective-permute-start.8
  182.9 25.4 %all-to-all-done.2 = bf16[32,2,12,2048]{3,1,2,0:T(2,128)(2,1)} async-done(((bf16[32,2,12,2048]{3,1,2,0:T(2,128)(2,1)}), bf16[32,2,12,2048]{3,1,2,0:T(2,128)(2,1)}, u32[]{:S(2)}, u32[]{:S(2)}) %all-to-all-start.2) | async-done | bytes 3145760 | tf_op jit(solution)/shard_map/all_to_all | solution.py:123
  208.2 9.0 %fusion.64 = (bf16[32,1,12,2048]{3,1,2,0:T(2,128)(2,1)S(1)}, bf16[32,1,12,2048]{3,1,2,0:T(2,128)(2,1)S(1)}) fusion(bf16[32,2,12,2048]{3,1,2,0:T(2,128)(2,1)} %all-to-all-done.2), kind=kLoop, calls=%fused_computation.126 | loop fusion | bytes 6291456 | tf_op jit(solution)/shard_map/slice | solution.py:129
  217.2 2.9 copy.189
  220.1 3.2 collective-permute-start.12
  227.9 3.1 pad_maximum_fusion
  231.0 7.0 %copy.150 = bf16[4,32,12,2048]{3,2,1,0:T(8,128)(2,1)} copy(bf16[4,32,12,2048]{3,1,2,0:T(8,128)(2,1)S(1)} %pad_maximum_fusion) | data formatting | bytes 12582912 | tf_op jit(solution)/shard_map/stack | solution.py:129
  238.0 10.7 %reshape.263 = bf16[1536,2048,1]{1,0,2:T(8,128)(2,1)} reshape(bf16[4,32,12,2048]{3,2,1,0:T(8,128)(2,1)} %copy.150) | data formatting | bytes 12582912 | tf_op jit(solution)/shard_map/reshape | solution.py:131
  248.7 7.8 %fusion.5 = f32[1536,2,352]{0,2,1:T(8,128)S(1)} fusion(bf16[1536,2048,1]{1,0,2:T(8,128)(2,1)} %reshape.263, bf16[2,2048,2,352]{1,3,2,0:T(8,128)(2,1)} %param.14), kind=kOutput, calls=%fused_computation.21 | convolution fusion | flops 4429185024 | bytes 13500416 | tf_op jit(solution)/shard_map/nd,dgf->ngf/dot_general | solution.py:40
  256.6 3.8 convolution_convert_fusion.1
  260.4 3.4 fusion.61
  272.7 3.2 collective-permute-start.9
  275.9 4.8 reshape.252
  283.0 3.7 pad_maximum_fusion.1
  286.7 7.0 %copy.159 = bf16[4,32,12,2048]{3,2,1,0:T(8,128)(2,1)} copy(bf16[4,32,12,2048]{3,1,2,0:T(8,128)(2,1)S(1)} %pad_maximum_fusion.1) | data formatting | bytes 12582912 | tf_op jit(solution)/shard_map/stack | solution.py:129
  293.7 10.7 %reshape.264 = bf16[1536,2048,1]{1,0,2:T(8,128)(2,1)} reshape(bf16[4,32,12,2048]{3,2,1,0:T(8,128)(2,1)} %copy.159) | data formatting | bytes 12582912 | tf_op jit(solution)/shard_map/reshape | solution.py:131
  304.4 7.8 %fusion.3 = f32[1536,2,352]{0,2,1:T(8,128)S(1)} fusion(bf16[1536,2048,1]{1,0,2:T(8,128)(2,1)} %reshape.264, bf16[2,2048,2,352]{1,3,2,0:T(8,128)(2,1)} %param.14), kind=kOutput, calls=%fused_computation.19 | convolution fusion | flops 4429185024 | bytes 13500416 | tf_op jit(solution)/shard_map/nd,dgf->ngf/dot_general | solution.py:40
  312.3 5.9 %convolution_convert_fusion = bf16[1536,2048]{1,0:T(8,128)(2,1)} fusion(bf16[2,352,2048]{2,1,0:T(8,128)(2,1)S(1)} %copy-done.12, f32[1536,2,352]{0,2,1:T(8,128)S(1)} %fusion.3), kind=kOutput, calls=%fused_computation.2 | convolution fusion | flops 2220982272 | bytes 12058624 | tf_op jit(solution)/shard_map/dot_general | solution.py:42
  318.2 3.9 fusion.11
  322.6 5.0 %copy.155 = bf16[32,2,12,2048]{3,1,2,0:T(2,128)(2,1)} copy(bf16[32,2,12,2048]{3,2,0,1:T(8,128)(2,1)S(1)} %pad_maximum_fusion.3) | data formatting | bytes 6291456 | tf_op jit(solution)/shard_map/stack | solution.py:140
  327.6 4.8 all-to-all-start.1
  332.4 6.6 %fusion.62 = (bf16[384,2048]{1,0:T(8,128)(2,1)}, bf16[384,2048]{1,0:T(8,128)(2,1)}, bf16[384,2048]{1,0:T(8,128)(2,1)}, f32[384,2048]{1,0:T(8,128)}) fusion(bf16[1536,2048]{1,0:T(8,128)(2,1)} %convolution_convert_fusion), kind=kLoop, calls=%fused_computation.124 | loop fusion | flops 786432 | bytes 14155776 | tf_op jit(solution)/shard_map/slice | solution.py:133
  349.9 4.8 reshape.253
  357.1 23.1 %collective-permute-done.13 = bf16[32,12,2048]{2,0,1:T(8,128)(2,1)} collective-permute-done((bf16[32,12,2048]{2,0,1:T(8,128)(2,1)}, bf16[32,12,2048]{2,0,1:T(8,128)(2,1)}, u32[]{:S(2)}, u32[]{:S(2)}) %collective-permute-start.13) | collective-permute-done | bytes 1572896 | tf_op jit(solution)/shard_map/ppermute | solution.py:67
  380.2 5.6 %collective-permute-done.14 = bf16[32,12,2048]{2,0,1:T(8,128)(2,1)} collective-permute-done((bf16[32,12,2048]{2,0,1:T(8,128)(2,1)}, bf16[32,12,2048]{2,0,1:T(8,128)(2,1)}, u32[]{:S(2)}, u32[]{:S(2)}) %collective-permute-start.14) | collective-permute-done | bytes 1572896 | tf_op jit(solution)/shard_map/ppermute | solution.py:67
  385.8 5.0 %fusion.12 = bf16[32,1,12,2048]{3,2,0,1:T(8,128)(2,1)S(1)} fusion(f32[32,12,2048]{2,1,0:T(8,128)} %reshape.253, bf16[32,12,2048]{2,0,1:T(8,128)(2,1)} %collective-permute-done.14, bf16[32,12,2048]{2,0,1:T(8,128)(2,1)} %collective-permute-done.13), kind=kLoop, calls=%fused_computation.33 | loop fusion | flops 3932160 | bytes 7864320 | tf_op jit(solution)/shard_map/stack | solution.py:140
  391.4 5.0 %copy.164 = bf16[32,2,12,2048]{3,1,2,0:T(2,128)(2,1)} copy(bf16[32,2,12,2048]{3,2,0,1:T(8,128)(2,1)S(1)} %pad_maximum_fusion.4) | data formatting | bytes 6291456 | tf_op jit(solution)/shard_map/stack | solution.py:140
  396.4 7.8 %all-to-all-start.3 = ((bf16[32,2,12,2048]{3,1,2,0:T(2,128)(2,1)}), bf16[32,2,12,2048]{3,1,2,0:T(2,128)(2,1)}, u32[]{:S(2)}, u32[]{:S(2)}) async-start(bf16[32,2,12,2048]{3,1,2,0:T(2,128)(2,1)} %copy.164), calls=%async_computation.3 | async-start | bytes 6291456 | tf_op jit(solution)/shard_map/all_to_all | solution.py:141
  405.8 38.5 %all-to-all-done.3 = bf16[32,2,12,2048]{3,1,2,0:T(2,128)(2,1)} async-done(((bf16[32,2,12,2048]{3,1,2,0:T(2,128)(2,1)}), bf16[32,2,12,2048]{3,1,2,0:T(2,128)(2,1)}, u32[]{:S(2)}, u32[]{:S(2)}) %all-to-all-start.3) | async-done | bytes 3145760 | tf_op jit(solution)/shard_map/all_to_all | solution.py:141
  444.3 10.8 %pad_maximum_fusion.2 = bf16[32,2,2,12,2048]{4,2,3,0,1:T(2,128)(2,1)S(1)} fusion(bf16[32,1,2,12,2048]{4,2,3,0,1:T(2,128)(2,1)} %bitcast.40, bf16[32,1,2,12,2048]{4,2,3,0,1:T(2,128)(2,1)} %bitcast.29), kind=kLoop, calls=%fused_computation.11 | loop fusion | flops 3145728 | bytes 12582912 | tf_op jit(solution)/shard_map/stack | solution.py:142
  455.1 6.8 %copy.165 = bf16[32,2,2,12,2048]{4,3,2,1,0:T(8,128)(2,1)} copy(bf16[32,2,2,12,2048]{4,2,3,0,1:T(2,128)(2,1)S(1)} %pad_maximum_fusion.2) | data formatting | bytes 12582912 | tf_op jit(solution)/shard_map/stack | solution.py:142
  461.9 10.7 %reshape.249 = bf16[1536,2048]{1,0:T(8,128)(2,1)} reshape(bf16[32,2,2,12,2048]{4,3,2,1,0:T(8,128)(2,1)} %copy.165) | data formatting | bytes 12582912 | tf_op jit(solution)/shard_map/reshape | solution.py:142
  472.6 4.3 fusion.46
  479.7 11.4 %collective-permute-done.15 = bf16[96,2048]{1,0:T(8,128)(2,1)S(1)} collective-permute-done((bf16[96,2048]{1,0:T(8,128)(2,1)S(1)}, bf16[96,2048]{1,0:T(8,128)(2,1)S(1)}, u32[]{:S(2)}, u32[]{:S(2)}) %collective-permute-start.15) | collective-permute-done | bytes 393248 | tf_op jit(solution)/shard_map/ppermute | solution.py:67
  (111 shorter events, 69.9 us)
Async XLA Ops:
  0.0 30.2 %copy-start = (bf16[512,2048]{1,0:T(8,128)(2,1)S(1)}, bf16[512,2048]{1,0:T(8,128)(2,1)}, u32[]{:S(2)}) copy-start(bf16[512,2048]{1,0:T(8,128)(2,1)} %param.10) | copy-start | bytes 6291460
  4.6 8.1 %copy-start.9 = (s32[1,384,6]{1,0,2:T(1,128)S(1)}, s32[1,384,6]{1,0,2:T(1,128)}, u32[]{:S(2)}) copy-start(s32[1,384,6]{1,0,2:T(1,128)} %param.13) | copy-start | bytes 27652
  5.4 10.1 %collective-permute-start = (bf16[96,3,512]{2,0,1:T(8,128)(2,1)}, bf16[96,3,512]{2,0,1:T(8,128)(2,1)S(1)}, u32[]{:S(2)}, u32[]{:S(2)}) collective-permute-start(bf16[96,3,512]{2,0,1:T(8,128)(2,1)} %bitcast.110), channel_id=1, source_target_pairs={{0,32},{32,64},{64,96},{96,0},{1,33},{33,65},{65,97},{97,1},{2,34}... | collective-permute-start | bytes 884744 | tf_op jit(solution)/shard_map/ppermute | solution.py:67
  7.7 15.2 %collective-permute-start.1 = (bf16[96,3,512]{2,0,1:T(8,128)(2,1)}, bf16[96,3,512]{2,0,1:T(8,128)(2,1)S(1)}, u32[]{:S(2)}, u32[]{:S(2)}) collective-permute-start(bf16[96,3,512]{2,0,1:T(8,128)(2,1)} %bitcast.109), channel_id=1, source_target_pairs={{0,64},{32,96},{64,0},{96,32},{1,65},{33,97},{65,1},{97,33},{2,66}... | collective-permute-start | bytes 884744 | tf_op jit(solution)/shard_map/ppermute | solution.py:67
  11.2 11.9 %collective-permute-start.2 = (bf16[96,3,512]{2,0,1:T(8,128)(2,1)}, bf16[96,3,512]{2,0,1:T(8,128)(2,1)S(1)}, u32[]{:S(2)}, u32[]{:S(2)}) collective-permute-start(bf16[96,3,512]{2,0,1:T(8,128)(2,1)} %bitcast.108), channel_id=1, source_target_pairs={{0,96},{32,0},{64,32},{96,64},{1,97},{33,1},{65,33},{97,65},{2,98}... | collective-permute-start | bytes 884744 | tf_op jit(solution)/shard_map/ppermute | solution.py:67
  31.2 2.2 copy-start.4
  31.2 42.6 %copy-start.8 = (bf16[1,96,2048]{2,1,0:T(8,128)(2,1)S(1)}, bf16[1,96,2048]{2,1,0:T(8,128)(2,1)}, u32[]{:S(2)}) copy-start(bf16[1,96,2048]{2,1,0:T(8,128)(2,1)} %param.8) | copy-start | bytes 1179652
  33.4 36.8 %collective-permute-start.3 = (f32[96,2048]{1,0:T(8,128)}, f32[96,2048]{1,0:T(8,128)S(1)}, u32[]{:S(2)}, u32[]{:S(2)}) collective-permute-start(f32[96,2048]{1,0:T(8,128)} %get-tuple-element.25), channel_id=1, source_target_pairs={{0,96},{32,0},{64,32},{96,64},{1,97},{33,1},{65,33},{97,65},{2,98}... | collective-permute-start | bytes 2359304 | tf_op jit(solution)/shard_map/ppermute | solution.py:67
  36.0 34.2 %collective-permute-start.4 = (f32[96,2048]{1,0:T(8,128)}, f32[96,2048]{1,0:T(8,128)S(1)}, u32[]{:S(2)}, u32[]{:S(2)}) collective-permute-start(f32[96,2048]{1,0:T(8,128)} %get-tuple-element.27), channel_id=1, source_target_pairs={{0,64},{32,96},{64,0},{96,32},{1,65},{33,97},{65,1},{97,33},{2,66}... | collective-permute-start | bytes 2359304 | tf_op jit(solution)/shard_map/ppermute | solution.py:67
  37.9 36.0 %collective-permute-start.5 = (f32[96,2048]{1,0:T(8,128)S(1)}, f32[96,2048]{1,0:T(8,128)}, u32[]{:S(2)}, u32[]{:S(2)}) collective-permute-start(f32[96,2048]{1,0:T(8,128)S(1)} %get-tuple-element.26), channel_id=1, source_target_pairs={{0,32},{32,64},{64,96},{96,0},{1,33},{33,65},{65,97},{97,1},{2,34}... | collective-permute-start | bytes 2359304 | tf_op jit(solution)/shard_map/ppermute | solution.py:67
  38.8 36.8 %copy-start.10 = (f32[2048]{0:T(1024)S(1)}, f32[2048]{0:T(1024)}, u32[]{:S(2)}) copy-start(f32[2048]{0:T(1024)} %param.11) | copy-start | bytes 24580
  75.6 17.5 %copy-start.6 = (f32[96,2048]{1,0:T(8,128)}, f32[96,2048]{1,0:T(8,128)S(1)}, u32[]{:S(2)}) copy-start(f32[96,2048]{1,0:T(8,128)S(1)} %get-tuple-element.6) | copy-start | bytes 2359300
  75.7 12.8 %collective-permute-start.6 = (bf16[96,2048]{1,0:T(8,128)(2,1)S(1)}, bf16[96,2048]{1,0:T(8,128)(2,1)S(1)}, u32[]{:S(2)}, u32[]{:S(2)}) collective-permute-start(bf16[96,2048]{1,0:T(8,128)(2,1)S(1)} %multiply_convert_fusion), channel_id=1, source_target_pairs={{0,64},{32,96},{64,0},{96,32},{1,65},{33,97},{65,1},{97,33},{2,66}... | collective-permute-start | bytes 1179656 | tf_op jit(solution)/shard_map/ppermute | solution.py:67
  114.0 48.8 %all-to-all-start = ((bf16[32,2,12,2048]{3,1,2,0:T(2,128)(2,1)}), bf16[32,2,12,2048]{3,1,2,0:T(2,128)(2,1)}, u32[]{:S(2)}, u32[]{:S(2)}) async-start(bf16[32,2,12,2048]{3,1,2,0:T(2,128)(2,1)} %copy.147), calls=%async_computation | async-start | bytes 6291456 | tf_op jit(solution)/shard_map/all_to_all | solution.py:123
  162.8 45.4 %all-to-all-start.2 = ((bf16[32,2,12,2048]{3,1,2,0:T(2,128)(2,1)}), bf16[32,2,12,2048]{3,1,2,0:T(2,128)(2,1)}, u32[]{:S(2)}, u32[]{:S(2)}) async-start(bf16[32,2,12,2048]{3,1,2,0:T(2,128)(2,1)} %copy.156), calls=%async_computation.2 | async-start | bytes 6291456 | tf_op jit(solution)/shard_map/all_to_all | solution.py:123
  179.6 48.3 %collective-permute-start.7 = (bf16[32,12,2048]{2,0,1:T(8,128)(2,1)S(1)}, bf16[32,12,2048]{2,0,1:T(8,128)(2,1)}, u32[]{:S(2)}, u32[]{:S(2)}) collective-permute-start(bf16[32,12,2048]{2,0,1:T(8,128)(2,1)S(1)} %bitcast.113), channel_id=1, source_target_pairs={{0,32},{32,64},{64,96},{96,0},{1,33},{33,65},{65,97},{97,1},{2,34}... | collective-permute-start | bytes 4718600 | tf_op jit(solution)/shard_map/ppermute | solution.py:67
  179.7 48.2 %collective-permute-start.8 = (bf16[32,12,2048]{2,0,1:T(8,128)(2,1)S(1)}, bf16[32,12,2048]{2,0,1:T(8,128)(2,1)}, u32[]{:S(2)}, u32[]{:S(2)}) collective-permute-start(bf16[32,12,2048]{2,0,1:T(8,128)(2,1)S(1)} %bitcast.114), channel_id=1, source_target_pairs={{0,96},{32,0},{64,32},{96,64},{1,97},{33,1},{65,33},{97,65},{2,98}... | collective-permute-start | bytes 4718600 | tf_op jit(solution)/shard_map/ppermute | solution.py:67
  217.2 6.1 %copy-start.5 = (bf16[32,1,12,2048]{3,1,2,0:T(2,128)(2,1)S(1)}, bf16[32,1,12,2048]{3,1,2,0:T(2,128)(2,1)}, u32[]{:S(2)}) copy-start(bf16[32,1,12,2048]{3,1,2,0:T(2,128)(2,1)} %get-tuple-element.19) | copy-start | bytes 4718596
  220.1 62.9 %collective-permute-start.11 = (bf16[32,12,2048]{2,0,1:T(8,128)(2,1)}, bf16[32,12,2048]{2,0,1:T(8,128)(2,1)}, u32[]{:S(2)}, u32[]{:S(2)}) collective-permute-start(bf16[32,12,2048]{2,0,1:T(8,128)(2,1)} %bitcast.76.clone.2), channel_id=1, source_target_pairs={{0,32},{32,64},{64,96},{96,0},{1,33},{33,65},{65,97},{97,1},{2,34}... | collective-permute-start | bytes 4718600 | tf_op jit(solution)/shard_map/ppermute | solution.py:67
  220.1 62.9 %collective-permute-start.12 = (bf16[32,12,2048]{2,0,1:T(8,128)(2,1)}, bf16[32,12,2048]{2,0,1:T(8,128)(2,1)}, u32[]{:S(2)}, u32[]{:S(2)}) collective-permute-start(bf16[32,12,2048]{2,0,1:T(8,128)(2,1)} %bitcast.76.clone.2), channel_id=1, source_target_pairs={{0,96},{32,0},{64,32},{96,64},{1,97},{33,1},{65,33},{97,65},{2,98}... | collective-permute-start | bytes 4718600 | tf_op jit(solution)/shard_map/ppermute | solution.py:67
  248.7 7.8 %copy-start.11 = (bf16[2,352,2048]{2,1,0:T(8,128)(2,1)S(1)}, bf16[2,352,2048]{2,1,0:T(8,128)(2,1)}, u32[]{:S(2)}) copy-start(bf16[2,352,2048]{2,1,0:T(8,128)(2,1)} %param.15) | copy-start | bytes 8650756
  268.2 50.0 %collective-permute-start.10 = (bf16[32,12,2048]{2,0,1:T(8,128)(2,1)}, bf16[32,12,2048]{2,0,1:T(8,128)(2,1)}, u32[]{:S(2)}, u32[]{:S(2)}) collective-permute-start(bf16[32,12,2048]{2,0,1:T(8,128)(2,1)} %copy.153), channel_id=1, source_target_pairs={{0,32},{32,64},{64,96},{96,0},{1,33},{33,65},{65,97},{97,1},{2,34}... | collective-permute-start | bytes 4718600 | tf_op jit(solution)/shard_map/ppermute | solution.py:67
  272.7 45.5 %collective-permute-start.9 = (bf16[32,12,2048]{2,0,1:T(8,128)(2,1)}, bf16[32,12,2048]{2,0,1:T(8,128)(2,1)}, u32[]{:S(2)}, u32[]{:S(2)}) collective-permute-start(bf16[32,12,2048]{2,0,1:T(8,128)(2,1)} %copy.151), channel_id=1, source_target_pairs={{0,96},{32,0},{64,32},{96,64},{1,97},{33,1},{65,33},{97,65},{2,98}... | collective-permute-start | bytes 4718600 | tf_op jit(solution)/shard_map/ppermute | solution.py:67
  304.4 7.8 %copy-start.12 = (bf16[2,352,2048]{2,1,0:T(8,128)(2,1)S(1)}, bf16[2,352,2048]{2,1,0:T(8,128)(2,1)}, u32[]{:S(2)}) copy-start(bf16[2,352,2048]{2,1,0:T(8,128)(2,1)} %param.15) | copy-start | bytes 8650756
  312.3 5.9 %copy-start.3 = (f32[32,12,2048]{2,1,0:T(8,128)S(1)}, f32[32,12,2048]{2,1,0:T(8,128)}, u32[]{:S(2)}) copy-start(f32[32,12,2048]{2,1,0:T(8,128)} %reshape.252) | copy-start | bytes 9437188
  327.6 68.8 %all-to-all-start.1 = ((bf16[32,2,12,2048]{3,1,2,0:T(2,128)(2,1)}), bf16[32,2,12,2048]{3,1,2,0:T(2,128)(2,1)}, u32[]{:S(2)}, u32[]{:S(2)}) async-start(bf16[32,2,12,2048]{3,1,2,0:T(2,128)(2,1)} %copy.155), calls=%async_computation.1 | async-start | bytes 6291456 | tf_op jit(solution)/shard_map/all_to_all | solution.py:141
  343.5 36.7 %collective-permute-start.13 = (bf16[32,12,2048]{2,0,1:T(8,128)(2,1)}, bf16[32,12,2048]{2,0,1:T(8,128)(2,1)}, u32[]{:S(2)}, u32[]{:S(2)}) collective-permute-start(bf16[32,12,2048]{2,0,1:T(8,128)(2,1)} %copy.160), channel_id=1, source_target_pairs={{0,96},{32,0},{64,32},{96,64},{1,97},{33,1},{65,33},{97,65},{2,98}... | collective-permute-start | bytes 4718600 | tf_op jit(solution)/shard_map/ppermute | solution.py:67
  347.9 37.9 %collective-permute-start.14 = (bf16[32,12,2048]{2,0,1:T(8,128)(2,1)}, bf16[32,12,2048]{2,0,1:T(8,128)(2,1)}, u32[]{:S(2)}, u32[]{:S(2)}) collective-permute-start(bf16[32,12,2048]{2,0,1:T(8,128)(2,1)} %copy.162), channel_id=1, source_target_pairs={{0,32},{32,64},{64,96},{96,0},{1,33},{33,65},{65,97},{97,1},{2,34}... | collective-permute-start | bytes 4718600 | tf_op jit(solution)/shard_map/ppermute | solution.py:67
  396.3 7.8 %copy-start.13 = (bf16[2048,64]{0,1:T(8,128)(2,1)S(1)}, bf16[2048,64]{0,1:T(8,128)(2,1)}, u32[]{:S(2)}) copy-start(bf16[2048,64]{0,1:T(8,128)(2,1)} %param.12) | copy-start | bytes 786436
  396.4 48.0 %all-to-all-start.3 = ((bf16[32,2,12,2048]{3,1,2,0:T(2,128)(2,1)}), bf16[32,2,12,2048]{3,1,2,0:T(2,128)(2,1)}, u32[]{:S(2)}, u32[]{:S(2)}) async-start(bf16[32,2,12,2048]{3,1,2,0:T(2,128)(2,1)} %copy.164), calls=%async_computation.3 | async-start | bytes 6291456 | tf_op jit(solution)/shard_map/all_to_all | solution.py:141
  472.6 4.6 copy-start.2
  477.2 13.9 %copy-start.7 = (f32[96,2048]{1,0:T(8,128)S(1)}, f32[96,2048]{1,0:T(8,128)}, u32[]{:S(2)}) copy-start(f32[96,2048]{1,0:T(8,128)} %copy-done.6) | copy-start | bytes 2359300
  477.2 14.8 %copy-start.1 = (bf16[512,2048]{1,0:T(8,128)(2,1)S(1)}, bf16[512,2048]{1,0:T(8,128)(2,1)}, u32[]{:S(2)}) copy-start(bf16[512,2048]{1,0:T(8,128)(2,1)} %param.10) | copy-start | bytes 6291460
  478.8 12.4 %collective-permute-start.15 = (bf16[96,2048]{1,0:T(8,128)(2,1)S(1)}, bf16[96,2048]{1,0:T(8,128)(2,1)S(1)}, u32[]{:S(2)}, u32[]{:S(2)}) collective-permute-start(bf16[96,2048]{1,0:T(8,128)(2,1)S(1)} %slice.237), channel_id=1, source_target_pairs={{0,64},{32,96},{64,0},{96,32},{1,65},{33,97},{65,1},{97,33},{2,66}... | collective-permute-start | bytes 1179656 | tf_op jit(solution)/shard_map/ppermute | solution.py:67

commit v4 on v3

--- a/solution.py
+++ b/solution.py
@@ -36,10 +36,12 @@
     return ranks.astype(jnp.int32).reshape(chosen.shape)
 
 
-def expert_one(rows, gate_up, down):
-    both = jnp.einsum("nd,dgf->ngf", rows, gate_up, preferred_element_type=jnp.float32)
-    hidden = (jax.nn.silu(both[:, 0]) * both[:, 1]).astype(jnp.bfloat16)
-    return jnp.dot(hidden, down, preferred_element_type=jnp.float32).astype(jnp.bfloat16)
+def expert_group(rows, gate_up, down):
+    both = jnp.einsum("gsd,dxf->gsxf", rows, gate_up, preferred_element_type=jnp.float32)
+    hidden = (jax.nn.silu(both[..., 0, :]) * both[..., 1, :]).astype(jnp.bfloat16)
+    return jnp.einsum("gsf,fd->gsd", hidden, down, preferred_element_type=jnp.float32).astype(
+        jnp.bfloat16
+    )
 
 
 def scatter_rows(normed_rows, slot_index, buffer_rows):
@@ -115,32 +117,44 @@
     gate_vals = gate_weights(direct_rows, router_w, chosen)
     ranks = slot_ranks(chosen, row_count, EXPERTS)
     kind = (jnp.arange(2 * row_count, dtype=jnp.int32) // row_count)[:, None]
-    slot_index = chosen * (2 * slot_cap) + kind * slot_cap + ranks
-    outgoing = scatter_rows(direct_rows, slot_index, EXPERTS * 2 * slot_cap)
-    outgoing = outgoing.reshape(exp_size, exp_local, 2, slot_cap, model_width)
+    owner = chosen // exp_local
+    local_of = chosen % exp_local
+    slot_index = ((local_of * exp_size + owner) * 2 + kind) * slot_cap + ranks
+    grid = (exp_local, exp_size, 2 * slot_cap)
+    slot_ids = jnp.arange(math.prod(grid), dtype=jnp.int32).reshape(grid)
+    select = jnp.sum(
+        (slot_index[None, None, None, :, :] == slot_ids[..., None, None]).astype(
+            jnp.bfloat16
+        ),
+        axis=-1,
+    )
+    outgoing = jnp.einsum(
+        "cgsp,pd->cgsd", select, direct_rows, preferred_element_type=jnp.float32
+    ).astype(jnp.bfloat16)
     homes = []
     for local in range(exp_local):
-        received = lax.all_to_all(
-            outgoing[:, local], "exp", split_axis=0, concat_axis=0, tiled=True
-        )
-        own_rows = received[:, 0]
-        left_rows = seq_shift(own_rows, 1, seq_size)
-        right_rows = seq_shift(own_rows, -1, seq_size)
-        rows_in = jnp.stack([own_rows, received[:, 1], left_rows, right_rows], axis=0)
-        parts = expert_one(
-            rows_in.reshape(-1, model_width), w_gate_up[local], w_down[local]
-        ).reshape(rows_in.shape)
-        from_right = seq_shift(parts[2], -1, seq_size)
-        from_left = seq_shift(parts[3], 1, seq_size)
-        own_sum = (
-            parts[0].astype(jnp.float32)
-            + from_right.astype(jnp.float32)
-            + from_left.astype(jnp.float32)
-        ).astype(jnp.bfloat16)
-        back = jnp.stack([own_sum, parts[1]], axis=1)
-        homes.append(lax.all_to_all(back, "exp", split_axis=0, concat_axis=0, tiled=True))
-    out_table = jnp.stack(homes, axis=1).reshape(-1, model_width)
-    combined = combine_rows(out_table, slot_index, gate_vals)
+        direction = 1 if local % 2 == 0 else -1
+        received = lax.all_to_all(outgoing[local], "exp", split_axis=0, concat_axis=0, tiled=True)
+        forwarded = seq_shift(received, direction, seq_size)
+        mine = expert_group(received, w_gate_up[local], w_down[local])
+        theirs = expert_group(forwarded, w_gate_up[local], w_down[local])
+        returned = seq_shift(theirs, -direction, seq_size)
+        pair_sum = (mine.astype(jnp.float32) + returned.astype(jnp.float32)).astype(jnp.bfloat16)
+        homes.append(lax.all_to_all(pair_sum, "exp", split_axis=0, concat_axis=0, tiled=True))
+    table = jnp.stack(homes, axis=0)
+    weights = jnp.sum(
+        jnp.where(
+            slot_index[:, :, None, None, None] == slot_ids[None, None],
+            gate_vals[:, :, None, None, None],
+            0.0,
+        ),
+        axis=1,
+    )
+    high = weights.astype(jnp.bfloat16)
+    low = (weights - high.astype(jnp.float32)).astype(jnp.bfloat16)
+    combined = jnp.einsum(
+        "pcgs,cgsd->pd", high, table, preferred_element_type=jnp.float32
+    ) + jnp.einsum("pcgs,cgsd->pd", low, table, preferred_element_type=jnp.float32)
     far_part = seq_shift(combined[row_count:].astype(jnp.bfloat16), far, seq_size)
     expert_sum = combined[:row_count] + far_part.astype(jnp.float32)
     return (mixed + expert_sum).astype(jnp.bfloat16).reshape(1, row_count, model_width)

time: 502 us -> 441 us (0.88); the launches traced: 492 us -> 440 us
  local copies, waits for them, and re-layouts: 163 us -> 15 us
  waiting for transfers between devices: 192 us -> 290 us
  blocking collectives: 0 us -> 47.5 us
  other arithmetic: 43 us -> 5.43 us
  starting transfers between devices: 51.5 us -> 31.4 us
  matrix products: 42.7 us -> 50.6 us
    ppermute x16 -> x12, waiting for transfers between devices: 94.6 us -> 185 us  [seq_shift(): lax.ppermute(x, 'seq', [(i, (i + shift) % size) for i in range(size)])]
    all_to_all x0 -> x1, blocking collectives: none -> 47.5 us  [on_device(): lax.all_to_all(outgoing[local], 'exp', split_axis=0, concat_axis=0, tiled...]
    reshape x4 -> x0, local copies, waits for them, and re-layouts: 42.7 us -> none  [the longest x2 21.4 us: on_device(): rows_in.reshape(-1, model_width)]
    another operation x7 -> x0, local copies, waits for them, and re-layouts: 35.5 us -> none  [the longest x4 14.7 us: on_device(): back = jnp.stack([own_sum, parts[1]], axis=1)]
    squeeze x11 -> x1, local copies, waits for them, and re-layouts: 35.1 us -> 2.57 us  [on_device(): outgoing[local]]
    another operation x7 -> x1, other arithmetic: 27.6 us -> 0.01 us  [on_device(): slot_ids[None, None]]
    slice x2 -> x0, local copies, waits for them, and re-layouts: 18.8 us -> none  [on_device(): received[:, 1]]
    all_to_all x4 -> x3, starting transfers between devices: 26.5 us -> 14.7 us  [the longest x2 9.9 us: on_device(): lax.all_to_all(pair_sum, 'exp', split_axis=0, concat_axis=0, tiled=True)]
  transfers between devices with their start and end apart: 20 -> 15, of which waited for: 12 -> 12; matrix products, arithmetic and copies ran while one was open for 33% -> 9% of each run, Pallas kernels for 0% -> 0%
where the time goes in v4:
time: 441 us; the launch traced here: 440 us
  waiting for transfers between devices  290 us (66%)
  matrix products  50.6 us (11%)
  blocking collectives  47.5 us (11%)
  starting transfers between devices  31.4 us (7%)
  local copies, waits for them, and re-layouts  15 us (3%)
  other arithmetic  5.43 us (1%)
    ppermute x12, waiting for transfers between devices, seq_shift(): lax.ppermute(x, 'seq', [(i, (i + shift) % size) for i in range(size)])  185 us
    all_to_all x2, waiting for transfers between devices, on_device(): lax.all_to_all(pair_sum, 'exp', split_axis=0, concat_axis=0, tiled=True)  67.5 us
    all_to_all x1, blocking collectives, on_device(): lax.all_to_all(outgoing[local], 'exp', split_axis=0, concat_axis=0, tiled...  47.5 us
    all_to_all x1, waiting for transfers between devices, on_device(): lax.all_to_all(outgoing[local], 'exp', split_axis=0, concat_axis=0, tiled...  37.4 us
    dot_general x4, matrix products, expert_group(): jnp.einsum('gsd,dxf->gsxf', rows, gate_up, preferred_element_type=jnp.flo...  18.2 us
    ppermute x12, starting transfers between devices, seq_shift(): lax.ppermute(x, 'seq', [(i, (i + shift) % size) for i in range(size)])  16.7 us
    dot_general x4, matrix products, expert_group(): jnp.einsum('gsf,fd->gsd', hidden, down, preferred_element_type=jnp.float32)  14.3 us
    all_to_all x2, starting transfers between devices, on_device(): lax.all_to_all(pair_sum, 'exp', split_axis=0, concat_axis=0, tiled=True)  9.9 us
  transfers between devices with their start and end apart: 15, of which 12 were waited for; matrix products, arithmetic and copies ran while one was open for 9% of the time, Pallas kernels for 0%

profile of v4, /device:TPU:0, one launch (start us, length us, event | category | flops | bytes accessed | tf_op | source)
XLA Modules:
  0.0 440.0 jit_solution(11551544413682386968)
XLA Ops:
  0.0 2.1 reshape_squeeze.15
  2.1 2.4 constant_dynamic-slice_fusion.3
  5.4 2.9 collective-permute-start.2
  10.5 0.9 collective-permute-start
  12.3 8.9 %collective-permute-done.2 = bf16[96,3,512]{2,0,1:T(8,128)(2,1)S(1)} collective-permute-done((bf16[96,3,512]{2,0,1:T(8,128)(2,1)}, bf16[96,3,512]{2,0,1:T(8,128)(2,1)S(1)}, u32[]{:S(2)}, u32[]{:S(2)}) %collective-permute-start.2) | collective-permute-done | bytes 294944 | tf_op jit(solution)/shard_map/ppermute | solution.py:69
  21.1 4.3 collective-permute-done
  25.8 0.9 copy.58
  26.7 0.9 copy.59
  27.9 3.3 fusion.98
  31.1 2.1 convolution_convert_fusion.5
  33.3 1.0 fusion.99
  34.3 1.4 fusion.96
  36.4 2.1 collective-permute-start.4
  38.5 1.4 collective-permute-start.3
  40.8 33.3 %collective-permute-done.5 = f32[96,2048]{1,0:T(8,128)S(1)} collective-permute-done((f32[96,2048]{1,0:T(8,128)}, f32[96,2048]{1,0:T(8,128)S(1)}, u32[]{:S(2)}, u32[]{:S(2)}) %collective-permute-start.5) | collective-permute-done | bytes 786464 | tf_op jit(solution)/shard_map/ppermute | solution.py:69
  74.9 1.7 multiply_reduce_fusion.1
  76.7 1.1 collective-permute-start.6
  78.0 1.1 fusion.1
  79.1 9.4 %collective-permute-done.6 = bf16[96,2048]{1,0:T(8,128)(2,1)S(1)} collective-permute-done((bf16[96,2048]{1,0:T(8,128)(2,1)S(1)}, bf16[96,2048]{1,0:T(8,128)(2,1)S(1)}, u32[]{:S(2)}, u32[]{:S(2)}) %collective-permute-start.6) | collective-permute-done | bytes 393248 | tf_op jit(solution)/shard_map/ppermute | solution.py:69
  88.4 1.8 convolution_convert_fusion
  90.2 2.6 slice_bitcast_fusion.1
  92.8 47.5 %all_to_all.20 = bf16[32,24,2048]{2,1,0:T(8,128)(2,1)} all-to-all(bf16[32,24,2048]{2,1,0:T(8,128)(2,1)S(1)} %get-tuple-element.8), channel_id=1, replica_groups=mesh['seq'=4,'exp'=32] {'exp'}, dimensions={0} | all-to-all | bytes 6291456 | tf_op jit(solution)/shard_map/all_to_all | solution.py:137
  140.3 4.8 %all-to-all-start = ((bf16[32,24,2048]{2,1,0:T(8,128)(2,1)}), bf16[32,24,2048]{2,1,0:T(8,128)(2,1)}, u32[]{:S(2)}, u32[]{:S(2)}) async-start(bf16[32,24,2048]{2,1,0:T(8,128)(2,1)} %get-tuple-element.7), calls=%async_computation | async-start | bytes 6291456 | tf_op jit(solution)/shard_map/all_to_all | solution.py:137
  145.1 2.8 collective-permute-start.9
  147.9 37.4 %all-to-all-done = bf16[32,24,2048]{2,1,0:T(8,128)(2,1)} async-done(((bf16[32,24,2048]{2,1,0:T(8,128)(2,1)}), bf16[32,24,2048]{2,1,0:T(8,128)(2,1)}, u32[]{:S(2)}, u32[]{:S(2)}) %all-to-all-start) | async-done | bytes 3145760 | tf_op jit(solution)/shard_map/all_to_all | solution.py:137
  185.3 1.3 collective-permute-start.7
  186.7 29.3 %collective-permute-done.9 = bf16[32,24,2048]{2,1,0:T(8,128)(2,1)} collective-permute-done((bf16[32,24,2048]{2,1,0:T(8,128)(2,1)}, bf16[32,24,2048]{2,1,0:T(8,128)(2,1)}, u32[]{:S(2)}, u32[]{:S(2)}) %collective-permute-start.9) | collective-permute-done | bytes 3145760 | tf_op jit(solution)/shard_map/ppermute | solution.py:69
  215.9 5.4 %fusion.4 = f32[32,24,2,352]{3,1,2,0:T(8,128)S(1)} fusion(bf16[32,24,2048]{2,1,0:T(8,128)(2,1)} %collective-permute-done.9, bf16[2,2048,2,352]{1,3,2,0:T(8,128)(2,1)} %param.14), kind=kOutput, calls=%fused_computation.17 | convolution fusion | flops 2214592512 | bytes 8192000 | tf_op jit(solution)/shard_map/gsd,dxf->gsxf/dot_general | solution.py:40
  221.4 1.9 convolution_convert_fusion.1
  223.3 1.4 collective-permute-start.10
  224.7 33.0 %collective-permute-done.7 = bf16[32,24,2048]{2,1,0:T(8,128)(2,1)S(1)} collective-permute-done((bf16[32,24,2048]{2,1,0:T(8,128)(2,1)}, bf16[32,24,2048]{2,1,0:T(8,128)(2,1)S(1)}, u32[]{:S(2)}, u32[]{:S(2)}) %collective-permute-start.7) | collective-permute-done | bytes 3145760 | tf_op jit(solution)/shard_map/ppermute | solution.py:69
  257.7 4.6 %fusion.8 = f32[32,24,2,352]{3,1,2,0:T(8,128)S(1)} fusion(bf16[32,24,2048]{2,1,0:T(8,128)(2,1)S(1)} %collective-permute-done.7, bf16[2,2048,2,352]{1,3,2,0:T(8,128)(2,1)} %param.14), kind=kOutput, calls=%fused_computation.21 | convolution fusion | flops 2214592512 | bytes 8192000 | tf_op jit(solution)/shard_map/gsd,dxf->gsxf/dot_general | solution.py:40
  262.3 3.5 convolution_convert_fusion.3
  265.8 1.5 collective-permute-start.8
  267.3 2.7 fusion.6
  270.0 53.9 %collective-permute-done.10 = bf16[32,24,2048]{2,1,0:T(8,128)(2,1)S(1)} collective-permute-done((bf16[32,24,2048]{2,1,0:T(8,128)(2,1)S(1)}, bf16[32,24,2048]{2,1,0:T(8,128)(2,1)S(1)}, u32[]{:S(2)}, u32[]{:S(2)}) %collective-permute-start.10) | collective-permute-done | bytes 3145760 | tf_op jit(solution)/shard_map/ppermute | solution.py:69
  324.0 3.5 add_convert_fusion
  327.5 5.1 %all-to-all-start.3 = ((bf16[32,24,2048]{2,1,0:T(8,128)(2,1)}), bf16[32,24,2048]{2,1,0:T(8,128)(2,1)}, u32[]{:S(2)}, u32[]{:S(2)}) async-start(bf16[32,24,2048]{2,1,0:T(8,128)(2,1)} %add_convert_fusion), calls=%async_computation.3 | async-start | bytes 6291456 | tf_op jit(solution)/shard_map/all_to_all | solution.py:143
  332.6 5.5 %fusion.10 = f32[32,24,2,352]{3,1,2,0:T(8,128)S(1)} fusion(bf16[32,24,2048]{2,1,0:T(8,128)(2,1)} %all-to-all-done, bf16[2,2048,2,352]{1,3,2,0:T(8,128)(2,1)} %param.14), kind=kOutput, calls=%fused_computation.23 | convolution fusion | flops 2214592512 | bytes 8192000 | tf_op jit(solution)/shard_map/gsd,dxf->gsxf/dot_general | solution.py:40
  338.2 5.4 %add_convert_fusion.1 = bf16[32,24,2048]{2,1,0:T(8,128)(2,1)} fusion(bf16[32,24,2048]{2,1,0:T(8,128)(2,1)} %collective-permute-done.8, bf16[2,352,2048]{2,1,0:T(8,128)(2,1)S(1)} %copy-done.10, f32[32,24,2,352]{3,1,2,0:T(8,128)S(1)} %fusion.10), kind=kOutput, calls=%fused_computation.6 | convolution fusion | flops 1116782592 | bytes 10092544 | tf_op jit(solution)/shard_map/gsf,fd->gsd/dot_general | solution.py:42
  343.6 28.9 %all-to-all-done.3 = bf16[32,24,2048]{2,1,0:T(8,128)(2,1)} async-done(((bf16[32,24,2048]{2,1,0:T(8,128)(2,1)}), bf16[32,24,2048]{2,1,0:T(8,128)(2,1)}, u32[]{:S(2)}, u32[]{:S(2)}) %all-to-all-start.3) | async-done | bytes 3145760 | tf_op jit(solution)/shard_map/all_to_all | solution.py:143
  372.5 4.8 %all-to-all-start.1 = ((bf16[32,24,2048]{2,1,0:T(8,128)(2,1)}), bf16[32,24,2048]{2,1,0:T(8,128)(2,1)}, u32[]{:S(2)}, u32[]{:S(2)}) async-start(bf16[32,24,2048]{2,1,0:T(8,128)(2,1)} %add_convert_fusion.1), calls=%async_computation.1 | async-start | bytes 6291456 | tf_op jit(solution)/shard_map/all_to_all | solution.py:143
  377.9 1.1 select_reduce_fusion
  379.0 38.6 %all-to-all-done.1 = bf16[32,24,2048]{2,1,0:T(8,128)(2,1)} async-done(((bf16[32,24,2048]{2,1,0:T(8,128)(2,1)}), bf16[32,24,2048]{2,1,0:T(8,128)(2,1)}, u32[]{:S(2)}, u32[]{:S(2)}) %all-to-all-start.1) | async-done | bytes 3145760 | tf_op jit(solution)/shard_map/all_to_all | solution.py:143
  417.6 3.7 fusion.16
  421.2 5.5 %fusion.22 = f32[192,2048]{1,0:T(8,128)S(1)} fusion(f32[192,2048]{1,0:T(8,128)S(1)} %fusion.16, bf16[1,32,24,2048]{3,2,1,0:T(8,128)(2,1)} %bitcast.44, bf16[1,32,24,2048]{3,2,1,0:T(8,128)(2,1)} %bitcast.32, f32[192,2,32,24]{0,3,2,1:T(8,128)} %copy-done.4), kind=kOutput, calls=%fused_computation.35 | convolution fusion | flops 1212678144 | bytes 10616832 | tf_op jit(solution)/shard_map/pcgs,cgsd->pd/dot_general | solution.py:157
  427.3 11.8 %collective-permute-done.11 = bf16[96,2048]{1,0:T(8,128)(2,1)S(1)} collective-permute-done((bf16[96,2048]{1,0:T(8,128)(2,1)S(1)}, bf16[96,2048]{1,0:T(8,128)(2,1)S(1)}, u32[]{:S(2)}, u32[]{:S(2)}) %collective-permute-start.11) | collective-permute-done | bytes 393248 | tf_op jit(solution)/shard_map/ppermute | solution.py:69
  439.2 0.9 fusion.66
  (70 shorter events, 8.2 us)
Async XLA Ops:
  0.0 33.2 %copy-start = (bf16[512,2048]{1,0:T(8,128)(2,1)S(1)}, bf16[512,2048]{1,0:T(8,128)(2,1)}, u32[]{:S(2)}) copy-start(bf16[512,2048]{1,0:T(8,128)(2,1)} %param.10) | copy-start | bytes 6291460
  4.6 6.9 %copy-start.7 = (s32[1,384,6]{1,0,2:T(1,128)S(1)}, s32[1,384,6]{1,0,2:T(1,128)}, u32[]{:S(2)}) copy-start(s32[1,384,6]{1,0,2:T(1,128)} %param.13) | copy-start | bytes 27652
  5.4 15.8 %collective-permute-start.2 = (bf16[96,3,512]{2,0,1:T(8,128)(2,1)}, bf16[96,3,512]{2,0,1:T(8,128)(2,1)S(1)}, u32[]{:S(2)}, u32[]{:S(2)}) collective-permute-start(bf16[96,3,512]{2,0,1:T(8,128)(2,1)} %bitcast.133), channel_id=1, source_target_pairs={{0,96},{32,0},{64,32},{96,64},{1,97},{33,1},{65,33},{97,65},{2,98}... | collective-permute-start | bytes 884744 | tf_op jit(solution)/shard_map/ppermute | solution.py:69
  9.0 12.2 %collective-permute-start.1 = (bf16[96,3,512]{2,0,1:T(8,128)(2,1)}, bf16[96,3,512]{2,0,1:T(8,128)(2,1)S(1)}, u32[]{:S(2)}, u32[]{:S(2)}) collective-permute-start(bf16[96,3,512]{2,0,1:T(8,128)(2,1)} %bitcast.134), channel_id=1, source_target_pairs={{0,64},{32,96},{64,0},{96,32},{1,65},{33,97},{65,1},{97,33},{2,66}... | collective-permute-start | bytes 884744 | tf_op jit(solution)/shard_map/ppermute | solution.py:69
  10.5 15.0 %collective-permute-start = (bf16[96,3,512]{2,0,1:T(8,128)(2,1)}, bf16[96,3,512]{2,0,1:T(8,128)(2,1)S(1)}, u32[]{:S(2)}, u32[]{:S(2)}) collective-permute-start(bf16[96,3,512]{2,0,1:T(8,128)(2,1)} %bitcast.135), channel_id=1, source_target_pairs={{0,32},{32,64},{64,96},{96,0},{1,33},{33,65},{65,97},{97,1},{2,34}... | collective-permute-start | bytes 884744 | tf_op jit(solution)/shard_map/ppermute | solution.py:69
  26.7 4.4 %copy-start.6 = (bf16[384,1,512]{0,2,1:T(8,128)(2,1)S(1)}, bf16[384,1,512]{0,2,1:T(8,128)(2,1)}, u32[]{:S(2)}) copy-start(bf16[384,1,512]{0,2,1:T(8,128)(2,1)} %copy.58) | copy-start | bytes 1179652
  34.3 2.1 copy-start.2
  34.3 40.6 %copy-start.5 = (bf16[1,96,2048]{2,1,0:T(8,128)(2,1)S(1)}, bf16[1,96,2048]{2,1,0:T(8,128)(2,1)}, u32[]{:S(2)}) copy-start(bf16[1,96,2048]{2,1,0:T(8,128)(2,1)} %param.8) | copy-start | bytes 1179652
  36.4 37.7 %collective-permute-start.5 = (f32[96,2048]{1,0:T(8,128)}, f32[96,2048]{1,0:T(8,128)S(1)}, u32[]{:S(2)}, u32[]{:S(2)}) collective-permute-start(f32[96,2048]{1,0:T(8,128)} %get-tuple-element.10), channel_id=1, source_target_pairs={{0,32},{32,64},{64,96},{96,0},{1,33},{33,65},{65,97},{97,1},{2,34}... | collective-permute-start | bytes 2359304 | tf_op jit(solution)/shard_map/ppermute | solution.py:69
  36.4 37.7 %collective-permute-start.4 = (f32[96,2048]{1,0:T(8,128)}, f32[96,2048]{1,0:T(8,128)S(1)}, u32[]{:S(2)}, u32[]{:S(2)}) collective-permute-start(f32[96,2048]{1,0:T(8,128)} %get-tuple-element.11), channel_id=1, source_target_pairs={{0,64},{32,96},{64,0},{96,32},{1,65},{33,97},{65,1},{97,33},{2,66}... | collective-permute-start | bytes 2359304 | tf_op jit(solution)/shard_map/ppermute | solution.py:69
  38.5 36.4 %collective-permute-start.3 = (f32[96,2048]{1,0:T(8,128)S(1)}, f32[96,2048]{1,0:T(8,128)}, u32[]{:S(2)}, u32[]{:S(2)}) collective-permute-start(f32[96,2048]{1,0:T(8,128)S(1)} %get-tuple-element.9), channel_id=1, source_target_pairs={{0,96},{32,0},{64,32},{96,64},{1,97},{33,1},{65,33},{97,65},{2,98}... | collective-permute-start | bytes 2359304 | tf_op jit(solution)/shard_map/ppermute | solution.py:69
  40.6 36.0 %copy-start.8 = (f32[2048]{0:T(1024)S(1)}, f32[2048]{0:T(1024)}, u32[]{:S(2)}) copy-start(f32[2048]{0:T(1024)} %param.11) | copy-start | bytes 24580
  76.7 11.7 %collective-permute-start.6 = (bf16[96,2048]{1,0:T(8,128)(2,1)S(1)}, bf16[96,2048]{1,0:T(8,128)(2,1)S(1)}, u32[]{:S(2)}, u32[]{:S(2)}) collective-permute-start(bf16[96,2048]{1,0:T(8,128)(2,1)S(1)} %multiply_convert_fusion), channel_id=1, source_target_pairs={{0,64},{32,96},{64,0},{96,32},{1,65},{33,97},{65,1},{97,33},{2,66}... | collective-permute-start | bytes 1179656 | tf_op jit(solution)/shard_map/ppermute | solution.py:69
  140.3 45.0 %all-to-all-start = ((bf16[32,24,2048]{2,1,0:T(8,128)(2,1)}), bf16[32,24,2048]{2,1,0:T(8,128)(2,1)}, u32[]{:S(2)}, u32[]{:S(2)}) async-start(bf16[32,24,2048]{2,1,0:T(8,128)(2,1)} %get-tuple-element.7), calls=%async_computation | async-start | bytes 6291456 | tf_op jit(solution)/shard_map/all_to_all | solution.py:137
  145.1 70.8 %collective-permute-start.9 = (bf16[32,24,2048]{2,1,0:T(8,128)(2,1)}, bf16[32,24,2048]{2,1,0:T(8,128)(2,1)}, u32[]{:S(2)}, u32[]{:S(2)}) collective-permute-start(bf16[32,24,2048]{2,1,0:T(8,128)(2,1)} %all_to_all.20), channel_id=1, source_target_pairs={{0,96},{32,0},{64,32},{96,64},{1,97},{33,1},{65,33},{97,65},{2,98}... | collective-permute-start | bytes 9437192 | tf_op jit(solution)/shard_map/ppermute | solution.py:69
  185.3 36.0 %copy-start.9 = (bf16[2,352,2048]{2,1,0:T(8,128)(2,1)S(1)}, bf16[2,352,2048]{2,1,0:T(8,128)(2,1)}, u32[]{:S(2)}) copy-start(bf16[2,352,2048]{2,1,0:T(8,128)(2,1)} %param.15) | copy-start | bytes 8650756
  185.3 72.4 %collective-permute-start.7 = (bf16[32,24,2048]{2,1,0:T(8,128)(2,1)}, bf16[32,24,2048]{2,1,0:T(8,128)(2,1)S(1)}, u32[]{:S(2)}, u32[]{:S(2)}) collective-permute-start(bf16[32,24,2048]{2,1,0:T(8,128)(2,1)} %all-to-all-done), channel_id=1, source_target_pairs={{0,32},{32,64},{64,96},{96,0},{1,33},{33,65},{65,97},{97,1},{2,34}... | collective-permute-start | bytes 9437192 | tf_op jit(solution)/shard_map/ppermute | solution.py:69
  221.4 46.0 %slice-start = ((s8[5767168]{0:T(1024)(128)(4,1)}), s8[4194304]{0:T(1024)(128)(4,1)S(1)}, s32[]{:S(2)}) async-start(s8[5767168]{0:T(1024)(128)(4,1)} %bitcast.146), calls=%async_computation.4 | async-start | bytes 8388608
  223.3 44.1 %slice-start.1 = ((s8[5767168]{0:T(1024)(128)(4,1)}), s8[1572864]{0:T(1024)(128)(4,1)S(1)}, s32[]{:S(2)}) async-start(s8[5767168]{0:T(1024)(128)(4,1)} %bitcast.146), calls=%async_computation.5 | async-start | bytes 3145728
  223.3 100.7 %collective-permute-start.10 = (bf16[32,24,2048]{2,1,0:T(8,128)(2,1)S(1)}, bf16[32,24,2048]{2,1,0:T(8,128)(2,1)S(1)}, u32[]{:S(2)}, u32[]{:S(2)}) collective-permute-start(bf16[32,24,2048]{2,1,0:T(8,128)(2,1)S(1)} %convolution_convert_fusion.1), channel_id=1, source_target_pairs={{0,32},{32,64},{64,96},{96,0},{1,33},{33,65},{65,97},{97,1},{2,34}... | collective-permute-start | bytes 9437192 | tf_op jit(solution)/shard_map/ppermute | solution.py:69
  262.3 5.0 %copy-start.3 = (bf16[32,24,2048]{2,1,0:T(8,128)(2,1)S(1)}, bf16[32,24,2048]{2,1,0:T(8,128)(2,1)}, u32[]{:S(2)}) copy-start(bf16[32,24,2048]{2,1,0:T(8,128)(2,1)} %all_to_all.20) | copy-start | bytes 9437188
  265.8 72.4 %collective-permute-start.8 = (bf16[32,24,2048]{2,1,0:T(8,128)(2,1)}, bf16[32,24,2048]{2,1,0:T(8,128)(2,1)}, u32[]{:S(2)}, u32[]{:S(2)}) collective-permute-start(bf16[32,24,2048]{2,1,0:T(8,128)(2,1)} %convolution_convert_fusion.3), channel_id=1, source_target_pairs={{0,96},{32,0},{64,32},{96,64},{1,97},{33,1},{65,33},{97,65},{2,98}... | collective-permute-start | bytes 9437192 | tf_op jit(solution)/shard_map/ppermute | solution.py:69
  327.5 45.0 %all-to-all-start.3 = ((bf16[32,24,2048]{2,1,0:T(8,128)(2,1)}), bf16[32,24,2048]{2,1,0:T(8,128)(2,1)}, u32[]{:S(2)}, u32[]{:S(2)}) async-start(bf16[32,24,2048]{2,1,0:T(8,128)(2,1)} %add_convert_fusion), calls=%async_computation.3 | async-start | bytes 6291456 | tf_op jit(solution)/shard_map/all_to_all | solution.py:143
  332.6 5.6 %copy-start.10 = (bf16[2,352,2048]{2,1,0:T(8,128)(2,1)S(1)}, bf16[2,352,2048]{2,1,0:T(8,128)(2,1)}, u32[]{:S(2)}) copy-start(bf16[2,352,2048]{2,1,0:T(8,128)(2,1)} %param.15) | copy-start | bytes 8650756
  343.6 33.8 %copy-start.11 = (bf16[2048,64]{0,1:T(8,128)(2,1)S(1)}, bf16[2048,64]{0,1:T(8,128)(2,1)}, u32[]{:S(2)}) copy-start(bf16[2048,64]{0,1:T(8,128)(2,1)} %param.12) | copy-start | bytes 786436
  372.5 45.0 %all-to-all-start.1 = ((bf16[32,24,2048]{2,1,0:T(8,128)(2,1)}), bf16[32,24,2048]{2,1,0:T(8,128)(2,1)}, u32[]{:S(2)}, u32[]{:S(2)}) async-start(bf16[32,24,2048]{2,1,0:T(8,128)(2,1)} %add_convert_fusion.1), calls=%async_computation.1 | async-start | bytes 6291456 | tf_op jit(solution)/shard_map/all_to_all | solution.py:143
  379.0 38.6 %copy-start.4 = (f32[192,2,32,24]{0,3,2,1:T(8,128)}, f32[192,2,32,24]{0,3,2,1:T(8,128)S(1)}, u32[]{:S(2)}) copy-start(f32[192,2,32,24]{0,3,2,1:T(8,128)S(1)} %select_reduce_fusion) | copy-start | bytes 3538948
  421.2 18.8 %copy-start.1 = (bf16[512,2048]{1,0:T(8,128)(2,1)S(1)}, bf16[512,2048]{1,0:T(8,128)(2,1)}, u32[]{:S(2)}) copy-start(bf16[512,2048]{1,0:T(8,128)(2,1)} %param.10) | copy-start | bytes 6291460
  426.8 12.4 %collective-permute-start.11 = (bf16[96,2048]{1,0:T(8,128)(2,1)S(1)}, bf16[96,2048]{1,0:T(8,128)(2,1)S(1)}, u32[]{:S(2)}, u32[]{:S(2)}) collective-permute-start(bf16[96,2048]{1,0:T(8,128)(2,1)S(1)} %slice.227), channel_id=1, source_target_pairs={{0,64},{32,96},{64,0},{96,32},{1,65},{33,97},{65,1},{97,33},{2,66}... | collective-permute-start | bytes 1179656 | tf_op jit(solution)/shard_map/ppermute | solution.py:69

commit v5 on v4

--- a/solution.py
+++ b/solution.py
@@ -69,6 +69,17 @@
     return lax.ppermute(x, "seq", [(i, (i + shift) % size) for i in range(size)])
 
 
+def paired_shift(x, local, seq_size, exp_size, back):
+    pairs = []
+    for s in range(seq_size):
+        for e in range(exp_size):
+            step = 1 if (local + e) % 2 == 0 else -1
+            if back:
+                step = -step
+            pairs.append((s * exp_size + e, ((s + step) % seq_size) * exp_size + e))
+    return lax.ppermute(x, ("seq", "exp"), pairs)
+
+
 def on_device(resid, qkv, w_out, norm_gain, router_w, expert_ids, w_gate_up, w_down):
     row_count = resid.shape[1]
     model_width = resid.shape[2]
@@ -133,12 +144,11 @@
     ).astype(jnp.bfloat16)
     homes = []
     for local in range(exp_local):
-        direction = 1 if local % 2 == 0 else -1
         received = lax.all_to_all(outgoing[local], "exp", split_axis=0, concat_axis=0, tiled=True)
-        forwarded = seq_shift(received, direction, seq_size)
+        forwarded = paired_shift(received, local, seq_size, exp_size, False)
         mine = expert_group(received, w_gate_up[local], w_down[local])
         theirs = expert_group(forwarded, w_gate_up[local], w_down[local])
-        returned = seq_shift(theirs, -direction, seq_size)
+        returned = paired_shift(theirs, local, seq_size, exp_size, True)
         pair_sum = (mine.astype(jnp.float32) + returned.astype(jnp.float32)).astype(jnp.bfloat16)
         homes.append(lax.all_to_all(pair_sum, "exp", split_axis=0, concat_axis=0, tiled=True))
     table = jnp.stack(homes, axis=0)

time: 441 us -> 398 us (0.902)
  waiting for transfers between devices: 290 us -> 248 us
    ppermute x12 -> x8, waiting for transfers between devices: 185 us -> 68.7 us  [seq_shift(): lax.ppermute(x, 'seq', [(i, (i + shift) % size) for i in range(size)])]
    ppermute x0 -> x4, waiting for transfers between devices: none -> 74.1 us  [paired_shift(): return lax.ppermute(x, ('seq', 'exp'), pairs)]
    ppermute x12 -> x8, starting transfers between devices: 16.7 us -> 9.45 us  [seq_shift(): lax.ppermute(x, 'seq', [(i, (i + shift) % size) for i in range(size)])]
    ppermute x0 -> x4, starting transfers between devices: none -> 6.04 us  [paired_shift(): return lax.ppermute(x, ('seq', 'exp'), pairs)]
  transfers between devices with their start and end apart: 15 -> 15, of which waited for: 12 -> 11; matrix products, arithmetic and copies ran while one was open for 9% -> 10% of each run, Pallas kernels for 0% -> 0%
where the time goes in v5:
time: 398 us; the launch traced here: 397 us
  waiting for transfers between devices  248 us (62%)
  matrix products  50.6 us (13%)
  blocking collectives  47.5 us (12%)
  starting transfers between devices  30.5 us (8%)
  local copies, waits for them, and re-layouts  15 us (4%)
  other arithmetic  5.43 us (1%)
    ppermute x4, waiting for transfers between devices, paired_shift(): return lax.ppermute(x, ('seq', 'exp'), pairs)  74.1 us
    ppermute x8, waiting for transfers between devices, seq_shift(): lax.ppermute(x, 'seq', [(i, (i + shift) % size) for i in range(size)])  68.7 us
    all_to_all x2, waiting for transfers between devices, on_device(): lax.all_to_all(pair_sum, 'exp', split_axis=0, concat_axis=0, tiled=True)  67.5 us
    all_to_all x1, blocking collectives, on_device(): lax.all_to_all(outgoing[local], 'exp', split_axis=0, concat_axis=0, tiled...  47.5 us
    all_to_all x1, waiting for transfers between devices, on_device(): lax.all_to_all(outgoing[local], 'exp', split_axis=0, concat_axis=0, tiled...  37.4 us
    dot_general x4, matrix products, expert_group(): jnp.einsum('gsd,dxf->gsxf', rows, gate_up, preferred_element_type=jnp.flo...  18.2 us
    dot_general x4, matrix products, expert_group(): jnp.einsum('gsf,fd->gsd', hidden, down, preferred_element_type=jnp.float32)  14.3 us
    all_to_all x2, starting transfers between devices, on_device(): lax.all_to_all(pair_sum, 'exp', split_axis=0, concat_axis=0, tiled=True)  10.2 us
  transfers between devices with their start and end apart: 15, of which 11 were waited for; matrix products, arithmetic and copies ran while one was open for 10% of the time, Pallas kernels for 0%

profile of v5, /device:TPU:0, one launch (start us, length us, event | category | flops | bytes accessed | tf_op | source)
XLA Modules:
  0.0 397.2 jit_solution(1710568828610836337)
XLA Ops:
  0.0 2.1 reshape_squeeze.15
  2.1 2.4 constant_dynamic-slice_fusion.3
  5.4 2.9 collective-permute-start.2
  9.0 0.8 collective-permute-start.1
  10.5 0.9 collective-permute-start
  12.3 8.9 %collective-permute-done.2 = bf16[96,3,512]{2,0,1:T(8,128)(2,1)S(1)} collective-permute-done((bf16[96,3,512]{2,0,1:T(8,128)(2,1)}, bf16[96,3,512]{2,0,1:T(8,128)(2,1)S(1)}, u32[]{:S(2)}, u32[]{:S(2)}) %collective-permute-start.2) | collective-permute-done | bytes 294944 | tf_op jit(solution)/shard_map/ppermute | solution.py:69
  21.1 4.3 %collective-permute-done = bf16[96,3,512]{2,0,1:T(8,128)(2,1)S(1)} collective-permute-done((bf16[96,3,512]{2,0,1:T(8,128)(2,1)}, bf16[96,3,512]{2,0,1:T(8,128)(2,1)S(1)}, u32[]{:S(2)}, u32[]{:S(2)}) %collective-permute-start) | collective-permute-done | bytes 294944 | tf_op jit(solution)/shard_map/ppermute | solution.py:69
  25.8 0.9 copy.58
  26.7 0.9 copy.59
  27.9 3.3 fusion.98
  31.1 2.1 convolution_convert_fusion.5
  33.3 1.0 fusion.99
  34.3 1.4 fusion.96
  35.6 0.8 copy-done.2
  36.4 2.1 collective-permute-start.4
  38.5 1.4 collective-permute-start.3
  40.8 33.3 %collective-permute-done.5 = f32[96,2048]{1,0:T(8,128)S(1)} collective-permute-done((f32[96,2048]{1,0:T(8,128)}, f32[96,2048]{1,0:T(8,128)S(1)}, u32[]{:S(2)}, u32[]{:S(2)}) %collective-permute-start.5) | collective-permute-done | bytes 786464 | tf_op jit(solution)/shard_map/ppermute | solution.py:69
  74.9 1.7 multiply_reduce_fusion.1
  76.7 1.1 collective-permute-start.6
  78.0 1.1 fusion.1
  79.1 9.4 %collective-permute-done.6 = bf16[96,2048]{1,0:T(8,128)(2,1)S(1)} collective-permute-done((bf16[96,2048]{1,0:T(8,128)(2,1)S(1)}, bf16[96,2048]{1,0:T(8,128)(2,1)S(1)}, u32[]{:S(2)}, u32[]{:S(2)}) %collective-permute-start.6) | collective-permute-done | bytes 393248 | tf_op jit(solution)/shard_map/ppermute | solution.py:69
  88.4 1.8 convolution_convert_fusion
  90.2 2.6 slice_bitcast_fusion.1
  92.8 47.5 %all_to_all.20 = bf16[32,24,2048]{2,1,0:T(8,128)(2,1)} all-to-all(bf16[32,24,2048]{2,1,0:T(8,128)(2,1)S(1)} %get-tuple-element.8), channel_id=1, replica_groups=mesh['seq'=4,'exp'=32] {'exp'}, dimensions={0} | all-to-all | bytes 6291456 | tf_op jit(solution)/shard_map/all_to_all | solution.py:147
  140.3 4.8 %all-to-all-start = ((bf16[32,24,2048]{2,1,0:T(8,128)(2,1)}), bf16[32,24,2048]{2,1,0:T(8,128)(2,1)}, u32[]{:S(2)}, u32[]{:S(2)}) async-start(bf16[32,24,2048]{2,1,0:T(8,128)(2,1)} %get-tuple-element.7), calls=%async_computation | async-start | bytes 6291456 | tf_op jit(solution)/shard_map/all_to_all | solution.py:147
  145.1 2.8 collective-permute-start.9
  147.9 37.4 %all-to-all-done = bf16[32,24,2048]{2,1,0:T(8,128)(2,1)} async-done(((bf16[32,24,2048]{2,1,0:T(8,128)(2,1)}), bf16[32,24,2048]{2,1,0:T(8,128)(2,1)}, u32[]{:S(2)}, u32[]{:S(2)}) %all-to-all-start) | async-done | bytes 3145760 | tf_op jit(solution)/shard_map/all_to_all | solution.py:147
  185.3 1.3 collective-permute-start.7
  186.7 5.4 %fusion.4 = f32[32,24,2,352]{3,1,2,0:T(8,128)S(1)} fusion(bf16[32,24,2048]{2,1,0:T(8,128)(2,1)} %collective-permute-done.9, bf16[2,2048,2,352]{1,3,2,0:T(8,128)(2,1)} %param.14), kind=kOutput, calls=%fused_computation.17 | convolution fusion | flops 2214592512 | bytes 8192000 | tf_op jit(solution)/shard_map/gsd,dxf->gsxf/dot_general | solution.py:40
  192.1 1.9 convolution_convert_fusion.1
  194.4 29.6 %collective-permute-done.7 = bf16[32,24,2048]{2,1,0:T(8,128)(2,1)S(1)} collective-permute-done((bf16[32,24,2048]{2,1,0:T(8,128)(2,1)}, bf16[32,24,2048]{2,1,0:T(8,128)(2,1)S(1)}, u32[]{:S(2)}, u32[]{:S(2)}) %collective-permute-start.7) | collective-permute-done | bytes 3145760 | tf_op jit(solution)/shard_map/ppermute | solution.py:80
  224.0 4.6 %fusion.8 = f32[32,24,2,352]{3,1,2,0:T(8,128)S(1)} fusion(bf16[32,24,2048]{2,1,0:T(8,128)(2,1)S(1)} %collective-permute-done.7, bf16[2,2048,2,352]{1,3,2,0:T(8,128)(2,1)} %param.14), kind=kOutput, calls=%fused_computation.21 | convolution fusion | flops 2214592512 | bytes 8192000 | tf_op jit(solution)/shard_map/gsd,dxf->gsxf/dot_general | solution.py:40
  228.6 3.5 convolution_convert_fusion.3
  232.1 1.5 collective-permute-start.8
  233.6 2.7 fusion.6
  236.3 44.5 %collective-permute-done.10 = bf16[32,24,2048]{2,1,0:T(8,128)(2,1)S(1)} collective-permute-done((bf16[32,24,2048]{2,1,0:T(8,128)(2,1)S(1)}, bf16[32,24,2048]{2,1,0:T(8,128)(2,1)S(1)}, u32[]{:S(2)}, u32[]{:S(2)}) %collective-permute-start.10) | collective-permute-done | bytes 3145760 | tf_op jit(solution)/shard_map/ppermute | solution.py:80
  280.9 3.5 add_convert_fusion
  284.4 5.3 %all-to-all-start.3 = ((bf16[32,24,2048]{2,1,0:T(8,128)(2,1)}), bf16[32,24,2048]{2,1,0:T(8,128)(2,1)}, u32[]{:S(2)}, u32[]{:S(2)}) async-start(bf16[32,24,2048]{2,1,0:T(8,128)(2,1)} %add_convert_fusion), calls=%async_computation.3 | async-start | bytes 6291456 | tf_op jit(solution)/shard_map/all_to_all | solution.py:153
  289.8 5.6 %fusion.10 = f32[32,24,2,352]{3,1,2,0:T(8,128)S(1)} fusion(bf16[32,24,2048]{2,1,0:T(8,128)(2,1)} %all-to-all-done, bf16[2,2048,2,352]{1,3,2,0:T(8,128)(2,1)} %param.14), kind=kOutput, calls=%fused_computation.23 | convolution fusion | flops 2214592512 | bytes 8192000 | tf_op jit(solution)/shard_map/gsd,dxf->gsxf/dot_general | solution.py:40
  295.4 5.4 %add_convert_fusion.1 = bf16[32,24,2048]{2,1,0:T(8,128)(2,1)} fusion(bf16[32,24,2048]{2,1,0:T(8,128)(2,1)} %collective-permute-done.8, bf16[2,352,2048]{2,1,0:T(8,128)(2,1)S(1)} %copy-done.10, f32[32,24,2,352]{3,1,2,0:T(8,128)S(1)} %fusion.10), kind=kOutput, calls=%fused_computation.6 | convolution fusion | flops 1116782592 | bytes 10092544 | tf_op jit(solution)/shard_map/gsf,fd->gsd/dot_general | solution.py:42
  300.7 28.9 %all-to-all-done.3 = bf16[32,24,2048]{2,1,0:T(8,128)(2,1)} async-done(((bf16[32,24,2048]{2,1,0:T(8,128)(2,1)}), bf16[32,24,2048]{2,1,0:T(8,128)(2,1)}, u32[]{:S(2)}, u32[]{:S(2)}) %all-to-all-start.3) | async-done | bytes 3145760 | tf_op jit(solution)/shard_map/all_to_all | solution.py:153
  329.7 4.8 %all-to-all-start.1 = ((bf16[32,24,2048]{2,1,0:T(8,128)(2,1)}), bf16[32,24,2048]{2,1,0:T(8,128)(2,1)}, u32[]{:S(2)}, u32[]{:S(2)}) async-start(bf16[32,24,2048]{2,1,0:T(8,128)(2,1)} %add_convert_fusion.1), calls=%async_computation.1 | async-start | bytes 6291456 | tf_op jit(solution)/shard_map/all_to_all | solution.py:153
  335.0 1.1 select_reduce_fusion
  336.1 38.6 %all-to-all-done.1 = bf16[32,24,2048]{2,1,0:T(8,128)(2,1)} async-done(((bf16[32,24,2048]{2,1,0:T(8,128)(2,1)}), bf16[32,24,2048]{2,1,0:T(8,128)(2,1)}, u32[]{:S(2)}, u32[]{:S(2)}) %all-to-all-start.1) | async-done | bytes 3145760 | tf_op jit(solution)/shard_map/all_to_all | solution.py:153
  374.7 3.7 fusion.16
  378.4 5.5 %fusion.22 = f32[192,2048]{1,0:T(8,128)S(1)} fusion(f32[192,2048]{1,0:T(8,128)S(1)} %fusion.16, bf16[1,32,24,2048]{3,2,1,0:T(8,128)(2,1)} %bitcast.44, bf16[1,32,24,2048]{3,2,1,0:T(8,128)(2,1)} %bitcast.32, f32[192,2,32,24]{0,3,2,1:T(8,128)} %copy-done.4), kind=kOutput, calls=%fused_computation.35 | convolution fusion | flops 1212678144 | bytes 10616832 | tf_op jit(solution)/shard_map/pcgs,cgsd->pd/dot_general | solution.py:167
  384.2 12.1 %collective-permute-done.11 = bf16[96,2048]{1,0:T(8,128)(2,1)S(1)} collective-permute-done((bf16[96,2048]{1,0:T(8,128)(2,1)S(1)}, bf16[96,2048]{1,0:T(8,128)(2,1)S(1)}, u32[]{:S(2)}, u32[]{:S(2)}) %collective-permute-start.11) | collective-permute-done | bytes 393248 | tf_op jit(solution)/shard_map/ppermute | solution.py:69
  396.3 0.9 fusion.66
  (70 shorter events, 6.8 us)
Async XLA Ops:
  0.0 33.2 %copy-start = (bf16[512,2048]{1,0:T(8,128)(2,1)S(1)}, bf16[512,2048]{1,0:T(8,128)(2,1)}, u32[]{:S(2)}) copy-start(bf16[512,2048]{1,0:T(8,128)(2,1)} %param.10) | copy-start | bytes 6291460
  4.6 6.9 %copy-start.7 = (s32[1,384,6]{1,0,2:T(1,128)S(1)}, s32[1,384,6]{1,0,2:T(1,128)}, u32[]{:S(2)}) copy-start(s32[1,384,6]{1,0,2:T(1,128)} %param.13) | copy-start | bytes 27652
  5.4 15.8 %collective-permute-start.2 = (bf16[96,3,512]{2,0,1:T(8,128)(2,1)}, bf16[96,3,512]{2,0,1:T(8,128)(2,1)S(1)}, u32[]{:S(2)}, u32[]{:S(2)}) collective-permute-start(bf16[96,3,512]{2,0,1:T(8,128)(2,1)} %bitcast.133), channel_id=1, source_target_pairs={{0,96},{32,0},{64,32},{96,64},{1,97},{33,1},{65,33},{97,65},{2,98}... | collective-permute-start | bytes 884744 | tf_op jit(solution)/shard_map/ppermute | solution.py:69
  9.0 12.2 %collective-permute-start.1 = (bf16[96,3,512]{2,0,1:T(8,128)(2,1)}, bf16[96,3,512]{2,0,1:T(8,128)(2,1)S(1)}, u32[]{:S(2)}, u32[]{:S(2)}) collective-permute-start(bf16[96,3,512]{2,0,1:T(8,128)(2,1)} %bitcast.134), channel_id=1, source_target_pairs={{0,64},{32,96},{64,0},{96,32},{1,65},{33,97},{65,1},{97,33},{2,66}... | collective-permute-start | bytes 884744 | tf_op jit(solution)/shard_map/ppermute | solution.py:69
  10.5 15.0 %collective-permute-start = (bf16[96,3,512]{2,0,1:T(8,128)(2,1)}, bf16[96,3,512]{2,0,1:T(8,128)(2,1)S(1)}, u32[]{:S(2)}, u32[]{:S(2)}) collective-permute-start(bf16[96,3,512]{2,0,1:T(8,128)(2,1)} %bitcast.135), channel_id=1, source_target_pairs={{0,32},{32,64},{64,96},{96,0},{1,33},{33,65},{65,97},{97,1},{2,34}... | collective-permute-start | bytes 884744 | tf_op jit(solution)/shard_map/ppermute | solution.py:69
  26.7 4.4 %copy-start.6 = (bf16[384,1,512]{0,2,1:T(8,128)(2,1)S(1)}, bf16[384,1,512]{0,2,1:T(8,128)(2,1)}, u32[]{:S(2)}) copy-start(bf16[384,1,512]{0,2,1:T(8,128)(2,1)} %copy.58) | copy-start | bytes 1179652
  34.3 2.1 copy-start.2
  34.3 40.6 %copy-start.5 = (bf16[1,96,2048]{2,1,0:T(8,128)(2,1)S(1)}, bf16[1,96,2048]{2,1,0:T(8,128)(2,1)}, u32[]{:S(2)}) copy-start(bf16[1,96,2048]{2,1,0:T(8,128)(2,1)} %param.8) | copy-start | bytes 1179652
  36.4 37.7 %collective-permute-start.5 = (f32[96,2048]{1,0:T(8,128)}, f32[96,2048]{1,0:T(8,128)S(1)}, u32[]{:S(2)}, u32[]{:S(2)}) collective-permute-start(f32[96,2048]{1,0:T(8,128)} %get-tuple-element.10), channel_id=1, source_target_pairs={{0,32},{32,64},{64,96},{96,0},{1,33},{33,65},{65,97},{97,1},{2,34}... | collective-permute-start | bytes 2359304 | tf_op jit(solution)/shard_map/ppermute | solution.py:69
  36.4 37.7 %collective-permute-start.4 = (f32[96,2048]{1,0:T(8,128)}, f32[96,2048]{1,0:T(8,128)S(1)}, u32[]{:S(2)}, u32[]{:S(2)}) collective-permute-start(f32[96,2048]{1,0:T(8,128)} %get-tuple-element.11), channel_id=1, source_target_pairs={{0,64},{32,96},{64,0},{96,32},{1,65},{33,97},{65,1},{97,33},{2,66}... | collective-permute-start | bytes 2359304 | tf_op jit(solution)/shard_map/ppermute | solution.py:69
  38.5 36.4 %collective-permute-start.3 = (f32[96,2048]{1,0:T(8,128)S(1)}, f32[96,2048]{1,0:T(8,128)}, u32[]{:S(2)}, u32[]{:S(2)}) collective-permute-start(f32[96,2048]{1,0:T(8,128)S(1)} %get-tuple-element.9), channel_id=1, source_target_pairs={{0,96},{32,0},{64,32},{96,64},{1,97},{33,1},{65,33},{97,65},{2,98}... | collective-permute-start | bytes 2359304 | tf_op jit(solution)/shard_map/ppermute | solution.py:69
  40.6 36.0 %copy-start.8 = (f32[2048]{0:T(1024)S(1)}, f32[2048]{0:T(1024)}, u32[]{:S(2)}) copy-start(f32[2048]{0:T(1024)} %param.11) | copy-start | bytes 24580
  76.7 11.7 %collective-permute-start.6 = (bf16[96,2048]{1,0:T(8,128)(2,1)S(1)}, bf16[96,2048]{1,0:T(8,128)(2,1)S(1)}, u32[]{:S(2)}, u32[]{:S(2)}) collective-permute-start(bf16[96,2048]{1,0:T(8,128)(2,1)S(1)} %multiply_convert_fusion), channel_id=1, source_target_pairs={{0,64},{32,96},{64,0},{96,32},{1,65},{33,97},{65,1},{97,33},{2,66}... | collective-permute-start | bytes 1179656 | tf_op jit(solution)/shard_map/ppermute | solution.py:69
  140.3 45.0 %all-to-all-start = ((bf16[32,24,2048]{2,1,0:T(8,128)(2,1)}), bf16[32,24,2048]{2,1,0:T(8,128)(2,1)}, u32[]{:S(2)}, u32[]{:S(2)}) async-start(bf16[32,24,2048]{2,1,0:T(8,128)(2,1)} %get-tuple-element.7), calls=%async_computation | async-start | bytes 6291456 | tf_op jit(solution)/shard_map/all_to_all | solution.py:147
  145.1 41.5 %collective-permute-start.9 = (bf16[32,24,2048]{2,1,0:T(8,128)(2,1)}, bf16[32,24,2048]{2,1,0:T(8,128)(2,1)}, u32[]{:S(2)}, u32[]{:S(2)}) collective-permute-start(bf16[32,24,2048]{2,1,0:T(8,128)(2,1)} %all_to_all.20), channel_id=1, source_target_pairs={{0,96},{1,33},{2,98},{3,35},{4,100},{5,37},{6,102},{7,39},{8,104},... | collective-permute-start | bytes 9437192 | tf_op jit(solution)/shard_map/ppermute | solution.py:80
  185.3 6.8 %copy-start.9 = (bf16[2,352,2048]{2,1,0:T(8,128)(2,1)S(1)}, bf16[2,352,2048]{2,1,0:T(8,128)(2,1)}, u32[]{:S(2)}) copy-start(bf16[2,352,2048]{2,1,0:T(8,128)(2,1)} %param.15) | copy-start | bytes 8650756
  185.3 38.7 %collective-permute-start.7 = (bf16[32,24,2048]{2,1,0:T(8,128)(2,1)}, bf16[32,24,2048]{2,1,0:T(8,128)(2,1)S(1)}, u32[]{:S(2)}, u32[]{:S(2)}) collective-permute-start(bf16[32,24,2048]{2,1,0:T(8,128)(2,1)} %all-to-all-done), channel_id=1, source_target_pairs={{0,32},{1,97},{2,34},{3,99},{4,36},{5,101},{6,38},{7,103},{8,40},{... | collective-permute-start | bytes 9437192 | tf_op jit(solution)/shard_map/ppermute | solution.py:80
  192.1 41.5 %slice-start = ((s8[5767168]{0:T(1024)(128)(4,1)}), s8[4194304]{0:T(1024)(128)(4,1)S(1)}, s32[]{:S(2)}) async-start(s8[5767168]{0:T(1024)(128)(4,1)} %bitcast.146), calls=%async_computation.4 | async-start | bytes 8388608
  194.0 39.7 %slice-start.1 = ((s8[5767168]{0:T(1024)(128)(4,1)}), s8[1572864]{0:T(1024)(128)(4,1)S(1)}, s32[]{:S(2)}) async-start(s8[5767168]{0:T(1024)(128)(4,1)} %bitcast.146), calls=%async_computation.5 | async-start | bytes 3145728
  194.0 86.9 %collective-permute-start.10 = (bf16[32,24,2048]{2,1,0:T(8,128)(2,1)S(1)}, bf16[32,24,2048]{2,1,0:T(8,128)(2,1)S(1)}, u32[]{:S(2)}, u32[]{:S(2)}) collective-permute-start(bf16[32,24,2048]{2,1,0:T(8,128)(2,1)S(1)} %convolution_convert_fusion.1), channel_id=1, source_target_pairs={{0,32},{1,97},{2,34},{3,99},{4,36},{5,101},{6,38},{7,103},{8,40},{... | collective-permute-start | bytes 9437192 | tf_op jit(solution)/shard_map/ppermute | solution.py:80
  228.6 5.0 %copy-start.3 = (bf16[32,24,2048]{2,1,0:T(8,128)(2,1)S(1)}, bf16[32,24,2048]{2,1,0:T(8,128)(2,1)}, u32[]{:S(2)}) copy-start(bf16[32,24,2048]{2,1,0:T(8,128)(2,1)} %all_to_all.20) | copy-start | bytes 9437188
  232.1 63.2 %collective-permute-start.8 = (bf16[32,24,2048]{2,1,0:T(8,128)(2,1)}, bf16[32,24,2048]{2,1,0:T(8,128)(2,1)}, u32[]{:S(2)}, u32[]{:S(2)}) collective-permute-start(bf16[32,24,2048]{2,1,0:T(8,128)(2,1)} %convolution_convert_fusion.3), channel_id=1, source_target_pairs={{0,96},{1,33},{2,98},{3,35},{4,100},{5,37},{6,102},{7,39},{8,104},... | collective-permute-start | bytes 9437192 | tf_op jit(solution)/shard_map/ppermute | solution.py:80
  284.4 45.2 %all-to-all-start.3 = ((bf16[32,24,2048]{2,1,0:T(8,128)(2,1)}), bf16[32,24,2048]{2,1,0:T(8,128)(2,1)}, u32[]{:S(2)}, u32[]{:S(2)}) async-start(bf16[32,24,2048]{2,1,0:T(8,128)(2,1)} %add_convert_fusion), calls=%async_computation.3 | async-start | bytes 6291456 | tf_op jit(solution)/shard_map/all_to_all | solution.py:153
  289.8 5.6 %copy-start.10 = (bf16[2,352,2048]{2,1,0:T(8,128)(2,1)S(1)}, bf16[2,352,2048]{2,1,0:T(8,128)(2,1)}, u32[]{:S(2)}) copy-start(bf16[2,352,2048]{2,1,0:T(8,128)(2,1)} %param.15) | copy-start | bytes 8650756
  300.7 33.7 %copy-start.11 = (bf16[2048,64]{0,1:T(8,128)(2,1)S(1)}, bf16[2048,64]{0,1:T(8,128)(2,1)}, u32[]{:S(2)}) copy-start(bf16[2048,64]{0,1:T(8,128)(2,1)} %param.12) | copy-start | bytes 786436
  329.7 45.0 %all-to-all-start.1 = ((bf16[32,24,2048]{2,1,0:T(8,128)(2,1)}), bf16[32,24,2048]{2,1,0:T(8,128)(2,1)}, u32[]{:S(2)}, u32[]{:S(2)}) async-start(bf16[32,24,2048]{2,1,0:T(8,128)(2,1)} %add_convert_fusion.1), calls=%async_computation.1 | async-start | bytes 6291456 | tf_op jit(solution)/shard_map/all_to_all | solution.py:153
  336.1 38.6 %copy-start.4 = (f32[192,2,32,24]{0,3,2,1:T(8,128)}, f32[192,2,32,24]{0,3,2,1:T(8,128)S(1)}, u32[]{:S(2)}) copy-start(f32[192,2,32,24]{0,3,2,1:T(8,128)S(1)} %select_reduce_fusion) | copy-start | bytes 3538948
  378.3 18.8 %copy-start.1 = (bf16[512,2048]{1,0:T(8,128)(2,1)S(1)}, bf16[512,2048]{1,0:T(8,128)(2,1)}, u32[]{:S(2)}) copy-start(bf16[512,2048]{1,0:T(8,128)(2,1)} %param.10) | copy-start | bytes 6291460
  383.9 12.4 %collective-permute-start.11 = (bf16[96,2048]{1,0:T(8,128)(2,1)S(1)}, bf16[96,2048]{1,0:T(8,128)(2,1)S(1)}, u32[]{:S(2)}, u32[]{:S(2)}) collective-permute-start(bf16[96,2048]{1,0:T(8,128)(2,1)S(1)} %slice.227), channel_id=1, source_target_pairs={{0,64},{32,96},{64,0},{96,32},{1,65},{33,97},{65,1},{97,33},{2,66}... | collective-permute-start | bytes 1179656 | tf_op jit(solution)/shard_map/ppermute | solution.py:69

commit v6 on v5

--- a/solution.py
+++ b/solution.py
@@ -73,7 +73,7 @@
     pairs = []
     for s in range(seq_size):
         for e in range(exp_size):
-            step = 1 if (local + e) % 2 == 0 else -1
+            step = 1 if e % 2 == 0 else -1
             if back:
                 step = -step
             pairs.append((s * exp_size + e, ((s + step) % seq_size) * exp_size + e))

time: 398 us -> 380 us (0.955)
  waiting for transfers between devices: 248 us -> 228 us
    all_to_all x2, waiting for transfers between devices: 67.5 us -> 49.4 us  [on_device(): lax.all_to_all(pair_sum, 'exp', split_axis=0, concat_axis=0, tiled=True)]
where the time goes in v6:
time: 380 us
  waiting for transfers between devices  228 us (60%)
  matrix products  50.6 us (13%)
  blocking collectives  47.5 us (12%)
  starting transfers between devices  32.9 us (9%)
  local copies, waits for them, and re-layouts  15 us (4%)
  other arithmetic  5.43 us (1%)
    ppermute x4, waiting for transfers between devices, paired_shift(): return lax.ppermute(x, ('seq', 'exp'), pairs)  70.8 us
    ppermute x8, waiting for transfers between devices, seq_shift(): lax.ppermute(x, 'seq', [(i, (i + shift) % size) for i in range(size)])  68.9 us
    all_to_all x2, waiting for transfers between devices, on_device(): lax.all_to_all(pair_sum, 'exp', split_axis=0, concat_axis=0, tiled=True)  49.4 us
    all_to_all x1, blocking collectives, on_device(): lax.all_to_all(outgoing[local], 'exp', split_axis=0, concat_axis=0, tiled...  47.5 us
    all_to_all x1, waiting for transfers between devices, on_device(): lax.all_to_all(outgoing[local], 'exp', split_axis=0, concat_axis=0, tiled...  38.8 us
    dot_general x4, matrix products, expert_group(): jnp.einsum('gsd,dxf->gsxf', rows, gate_up, preferred_element_type=jnp.flo...  18.2 us
    dot_general x4, matrix products, expert_group(): jnp.einsum('gsf,fd->gsd', hidden, down, preferred_element_type=jnp.float32)  14.3 us
    all_to_all x2, starting transfers between devices, on_device(): lax.all_to_all(pair_sum, 'exp', split_axis=0, concat_axis=0, tiled=True)  9.9 us
  transfers between devices with their start and end apart: 15, of which 11 were waited for; matrix products, arithmetic and copies ran while one was open for 10% of the time, Pallas kernels for 0%

profile of v6, /device:TPU:0, one launch (start us, length us, event | category | flops | bytes accessed | tf_op | source)
XLA Modules:
  0.0 379.7 jit_solution(12041818938916316588)
XLA Ops:
  0.0 2.1 reshape_squeeze.15
  2.1 2.4 constant_dynamic-slice_fusion.3
  5.4 2.9 collective-permute-start.2
  9.0 0.8 collective-permute-start.1
  10.5 0.9 collective-permute-start
  12.3 8.9 %collective-permute-done.2 = bf16[96,3,512]{2,0,1:T(8,128)(2,1)S(1)} collective-permute-done((bf16[96,3,512]{2,0,1:T(8,128)(2,1)}, bf16[96,3,512]{2,0,1:T(8,128)(2,1)S(1)}, u32[]{:S(2)}, u32[]{:S(2)}) %collective-permute-start.2) | collective-permute-done | bytes 294944 | tf_op jit(solution)/shard_map/ppermute | solution.py:69
  21.1 4.3 %collective-permute-done = bf16[96,3,512]{2,0,1:T(8,128)(2,1)S(1)} collective-permute-done((bf16[96,3,512]{2,0,1:T(8,128)(2,1)}, bf16[96,3,512]{2,0,1:T(8,128)(2,1)S(1)}, u32[]{:S(2)}, u32[]{:S(2)}) %collective-permute-start) | collective-permute-done | bytes 294944 | tf_op jit(solution)/shard_map/ppermute | solution.py:69
  25.8 0.9 copy.58
  26.7 0.9 copy.59
  27.9 3.3 fusion.98
  31.1 2.1 convolution_convert_fusion.5
  33.3 1.0 fusion.99
  34.3 1.4 fusion.96
  36.4 2.1 collective-permute-start.4
  38.5 1.4 collective-permute-start.3
  40.8 33.3 %collective-permute-done.5 = f32[96,2048]{1,0:T(8,128)S(1)} collective-permute-done((f32[96,2048]{1,0:T(8,128)}, f32[96,2048]{1,0:T(8,128)S(1)}, u32[]{:S(2)}, u32[]{:S(2)}) %collective-permute-start.5) | collective-permute-done | bytes 786464 | tf_op jit(solution)/shard_map/ppermute | solution.py:69
  74.9 1.7 multiply_reduce_fusion.1
  76.7 1.1 collective-permute-start.6
  78.0 1.1 fusion.1
  79.1 9.4 %collective-permute-done.6 = bf16[96,2048]{1,0:T(8,128)(2,1)S(1)} collective-permute-done((bf16[96,2048]{1,0:T(8,128)(2,1)S(1)}, bf16[96,2048]{1,0:T(8,128)(2,1)S(1)}, u32[]{:S(2)}, u32[]{:S(2)}) %collective-permute-start.6) | collective-permute-done | bytes 393248 | tf_op jit(solution)/shard_map/ppermute | solution.py:69
  88.4 1.8 convolution_convert_fusion
  90.2 2.6 slice_bitcast_fusion.1
  92.8 47.5 %all_to_all.20 = bf16[32,24,2048]{2,1,0:T(8,128)(2,1)} all-to-all(bf16[32,24,2048]{2,1,0:T(8,128)(2,1)S(1)} %get-tuple-element.8), channel_id=1, replica_groups=mesh['seq'=4,'exp'=32] {'exp'}, dimensions={0} | all-to-all | bytes 6291456 | tf_op jit(solution)/shard_map/all_to_all | solution.py:147
  140.3 4.8 %all-to-all-start = ((bf16[32,24,2048]{2,1,0:T(8,128)(2,1)}), bf16[32,24,2048]{2,1,0:T(8,128)(2,1)}, u32[]{:S(2)}, u32[]{:S(2)}) async-start(bf16[32,24,2048]{2,1,0:T(8,128)(2,1)} %get-tuple-element.7), calls=%async_computation | async-start | bytes 6291456 | tf_op jit(solution)/shard_map/all_to_all | solution.py:147
  145.1 1.4 collective-permute-start.9
  146.5 38.8 %all-to-all-done = bf16[32,24,2048]{2,1,0:T(8,128)(2,1)} async-done(((bf16[32,24,2048]{2,1,0:T(8,128)(2,1)}), bf16[32,24,2048]{2,1,0:T(8,128)(2,1)}, u32[]{:S(2)}, u32[]{:S(2)}) %all-to-all-start) | async-done | bytes 3145760 | tf_op jit(solution)/shard_map/all_to_all | solution.py:147
  185.3 1.3 collective-permute-start.7
  186.7 5.4 %fusion.4 = f32[32,24,2,352]{3,1,2,0:T(8,128)S(1)} fusion(bf16[32,24,2048]{2,1,0:T(8,128)(2,1)} %collective-permute-done.9, bf16[2,2048,2,352]{1,3,2,0:T(8,128)(2,1)} %param.14), kind=kOutput, calls=%fused_computation.17 | convolution fusion | flops 2214592512 | bytes 8192000 | tf_op jit(solution)/shard_map/gsd,dxf->gsxf/dot_general | solution.py:40
  192.1 1.9 convolution_convert_fusion.1
  194.0 2.5 collective-permute-start.10
  196.4 52.6 %collective-permute-done.7 = bf16[32,24,2048]{2,1,0:T(8,128)(2,1)S(1)} collective-permute-done((bf16[32,24,2048]{2,1,0:T(8,128)(2,1)}, bf16[32,24,2048]{2,1,0:T(8,128)(2,1)S(1)}, u32[]{:S(2)}, u32[]{:S(2)}) %collective-permute-start.7) | collective-permute-done | bytes 3145760 | tf_op jit(solution)/shard_map/ppermute | solution.py:80
  249.0 4.6 %fusion.8 = f32[32,24,2,352]{3,1,2,0:T(8,128)S(1)} fusion(bf16[32,24,2048]{2,1,0:T(8,128)(2,1)S(1)} %collective-permute-done.7, bf16[2,2048,2,352]{1,3,2,0:T(8,128)(2,1)} %param.14), kind=kOutput, calls=%fused_computation.21 | convolution fusion | flops 2214592512 | bytes 8192000 | tf_op jit(solution)/shard_map/gsd,dxf->gsxf/dot_general | solution.py:40
  253.6 3.5 convolution_convert_fusion.3
  257.1 3.8 collective-permute-start.8
  260.9 2.7 fusion.6
  263.6 3.5 add_convert_fusion
  267.2 5.1 %all-to-all-start.3 = ((bf16[32,24,2048]{2,1,0:T(8,128)(2,1)}), bf16[32,24,2048]{2,1,0:T(8,128)(2,1)}, u32[]{:S(2)}, u32[]{:S(2)}) async-start(bf16[32,24,2048]{2,1,0:T(8,128)(2,1)} %add_convert_fusion), calls=%async_computation.3 | async-start | bytes 6291456 | tf_op jit(solution)/shard_map/all_to_all | solution.py:153
  272.3 5.5 %fusion.10 = f32[32,24,2,352]{3,1,2,0:T(8,128)S(1)} fusion(bf16[32,24,2048]{2,1,0:T(8,128)(2,1)} %all-to-all-done, bf16[2,2048,2,352]{1,3,2,0:T(8,128)(2,1)} %param.14), kind=kOutput, calls=%fused_computation.23 | convolution fusion | flops 2214592512 | bytes 8192000 | tf_op jit(solution)/shard_map/gsd,dxf->gsxf/dot_general | solution.py:40
  277.9 18.2 %collective-permute-done.8 = bf16[32,24,2048]{2,1,0:T(8,128)(2,1)} collective-permute-done((bf16[32,24,2048]{2,1,0:T(8,128)(2,1)}, bf16[32,24,2048]{2,1,0:T(8,128)(2,1)}, u32[]{:S(2)}, u32[]{:S(2)}) %collective-permute-start.8) | collective-permute-done | bytes 3145760 | tf_op jit(solution)/shard_map/ppermute | solution.py:80
  296.0 5.4 %add_convert_fusion.1 = bf16[32,24,2048]{2,1,0:T(8,128)(2,1)} fusion(bf16[32,24,2048]{2,1,0:T(8,128)(2,1)} %collective-permute-done.8, bf16[2,352,2048]{2,1,0:T(8,128)(2,1)S(1)} %copy-done.10, f32[32,24,2,352]{3,1,2,0:T(8,128)S(1)} %fusion.10), kind=kOutput, calls=%fused_computation.6 | convolution fusion | flops 1116782592 | bytes 10092544 | tf_op jit(solution)/shard_map/gsf,fd->gsd/dot_general | solution.py:42
  301.4 10.8 %all-to-all-done.3 = bf16[32,24,2048]{2,1,0:T(8,128)(2,1)} async-done(((bf16[32,24,2048]{2,1,0:T(8,128)(2,1)}), bf16[32,24,2048]{2,1,0:T(8,128)(2,1)}, u32[]{:S(2)}, u32[]{:S(2)}) %all-to-all-start.3) | async-done | bytes 3145760 | tf_op jit(solution)/shard_map/all_to_all | solution.py:153
  312.2 4.8 %all-to-all-start.1 = ((bf16[32,24,2048]{2,1,0:T(8,128)(2,1)}), bf16[32,24,2048]{2,1,0:T(8,128)(2,1)}, u32[]{:S(2)}, u32[]{:S(2)}) async-start(bf16[32,24,2048]{2,1,0:T(8,128)(2,1)} %add_convert_fusion.1), calls=%async_computation.1 | async-start | bytes 6291456 | tf_op jit(solution)/shard_map/all_to_all | solution.py:153
  317.5 1.1 select_reduce_fusion
  318.6 38.6 %all-to-all-done.1 = bf16[32,24,2048]{2,1,0:T(8,128)(2,1)} async-done(((bf16[32,24,2048]{2,1,0:T(8,128)(2,1)}), bf16[32,24,2048]{2,1,0:T(8,128)(2,1)}, u32[]{:S(2)}, u32[]{:S(2)}) %all-to-all-start.1) | async-done | bytes 3145760 | tf_op jit(solution)/shard_map/all_to_all | solution.py:153
  357.2 3.7 fusion.16
  360.9 5.5 %fusion.22 = f32[192,2048]{1,0:T(8,128)S(1)} fusion(f32[192,2048]{1,0:T(8,128)S(1)} %fusion.16, bf16[1,32,24,2048]{3,2,1,0:T(8,128)(2,1)} %bitcast.44, bf16[1,32,24,2048]{3,2,1,0:T(8,128)(2,1)} %bitcast.32, f32[192,2,32,24]{0,3,2,1:T(8,128)} %copy-done.4), kind=kOutput, calls=%fused_computation.35 | convolution fusion | flops 1212678144 | bytes 10616832 | tf_op jit(solution)/shard_map/pcgs,cgsd->pd/dot_general | solution.py:167
  366.5 12.3 %collective-permute-done.11 = bf16[96,2048]{1,0:T(8,128)(2,1)S(1)} collective-permute-done((bf16[96,2048]{1,0:T(8,128)(2,1)S(1)}, bf16[96,2048]{1,0:T(8,128)(2,1)S(1)}, u32[]{:S(2)}, u32[]{:S(2)}) %collective-permute-start.11) | collective-permute-done | bytes 393248 | tf_op jit(solution)/shard_map/ppermute | solution.py:69
  378.9 0.9 fusion.66
  (70 shorter events, 6.9 us)
Async XLA Ops:
  0.0 33.2 %copy-start = (bf16[512,2048]{1,0:T(8,128)(2,1)S(1)}, bf16[512,2048]{1,0:T(8,128)(2,1)}, u32[]{:S(2)}) copy-start(bf16[512,2048]{1,0:T(8,128)(2,1)} %param.10) | copy-start | bytes 6291460
  4.6 6.9 %copy-start.7 = (s32[1,384,6]{1,0,2:T(1,128)S(1)}, s32[1,384,6]{1,0,2:T(1,128)}, u32[]{:S(2)}) copy-start(s32[1,384,6]{1,0,2:T(1,128)} %param.13) | copy-start | bytes 27652
  5.4 15.8 %collective-permute-start.2 = (bf16[96,3,512]{2,0,1:T(8,128)(2,1)}, bf16[96,3,512]{2,0,1:T(8,128)(2,1)S(1)}, u32[]{:S(2)}, u32[]{:S(2)}) collective-permute-start(bf16[96,3,512]{2,0,1:T(8,128)(2,1)} %bitcast.133), channel_id=1, source_target_pairs={{0,96},{32,0},{64,32},{96,64},{1,97},{33,1},{65,33},{97,65},{2,98}... | collective-permute-start | bytes 884744 | tf_op jit(solution)/shard_map/ppermute | solution.py:69
  9.0 12.2 %collective-permute-start.1 = (bf16[96,3,512]{2,0,1:T(8,128)(2,1)}, bf16[96,3,512]{2,0,1:T(8,128)(2,1)S(1)}, u32[]{:S(2)}, u32[]{:S(2)}) collective-permute-start(bf16[96,3,512]{2,0,1:T(8,128)(2,1)} %bitcast.134), channel_id=1, source_target_pairs={{0,64},{32,96},{64,0},{96,32},{1,65},{33,97},{65,1},{97,33},{2,66}... | collective-permute-start | bytes 884744 | tf_op jit(solution)/shard_map/ppermute | solution.py:69
  10.5 15.0 %collective-permute-start = (bf16[96,3,512]{2,0,1:T(8,128)(2,1)}, bf16[96,3,512]{2,0,1:T(8,128)(2,1)S(1)}, u32[]{:S(2)}, u32[]{:S(2)}) collective-permute-start(bf16[96,3,512]{2,0,1:T(8,128)(2,1)} %bitcast.135), channel_id=1, source_target_pairs={{0,32},{32,64},{64,96},{96,0},{1,33},{33,65},{65,97},{97,1},{2,34}... | collective-permute-start | bytes 884744 | tf_op jit(solution)/shard_map/ppermute | solution.py:69
  26.7 4.4 %copy-start.6 = (bf16[384,1,512]{0,2,1:T(8,128)(2,1)S(1)}, bf16[384,1,512]{0,2,1:T(8,128)(2,1)}, u32[]{:S(2)}) copy-start(bf16[384,1,512]{0,2,1:T(8,128)(2,1)} %copy.58) | copy-start | bytes 1179652
  34.3 2.1 copy-start.2
  34.3 40.6 %copy-start.5 = (bf16[1,96,2048]{2,1,0:T(8,128)(2,1)S(1)}, bf16[1,96,2048]{2,1,0:T(8,128)(2,1)}, u32[]{:S(2)}) copy-start(bf16[1,96,2048]{2,1,0:T(8,128)(2,1)} %param.8) | copy-start | bytes 1179652
  36.4 37.7 %collective-permute-start.5 = (f32[96,2048]{1,0:T(8,128)}, f32[96,2048]{1,0:T(8,128)S(1)}, u32[]{:S(2)}, u32[]{:S(2)}) collective-permute-start(f32[96,2048]{1,0:T(8,128)} %get-tuple-element.10), channel_id=1, source_target_pairs={{0,32},{32,64},{64,96},{96,0},{1,33},{33,65},{65,97},{97,1},{2,34}... | collective-permute-start | bytes 2359304 | tf_op jit(solution)/shard_map/ppermute | solution.py:69
  36.4 37.7 %collective-permute-start.4 = (f32[96,2048]{1,0:T(8,128)}, f32[96,2048]{1,0:T(8,128)S(1)}, u32[]{:S(2)}, u32[]{:S(2)}) collective-permute-start(f32[96,2048]{1,0:T(8,128)} %get-tuple-element.11), channel_id=1, source_target_pairs={{0,64},{32,96},{64,0},{96,32},{1,65},{33,97},{65,1},{97,33},{2,66}... | collective-permute-start | bytes 2359304 | tf_op jit(solution)/shard_map/ppermute | solution.py:69
  38.5 36.4 %collective-permute-start.3 = (f32[96,2048]{1,0:T(8,128)S(1)}, f32[96,2048]{1,0:T(8,128)}, u32[]{:S(2)}, u32[]{:S(2)}) collective-permute-start(f32[96,2048]{1,0:T(8,128)S(1)} %get-tuple-element.9), channel_id=1, source_target_pairs={{0,96},{32,0},{64,32},{96,64},{1,97},{33,1},{65,33},{97,65},{2,98}... | collective-permute-start | bytes 2359304 | tf_op jit(solution)/shard_map/ppermute | solution.py:69
  40.6 36.0 %copy-start.8 = (f32[2048]{0:T(1024)S(1)}, f32[2048]{0:T(1024)}, u32[]{:S(2)}) copy-start(f32[2048]{0:T(1024)} %param.11) | copy-start | bytes 24580
  76.7 11.7 %collective-permute-start.6 = (bf16[96,2048]{1,0:T(8,128)(2,1)S(1)}, bf16[96,2048]{1,0:T(8,128)(2,1)S(1)}, u32[]{:S(2)}, u32[]{:S(2)}) collective-permute-start(bf16[96,2048]{1,0:T(8,128)(2,1)S(1)} %multiply_convert_fusion), channel_id=1, source_target_pairs={{0,64},{32,96},{64,0},{96,32},{1,65},{33,97},{65,1},{97,33},{2,66}... | collective-permute-start | bytes 1179656 | tf_op jit(solution)/shard_map/ppermute | solution.py:69
  140.3 45.0 %all-to-all-start = ((bf16[32,24,2048]{2,1,0:T(8,128)(2,1)}), bf16[32,24,2048]{2,1,0:T(8,128)(2,1)}, u32[]{:S(2)}, u32[]{:S(2)}) async-start(bf16[32,24,2048]{2,1,0:T(8,128)(2,1)} %get-tuple-element.7), calls=%async_computation | async-start | bytes 6291456 | tf_op jit(solution)/shard_map/all_to_all | solution.py:147
  145.1 41.5 %collective-permute-start.9 = (bf16[32,24,2048]{2,1,0:T(8,128)(2,1)}, bf16[32,24,2048]{2,1,0:T(8,128)(2,1)}, u32[]{:S(2)}, u32[]{:S(2)}) collective-permute-start(bf16[32,24,2048]{2,1,0:T(8,128)(2,1)} %all_to_all.20), channel_id=1, source_target_pairs={{0,32},{1,97},{2,34},{3,99},{4,36},{5,101},{6,38},{7,103},{8,40},{... | collective-permute-start | bytes 9437192 | tf_op jit(solution)/shard_map/ppermute | solution.py:80
  185.3 6.8 %copy-start.9 = (bf16[2,352,2048]{2,1,0:T(8,128)(2,1)S(1)}, bf16[2,352,2048]{2,1,0:T(8,128)(2,1)}, u32[]{:S(2)}) copy-start(bf16[2,352,2048]{2,1,0:T(8,128)(2,1)} %param.15) | copy-start | bytes 8650756
  185.3 63.7 %collective-permute-start.7 = (bf16[32,24,2048]{2,1,0:T(8,128)(2,1)}, bf16[32,24,2048]{2,1,0:T(8,128)(2,1)S(1)}, u32[]{:S(2)}, u32[]{:S(2)}) collective-permute-start(bf16[32,24,2048]{2,1,0:T(8,128)(2,1)} %all-to-all-done), channel_id=1, source_target_pairs={{0,32},{1,97},{2,34},{3,99},{4,36},{5,101},{6,38},{7,103},{8,40},{... | collective-permute-start | bytes 9437192 | tf_op jit(solution)/shard_map/ppermute | solution.py:80
  192.1 68.8 %slice-start = ((s8[5767168]{0:T(1024)(128)(4,1)}), s8[4194304]{0:T(1024)(128)(4,1)S(1)}, s32[]{:S(2)}) async-start(s8[5767168]{0:T(1024)(128)(4,1)} %bitcast.146), calls=%async_computation.4 | async-start | bytes 8388608
  194.0 67.0 %slice-start.1 = ((s8[5767168]{0:T(1024)(128)(4,1)}), s8[1572864]{0:T(1024)(128)(4,1)S(1)}, s32[]{:S(2)}) async-start(s8[5767168]{0:T(1024)(128)(4,1)} %bitcast.146), calls=%async_computation.5 | async-start | bytes 3145728
  194.0 69.7 %collective-permute-start.10 = (bf16[32,24,2048]{2,1,0:T(8,128)(2,1)S(1)}, bf16[32,24,2048]{2,1,0:T(8,128)(2,1)S(1)}, u32[]{:S(2)}, u32[]{:S(2)}) collective-permute-start(bf16[32,24,2048]{2,1,0:T(8,128)(2,1)S(1)} %convolution_convert_fusion.1), channel_id=1, source_target_pairs={{0,96},{1,33},{2,98},{3,35},{4,100},{5,37},{6,102},{7,39},{8,104},... | collective-permute-start | bytes 9437192 | tf_op jit(solution)/shard_map/ppermute | solution.py:80
  253.6 7.3 %copy-start.3 = (bf16[32,24,2048]{2,1,0:T(8,128)(2,1)S(1)}, bf16[32,24,2048]{2,1,0:T(8,128)(2,1)}, u32[]{:S(2)}) copy-start(bf16[32,24,2048]{2,1,0:T(8,128)(2,1)} %all_to_all.20) | copy-start | bytes 9437188
  257.1 38.9 %collective-permute-start.8 = (bf16[32,24,2048]{2,1,0:T(8,128)(2,1)}, bf16[32,24,2048]{2,1,0:T(8,128)(2,1)}, u32[]{:S(2)}, u32[]{:S(2)}) collective-permute-start(bf16[32,24,2048]{2,1,0:T(8,128)(2,1)} %convolution_convert_fusion.3), channel_id=1, source_target_pairs={{0,96},{1,33},{2,98},{3,35},{4,100},{5,37},{6,102},{7,39},{8,104},... | collective-permute-start | bytes 9437192 | tf_op jit(solution)/shard_map/ppermute | solution.py:80
  267.2 45.0 %all-to-all-start.3 = ((bf16[32,24,2048]{2,1,0:T(8,128)(2,1)}), bf16[32,24,2048]{2,1,0:T(8,128)(2,1)}, u32[]{:S(2)}, u32[]{:S(2)}) async-start(bf16[32,24,2048]{2,1,0:T(8,128)(2,1)} %add_convert_fusion), calls=%async_computation.3 | async-start | bytes 6291456 | tf_op jit(solution)/shard_map/all_to_all | solution.py:153
  272.3 23.7 %copy-start.10 = (bf16[2,352,2048]{2,1,0:T(8,128)(2,1)S(1)}, bf16[2,352,2048]{2,1,0:T(8,128)(2,1)}, u32[]{:S(2)}) copy-start(bf16[2,352,2048]{2,1,0:T(8,128)(2,1)} %param.15) | copy-start | bytes 8650756
  301.4 15.6 %copy-start.11 = (bf16[2048,64]{0,1:T(8,128)(2,1)S(1)}, bf16[2048,64]{0,1:T(8,128)(2,1)}, u32[]{:S(2)}) copy-start(bf16[2048,64]{0,1:T(8,128)(2,1)} %param.12) | copy-start | bytes 786436
  312.2 45.0 %all-to-all-start.1 = ((bf16[32,24,2048]{2,1,0:T(8,128)(2,1)}), bf16[32,24,2048]{2,1,0:T(8,128)(2,1)}, u32[]{:S(2)}, u32[]{:S(2)}) async-start(bf16[32,24,2048]{2,1,0:T(8,128)(2,1)} %add_convert_fusion.1), calls=%async_computation.1 | async-start | bytes 6291456 | tf_op jit(solution)/shard_map/all_to_all | solution.py:153
  318.6 38.6 %copy-start.4 = (f32[192,2,32,24]{0,3,2,1:T(8,128)}, f32[192,2,32,24]{0,3,2,1:T(8,128)S(1)}, u32[]{:S(2)}) copy-start(f32[192,2,32,24]{0,3,2,1:T(8,128)S(1)} %select_reduce_fusion) | copy-start | bytes 3538948
  360.9 18.8 %copy-start.1 = (bf16[512,2048]{1,0:T(8,128)(2,1)S(1)}, bf16[512,2048]{1,0:T(8,128)(2,1)}, u32[]{:S(2)}) copy-start(bf16[512,2048]{1,0:T(8,128)(2,1)} %param.10) | copy-start | bytes 6291460
  366.4 12.4 %collective-permute-start.11 = (bf16[96,2048]{1,0:T(8,128)(2,1)S(1)}, bf16[96,2048]{1,0:T(8,128)(2,1)S(1)}, u32[]{:S(2)}, u32[]{:S(2)}) collective-permute-start(bf16[96,2048]{1,0:T(8,128)(2,1)S(1)} %slice.227), channel_id=1, source_target_pairs={{0,64},{32,96},{64,0},{96,32},{1,65},{33,97},{65,1},{97,33},{2,66}... | collective-permute-start | bytes 1179656 | tf_op jit(solution)/shard_map/ppermute | solution.py:69

commit v7 on v6

--- a/solution.py
+++ b/solution.py
@@ -111,7 +111,9 @@
     )
     projected = partial[0]
     for shift in range(1, seq_size):
-        projected = projected + seq_shift(partial[shift], -shift, seq_size)
+        projected = projected + seq_shift(
+            partial[shift].astype(jnp.bfloat16), -shift, seq_size
+        ).astype(jnp.float32)
     mixed = resid[0].astype(jnp.float32) + projected
     meansq = jnp.mean(mixed * mixed, axis=-1, keepdims=True)
     normed = (mixed * lax.rsqrt(meansq + epsilon) * norm_gain).astype(jnp.bfloat16)

time: 380 us -> 364 us (0.958)
  waiting for transfers between devices: 228 us -> 210 us
    ppermute x8, waiting for transfers between devices: 68.9 us -> 51.8 us  [seq_shift(): lax.ppermute(x, 'seq', [(i, (i + shift) % size) for i in range(size)])]
  transfers between devices with their start and end apart: 15 -> 15, of which waited for: 11 -> 11; matrix products, arithmetic and copies ran while one was open for 10% -> 11% of each run, Pallas kernels for 0% -> 0%
where the time goes in v7:
time: 364 us; the launch traced here: 363 us
  waiting for transfers between devices  210 us (58%)
  matrix products  52.3 us (14%)
  blocking collectives  47.5 us (13%)
  starting transfers between devices  33.7 us (9%)
  local copies, waits for them, and re-layouts  13.7 us (4%)
  other arithmetic  5.38 us (1%)
    ppermute x4, waiting for transfers between devices, paired_shift(): return lax.ppermute(x, ('seq', 'exp'), pairs)  70.5 us
    ppermute x8, waiting for transfers between devices, seq_shift(): lax.ppermute(x, 'seq', [(i, (i + shift) % size) for i in range(size)])  51.8 us
    all_to_all x2, waiting for transfers between devices, on_device(): lax.all_to_all(pair_sum, 'exp', split_axis=0, concat_axis=0, tiled=True)  49.4 us
    all_to_all x1, blocking collectives, on_device(): lax.all_to_all(outgoing[local], 'exp', split_axis=0, concat_axis=0, tiled...  47.5 us
    all_to_all x1, waiting for transfers between devices, on_device(): lax.all_to_all(outgoing[local], 'exp', split_axis=0, concat_axis=0, tiled...  38.8 us
    dot_general x4, matrix products, expert_group(): jnp.einsum('gsd,dxf->gsxf', rows, gate_up, preferred_element_type=jnp.flo...  18.2 us
    dot_general x4, matrix products, expert_group(): jnp.einsum('gsf,fd->gsd', hidden, down, preferred_element_type=jnp.float32)  14.3 us
    all_to_all x2, starting transfers between devices, on_device(): lax.all_to_all(pair_sum, 'exp', split_axis=0, concat_axis=0, tiled=True)  9.9 us
  transfers between devices with their start and end apart: 15, of which 11 were waited for; matrix products, arithmetic and copies ran while one was open for 11% of the time, Pallas kernels for 0%

profile of v7, /device:TPU:0, one launch (start us, length us, event | category | flops | bytes accessed | tf_op | source)
XLA Modules:
  0.0 363.4 jit_solution(15103283775449148886)
XLA Ops:
  0.0 2.1 reshape_squeeze.15
  2.1 2.4 constant_dynamic-slice_fusion.3
  4.6 0.8 copy.89
  5.4 2.9 collective-permute-start.2
  9.0 0.8 collective-permute-start.1
  10.5 0.9 collective-permute-start
  12.6 8.5 %collective-permute-done.2 = bf16[96,3,512]{2,0,1:T(8,128)(2,1)S(1)} collective-permute-done((bf16[96,3,512]{2,0,1:T(8,128)(2,1)}, bf16[96,3,512]{2,0,1:T(8,128)(2,1)S(1)}, u32[]{:S(2)}, u32[]{:S(2)}) %collective-permute-start.2) | collective-permute-done | bytes 294944 | tf_op jit(solution)/shard_map/ppermute | solution.py:69
  21.1 4.3 %collective-permute-done = bf16[96,3,512]{2,0,1:T(8,128)(2,1)S(1)} collective-permute-done((bf16[96,3,512]{2,0,1:T(8,128)(2,1)}, bf16[96,3,512]{2,0,1:T(8,128)(2,1)S(1)}, u32[]{:S(2)}, u32[]{:S(2)}) %collective-permute-start) | collective-permute-done | bytes 294944 | tf_op jit(solution)/shard_map/ppermute | solution.py:69
  25.8 0.9 copy.58
  26.7 0.9 copy.59
  27.9 3.3 fusion.98
  31.1 2.1 convolution_convert_fusion.5
  33.2 2.7 fusion.99
  36.1 2.1 collective-permute-start.4
  38.2 1.4 collective-permute-start.3
  40.2 16.6 %collective-permute-done.5 = bf16[96,2048]{1,0:T(8,128)(2,1)S(1)} collective-permute-done((bf16[96,2048]{1,0:T(8,128)(2,1)S(1)}, bf16[96,2048]{1,0:T(8,128)(2,1)S(1)}, u32[]{:S(2)}, u32[]{:S(2)}) %collective-permute-start.5) | collective-permute-done | bytes 393248 | tf_op jit(solution)/shard_map/ppermute | solution.py:69
  58.2 1.6 multiply_reduce_fusion.1
  59.9 1.1 collective-permute-start.6
  61.2 1.1 fusion.1
  62.3 9.3 %collective-permute-done.6 = bf16[96,2048]{1,0:T(8,128)(2,1)S(1)} collective-permute-done((bf16[96,2048]{1,0:T(8,128)(2,1)S(1)}, bf16[96,2048]{1,0:T(8,128)(2,1)S(1)}, u32[]{:S(2)}, u32[]{:S(2)}) %collective-permute-start.6) | collective-permute-done | bytes 393248 | tf_op jit(solution)/shard_map/ppermute | solution.py:69
  71.7 1.8 convolution_convert_fusion
  73.5 2.6 slice_bitcast_fusion.1
  76.0 47.5 %all_to_all.20 = bf16[32,24,2048]{2,1,0:T(8,128)(2,1)} all-to-all(bf16[32,24,2048]{2,1,0:T(8,128)(2,1)S(1)} %get-tuple-element.8), channel_id=1, replica_groups=mesh['seq'=4,'exp'=32] {'exp'}, dimensions={0} | all-to-all | bytes 6291456 | tf_op jit(solution)/shard_map/all_to_all | solution.py:149
  123.5 4.8 %all-to-all-start = ((bf16[32,24,2048]{2,1,0:T(8,128)(2,1)}), bf16[32,24,2048]{2,1,0:T(8,128)(2,1)}, u32[]{:S(2)}, u32[]{:S(2)}) async-start(bf16[32,24,2048]{2,1,0:T(8,128)(2,1)} %get-tuple-element.7), calls=%async_computation | async-start | bytes 6291456 | tf_op jit(solution)/shard_map/all_to_all | solution.py:149
  128.4 1.4 collective-permute-start.9
  129.7 38.8 %all-to-all-done = bf16[32,24,2048]{2,1,0:T(8,128)(2,1)} async-done(((bf16[32,24,2048]{2,1,0:T(8,128)(2,1)}), bf16[32,24,2048]{2,1,0:T(8,128)(2,1)}, u32[]{:S(2)}, u32[]{:S(2)}) %all-to-all-start) | async-done | bytes 3145760 | tf_op jit(solution)/shard_map/all_to_all | solution.py:149
  168.6 1.3 collective-permute-start.7
  169.9 5.4 %fusion.4 = f32[32,24,2,352]{3,1,2,0:T(8,128)S(1)} fusion(bf16[32,24,2048]{2,1,0:T(8,128)(2,1)} %collective-permute-done.9, bf16[2,2048,2,352]{1,3,2,0:T(8,128)(2,1)} %param.14), kind=kOutput, calls=%fused_computation.17 | convolution fusion | flops 2214592512 | bytes 8192000 | tf_op jit(solution)/shard_map/gsd,dxf->gsxf/dot_general | solution.py:40
  175.3 1.9 convolution_convert_fusion.1
  177.2 2.4 collective-permute-start.10
  179.6 52.3 %collective-permute-done.7 = bf16[32,24,2048]{2,1,0:T(8,128)(2,1)S(1)} collective-permute-done((bf16[32,24,2048]{2,1,0:T(8,128)(2,1)}, bf16[32,24,2048]{2,1,0:T(8,128)(2,1)S(1)}, u32[]{:S(2)}, u32[]{:S(2)}) %collective-permute-start.7) | collective-permute-done | bytes 3145760 | tf_op jit(solution)/shard_map/ppermute | solution.py:80
  231.8 4.6 %fusion.8 = f32[32,24,2,352]{3,1,2,0:T(8,128)S(1)} fusion(bf16[32,24,2048]{2,1,0:T(8,128)(2,1)S(1)} %collective-permute-done.7, bf16[2,2048,2,352]{1,3,2,0:T(8,128)(2,1)} %param.14), kind=kOutput, calls=%fused_computation.21 | convolution fusion | flops 2214592512 | bytes 8192000 | tf_op jit(solution)/shard_map/gsd,dxf->gsxf/dot_general | solution.py:40
  236.4 3.5 convolution_convert_fusion.3
  240.0 4.6 %collective-permute-start.8 = (bf16[32,24,2048]{2,1,0:T(8,128)(2,1)}, bf16[32,24,2048]{2,1,0:T(8,128)(2,1)}, u32[]{:S(2)}, u32[]{:S(2)}) collective-permute-start(bf16[32,24,2048]{2,1,0:T(8,128)(2,1)} %convolution_convert_fusion.3), channel_id=1, source_target_pairs={{0,96},{1,33},{2,98},{3,35},{4,100},{5,37},{6,102},{7,39},{8,104},... | collective-permute-start | bytes 9437192 | tf_op jit(solution)/shard_map/ppermute | solution.py:80
  244.6 2.7 fusion.6
  247.3 3.5 add_convert_fusion
  250.9 5.1 %all-to-all-start.3 = ((bf16[32,24,2048]{2,1,0:T(8,128)(2,1)}), bf16[32,24,2048]{2,1,0:T(8,128)(2,1)}, u32[]{:S(2)}, u32[]{:S(2)}) async-start(bf16[32,24,2048]{2,1,0:T(8,128)(2,1)} %add_convert_fusion), calls=%async_computation.3 | async-start | bytes 6291456 | tf_op jit(solution)/shard_map/all_to_all | solution.py:155
  256.0 5.6 %fusion.10 = f32[32,24,2,352]{3,1,2,0:T(8,128)S(1)} fusion(bf16[32,24,2048]{2,1,0:T(8,128)(2,1)} %all-to-all-done, bf16[2,2048,2,352]{1,3,2,0:T(8,128)(2,1)} %param.14), kind=kOutput, calls=%fused_computation.23 | convolution fusion | flops 2214592512 | bytes 8192000 | tf_op jit(solution)/shard_map/gsd,dxf->gsxf/dot_general | solution.py:40
  261.5 18.2 %collective-permute-done.8 = bf16[32,24,2048]{2,1,0:T(8,128)(2,1)} collective-permute-done((bf16[32,24,2048]{2,1,0:T(8,128)(2,1)}, bf16[32,24,2048]{2,1,0:T(8,128)(2,1)}, u32[]{:S(2)}, u32[]{:S(2)}) %collective-permute-start.8) | collective-permute-done | bytes 3145760 | tf_op jit(solution)/shard_map/ppermute | solution.py:80
  279.7 5.4 %add_convert_fusion.1 = bf16[32,24,2048]{2,1,0:T(8,128)(2,1)} fusion(bf16[32,24,2048]{2,1,0:T(8,128)(2,1)} %collective-permute-done.8, bf16[2,352,2048]{2,1,0:T(8,128)(2,1)S(1)} %copy-done.10, f32[32,24,2,352]{3,1,2,0:T(8,128)S(1)} %fusion.10), kind=kOutput, calls=%fused_computation.6 | convolution fusion | flops 1116782592 | bytes 10092544 | tf_op jit(solution)/shard_map/gsf,fd->gsd/dot_general | solution.py:42
  285.1 10.8 %all-to-all-done.3 = bf16[32,24,2048]{2,1,0:T(8,128)(2,1)} async-done(((bf16[32,24,2048]{2,1,0:T(8,128)(2,1)}), bf16[32,24,2048]{2,1,0:T(8,128)(2,1)}, u32[]{:S(2)}, u32[]{:S(2)}) %all-to-all-start.3) | async-done | bytes 3145760 | tf_op jit(solution)/shard_map/all_to_all | solution.py:155
  295.9 4.8 %all-to-all-start.1 = ((bf16[32,24,2048]{2,1,0:T(8,128)(2,1)}), bf16[32,24,2048]{2,1,0:T(8,128)(2,1)}, u32[]{:S(2)}, u32[]{:S(2)}) async-start(bf16[32,24,2048]{2,1,0:T(8,128)(2,1)} %add_convert_fusion.1), calls=%async_computation.1 | async-start | bytes 6291456 | tf_op jit(solution)/shard_map/all_to_all | solution.py:155
  301.2 1.1 select_reduce_fusion
  302.3 38.6 %all-to-all-done.1 = bf16[32,24,2048]{2,1,0:T(8,128)(2,1)} async-done(((bf16[32,24,2048]{2,1,0:T(8,128)(2,1)}), bf16[32,24,2048]{2,1,0:T(8,128)(2,1)}, u32[]{:S(2)}, u32[]{:S(2)}) %all-to-all-start.1) | async-done | bytes 3145760 | tf_op jit(solution)/shard_map/all_to_all | solution.py:155
  340.9 3.7 %fusion.16 = f32[192,2048]{1,0:T(8,128)S(1)} fusion(bf16[1,32,24,2048]{3,2,1,0:T(8,128)(2,1)} %bitcast.44, bf16[1,32,24,2048]{3,2,1,0:T(8,128)(2,1)} %bitcast.32, f32[192,2,32,24]{0,3,2,1:T(8,128)S(1)} %select_reduce_fusion), kind=kOutput, calls=%fused_computation.29 | convolution fusion | flops 1211400192 | bytes 9043968 | tf_op jit(solution)/shard_map/pcgs,cgsd->pd/dot_general | solution.py:167
  344.6 5.5 %fusion.22 = f32[192,2048]{1,0:T(8,128)S(1)} fusion(f32[192,2048]{1,0:T(8,128)S(1)} %fusion.16, bf16[1,32,24,2048]{3,2,1,0:T(8,128)(2,1)} %bitcast.44, bf16[1,32,24,2048]{3,2,1,0:T(8,128)(2,1)} %bitcast.32, f32[192,2,32,24]{0,3,2,1:T(8,128)} %copy-done.3), kind=kOutput, calls=%fused_computation.35 | convolution fusion | flops 1212678144 | bytes 10616832 | tf_op jit(solution)/shard_map/pcgs,cgsd->pd/dot_general | solution.py:169
  350.2 12.3 %collective-permute-done.11 = bf16[96,2048]{1,0:T(8,128)(2,1)S(1)} collective-permute-done((bf16[96,2048]{1,0:T(8,128)(2,1)S(1)}, bf16[96,2048]{1,0:T(8,128)(2,1)S(1)}, u32[]{:S(2)}, u32[]{:S(2)}) %collective-permute-start.11) | collective-permute-done | bytes 393248 | tf_op jit(solution)/shard_map/ppermute | solution.py:69
  362.6 0.9 fusion.66
  (70 shorter events, 6.2 us)
Async XLA Ops:
  0.0 33.2 %copy-start = (bf16[512,2048]{1,0:T(8,128)(2,1)S(1)}, bf16[512,2048]{1,0:T(8,128)(2,1)}, u32[]{:S(2)}) copy-start(bf16[512,2048]{1,0:T(8,128)(2,1)} %param.10) | copy-start | bytes 6291460
  4.6 6.9 %copy-start.7 = (s32[1,384,6]{1,0,2:T(1,128)S(1)}, s32[1,384,6]{1,0,2:T(1,128)}, u32[]{:S(2)}) copy-start(s32[1,384,6]{1,0,2:T(1,128)} %param.13) | copy-start | bytes 27652
  5.4 15.8 %collective-permute-start.2 = (bf16[96,3,512]{2,0,1:T(8,128)(2,1)}, bf16[96,3,512]{2,0,1:T(8,128)(2,1)S(1)}, u32[]{:S(2)}, u32[]{:S(2)}) collective-permute-start(bf16[96,3,512]{2,0,1:T(8,128)(2,1)} %bitcast.133), channel_id=1, source_target_pairs={{0,96},{32,0},{64,32},{96,64},{1,97},{33,1},{65,33},{97,65},{2,98}... | collective-permute-start | bytes 884744 | tf_op jit(solution)/shard_map/ppermute | solution.py:69
  9.0 12.2 %collective-permute-start.1 = (bf16[96,3,512]{2,0,1:T(8,128)(2,1)}, bf16[96,3,512]{2,0,1:T(8,128)(2,1)S(1)}, u32[]{:S(2)}, u32[]{:S(2)}) collective-permute-start(bf16[96,3,512]{2,0,1:T(8,128)(2,1)} %bitcast.134), channel_id=1, source_target_pairs={{0,64},{32,96},{64,0},{96,32},{1,65},{33,97},{65,1},{97,33},{2,66}... | collective-permute-start | bytes 884744 | tf_op jit(solution)/shard_map/ppermute | solution.py:69
  10.5 15.0 %collective-permute-start = (bf16[96,3,512]{2,0,1:T(8,128)(2,1)}, bf16[96,3,512]{2,0,1:T(8,128)(2,1)S(1)}, u32[]{:S(2)}, u32[]{:S(2)}) collective-permute-start(bf16[96,3,512]{2,0,1:T(8,128)(2,1)} %bitcast.135), channel_id=1, source_target_pairs={{0,32},{32,64},{64,96},{96,0},{1,33},{33,65},{65,97},{97,1},{2,34}... | collective-permute-start | bytes 884744 | tf_op jit(solution)/shard_map/ppermute | solution.py:69
  26.7 4.4 %copy-start.4 = (bf16[384,1,512]{0,2,1:T(8,128)(2,1)S(1)}, bf16[384,1,512]{0,2,1:T(8,128)(2,1)}, u32[]{:S(2)}) copy-start(bf16[384,1,512]{0,2,1:T(8,128)(2,1)} %copy.58) | copy-start | bytes 1179652
  35.9 22.2 %copy-start.5 = (bf16[1,96,2048]{2,1,0:T(8,128)(2,1)S(1)}, bf16[1,96,2048]{2,1,0:T(8,128)(2,1)}, u32[]{:S(2)}) copy-start(bf16[1,96,2048]{2,1,0:T(8,128)(2,1)} %param.8) | copy-start | bytes 1179652
  36.0 23.8 %copy-start.8 = (f32[2048]{0:T(1024)S(1)}, f32[2048]{0:T(1024)}, u32[]{:S(2)}) copy-start(f32[2048]{0:T(1024)} %param.11) | copy-start | bytes 24580
  36.0 20.7 %collective-permute-start.5 = (bf16[96,2048]{1,0:T(8,128)(2,1)S(1)}, bf16[96,2048]{1,0:T(8,128)(2,1)S(1)}, u32[]{:S(2)}, u32[]{:S(2)}) collective-permute-start(bf16[96,2048]{1,0:T(8,128)(2,1)S(1)} %get-tuple-element.10), channel_id=1, source_target_pairs={{0,32},{32,64},{64,96},{96,0},{1,33},{33,65},{65,97},{97,1},{2,34}... | collective-permute-start | bytes 1179656 | tf_op jit(solution)/shard_map/ppermute | solution.py:69
  36.1 20.7 %collective-permute-start.4 = (bf16[96,2048]{1,0:T(8,128)(2,1)S(1)}, bf16[96,2048]{1,0:T(8,128)(2,1)S(1)}, u32[]{:S(2)}, u32[]{:S(2)}) collective-permute-start(bf16[96,2048]{1,0:T(8,128)(2,1)S(1)} %get-tuple-element.11), channel_id=1, source_target_pairs={{0,64},{32,96},{64,0},{96,32},{1,65},{33,97},{65,1},{97,33},{2,66}... | collective-permute-start | bytes 1179656 | tf_op jit(solution)/shard_map/ppermute | solution.py:69
  38.2 19.2 %collective-permute-start.3 = (bf16[96,2048]{1,0:T(8,128)(2,1)S(1)}, bf16[96,2048]{1,0:T(8,128)(2,1)S(1)}, u32[]{:S(2)}, u32[]{:S(2)}) collective-permute-start(bf16[96,2048]{1,0:T(8,128)(2,1)S(1)} %get-tuple-element.9), channel_id=1, source_target_pairs={{0,96},{32,0},{64,32},{96,64},{1,97},{33,1},{65,33},{97,65},{2,98}... | collective-permute-start | bytes 1179656 | tf_op jit(solution)/shard_map/ppermute | solution.py:69
  57.4 0.7 copy-start.6
  59.9 11.7 %collective-permute-start.6 = (bf16[96,2048]{1,0:T(8,128)(2,1)S(1)}, bf16[96,2048]{1,0:T(8,128)(2,1)S(1)}, u32[]{:S(2)}, u32[]{:S(2)}) collective-permute-start(bf16[96,2048]{1,0:T(8,128)(2,1)S(1)} %multiply_convert_fusion), channel_id=1, source_target_pairs={{0,64},{32,96},{64,0},{96,32},{1,65},{33,97},{65,1},{97,33},{2,66}... | collective-permute-start | bytes 1179656 | tf_op jit(solution)/shard_map/ppermute | solution.py:69
  123.5 45.0 %all-to-all-start = ((bf16[32,24,2048]{2,1,0:T(8,128)(2,1)}), bf16[32,24,2048]{2,1,0:T(8,128)(2,1)}, u32[]{:S(2)}, u32[]{:S(2)}) async-start(bf16[32,24,2048]{2,1,0:T(8,128)(2,1)} %get-tuple-element.7), calls=%async_computation | async-start | bytes 6291456 | tf_op jit(solution)/shard_map/all_to_all | solution.py:149
  128.4 41.5 %collective-permute-start.9 = (bf16[32,24,2048]{2,1,0:T(8,128)(2,1)}, bf16[32,24,2048]{2,1,0:T(8,128)(2,1)}, u32[]{:S(2)}, u32[]{:S(2)}) collective-permute-start(bf16[32,24,2048]{2,1,0:T(8,128)(2,1)} %all_to_all.20), channel_id=1, source_target_pairs={{0,32},{1,97},{2,34},{3,99},{4,36},{5,101},{6,38},{7,103},{8,40},{... | collective-permute-start | bytes 9437192 | tf_op jit(solution)/shard_map/ppermute | solution.py:80
  168.5 6.7 %copy-start.9 = (bf16[2,352,2048]{2,1,0:T(8,128)(2,1)S(1)}, bf16[2,352,2048]{2,1,0:T(8,128)(2,1)}, u32[]{:S(2)}) copy-start(bf16[2,352,2048]{2,1,0:T(8,128)(2,1)} %param.15) | copy-start | bytes 8650756
  168.6 63.3 %collective-permute-start.7 = (bf16[32,24,2048]{2,1,0:T(8,128)(2,1)}, bf16[32,24,2048]{2,1,0:T(8,128)(2,1)S(1)}, u32[]{:S(2)}, u32[]{:S(2)}) collective-permute-start(bf16[32,24,2048]{2,1,0:T(8,128)(2,1)} %all-to-all-done), channel_id=1, source_target_pairs={{0,32},{1,97},{2,34},{3,99},{4,36},{5,101},{6,38},{7,103},{8,40},{... | collective-permute-start | bytes 9437192 | tf_op jit(solution)/shard_map/ppermute | solution.py:80
  175.3 69.3 %slice-start = ((s8[5767168]{0:T(1024)(128)(4,1)}), s8[4194304]{0:T(1024)(128)(4,1)S(1)}, s32[]{:S(2)}) async-start(s8[5767168]{0:T(1024)(128)(4,1)} %bitcast.146), calls=%async_computation.4 | async-start | bytes 8388608
  177.2 67.4 %slice-start.1 = ((s8[5767168]{0:T(1024)(128)(4,1)}), s8[1572864]{0:T(1024)(128)(4,1)S(1)}, s32[]{:S(2)}) async-start(s8[5767168]{0:T(1024)(128)(4,1)} %bitcast.146), calls=%async_computation.5 | async-start | bytes 3145728
  177.2 70.1 %collective-permute-start.10 = (bf16[32,24,2048]{2,1,0:T(8,128)(2,1)S(1)}, bf16[32,24,2048]{2,1,0:T(8,128)(2,1)S(1)}, u32[]{:S(2)}, u32[]{:S(2)}) collective-permute-start(bf16[32,24,2048]{2,1,0:T(8,128)(2,1)S(1)} %convolution_convert_fusion.1), channel_id=1, source_target_pairs={{0,96},{1,33},{2,98},{3,35},{4,100},{5,37},{6,102},{7,39},{8,104},... | collective-permute-start | bytes 9437192 | tf_op jit(solution)/shard_map/ppermute | solution.py:80
  236.4 8.2 %copy-start.2 = (bf16[32,24,2048]{2,1,0:T(8,128)(2,1)S(1)}, bf16[32,24,2048]{2,1,0:T(8,128)(2,1)}, u32[]{:S(2)}) copy-start(bf16[32,24,2048]{2,1,0:T(8,128)(2,1)} %all_to_all.20) | copy-start | bytes 9437188
  240.0 39.7 %collective-permute-start.8 = (bf16[32,24,2048]{2,1,0:T(8,128)(2,1)}, bf16[32,24,2048]{2,1,0:T(8,128)(2,1)}, u32[]{:S(2)}, u32[]{:S(2)}) collective-permute-start(bf16[32,24,2048]{2,1,0:T(8,128)(2,1)} %convolution_convert_fusion.3), channel_id=1, source_target_pairs={{0,96},{1,33},{2,98},{3,35},{4,100},{5,37},{6,102},{7,39},{8,104},... | collective-permute-start | bytes 9437192 | tf_op jit(solution)/shard_map/ppermute | solution.py:80
  250.9 45.0 %all-to-all-start.3 = ((bf16[32,24,2048]{2,1,0:T(8,128)(2,1)}), bf16[32,24,2048]{2,1,0:T(8,128)(2,1)}, u32[]{:S(2)}, u32[]{:S(2)}) async-start(bf16[32,24,2048]{2,1,0:T(8,128)(2,1)} %add_convert_fusion), calls=%async_computation.3 | async-start | bytes 6291456 | tf_op jit(solution)/shard_map/all_to_all | solution.py:155
  256.0 23.7 %copy-start.10 = (bf16[2,352,2048]{2,1,0:T(8,128)(2,1)S(1)}, bf16[2,352,2048]{2,1,0:T(8,128)(2,1)}, u32[]{:S(2)}) copy-start(bf16[2,352,2048]{2,1,0:T(8,128)(2,1)} %param.15) | copy-start | bytes 8650756
  285.1 15.6 %copy-start.11 = (bf16[2048,64]{0,1:T(8,128)(2,1)S(1)}, bf16[2048,64]{0,1:T(8,128)(2,1)}, u32[]{:S(2)}) copy-start(bf16[2048,64]{0,1:T(8,128)(2,1)} %param.12) | copy-start | bytes 786436
  295.9 45.0 %all-to-all-start.1 = ((bf16[32,24,2048]{2,1,0:T(8,128)(2,1)}), bf16[32,24,2048]{2,1,0:T(8,128)(2,1)}, u32[]{:S(2)}, u32[]{:S(2)}) async-start(bf16[32,24,2048]{2,1,0:T(8,128)(2,1)} %add_convert_fusion.1), calls=%async_computation.1 | async-start | bytes 6291456 | tf_op jit(solution)/shard_map/all_to_all | solution.py:155
  302.3 38.6 %copy-start.3 = (f32[192,2,32,24]{0,3,2,1:T(8,128)}, f32[192,2,32,24]{0,3,2,1:T(8,128)S(1)}, u32[]{:S(2)}) copy-start(f32[192,2,32,24]{0,3,2,1:T(8,128)S(1)} %select_reduce_fusion) | copy-start | bytes 3538948
  344.6 18.8 %copy-start.1 = (bf16[512,2048]{1,0:T(8,128)(2,1)S(1)}, bf16[512,2048]{1,0:T(8,128)(2,1)}, u32[]{:S(2)}) copy-start(bf16[512,2048]{1,0:T(8,128)(2,1)} %param.10) | copy-start | bytes 6291460
  350.1 12.4 %collective-permute-start.11 = (bf16[96,2048]{1,0:T(8,128)(2,1)S(1)}, bf16[96,2048]{1,0:T(8,128)(2,1)S(1)}, u32[]{:S(2)}, u32[]{:S(2)}) collective-permute-start(bf16[96,2048]{1,0:T(8,128)(2,1)S(1)} %slice.230), channel_id=1, source_target_pairs={{0,64},{32,96},{64,0},{96,32},{1,65},{33,97},{65,1},{97,33},{2,66}... | collective-permute-start | bytes 1179656 | tf_op jit(solution)/shard_map/ppermute | solution.py:69
